TPU v7x, 256 devices: a whole 4x4x8 slice. The times are simulated.
256 devices in a mesh: sec: 2 (over y_hi), gx: 16 (over y_lo, z), gy: 8 (over x, core).
Axes of the slice: x: 4, y: 4 (y_hi: 2, y_lo: 2; y = y_hi * 2 + y_lo), z: 8, core: 2. Of those that a mesh axis runs over, the one named last changes fastest.
Arguments:
- ocean_velocity: float32 [2, 8, 1024, 2048], P(None, None, 'gx', ('sec', 'gy')), may hold values from -6 to 6
- wind_stress: float32 [2, 1024, 2048], P(None, 'gx', ('sec', 'gy')), may hold values from -6 to 6
- level_counts: int32 [1024, 2048], P('gx', ('sec', 'gy')), may hold values from 1 to 8
- floe_position: float32 [16, 16, 2, 2048], P('gx', ('sec', 'gy')), may hold values from 0 to 4
- floe_velocity: float32 [16, 16, 2, 2048], P('gx', ('sec', 'gy')), may hold values from -3 to 3
- floe_radius: float32 [16, 16, 2048], P('gx', ('sec', 'gy')), may hold values from 0.5 to 1.5
- floe_mass: float32 [16, 16, 2048], P('gx', ('sec', 'gy')), may hold values from 0.5 to 5
- floe_polygon: float32 [16, 16, 32, 2048], P('gx', ('sec', 'gy')), may hold values from -2 to 2
- remap_cells: int32 [16, 16, 2048], P('gx', ('sec', 'gy')), may hold values from 0 to 131071, as said below
- contact_count: int32 [16, 16], P('gx', ('sec', 'gy')), may hold values from 8 to 64, as said below
- contact_list: int32 [16, 16, 3, 64], P('gx', ('sec', 'gy')), may hold values from 0 to 15, as said below
- move_index: int32 [16, 16, 8, 128], P('gx', ('sec', 'gy')), may hold values from 0 to 2047, as said below
- move_count: int32 [16, 16, 8], P('gx', ('sec', 'gy')), may hold values from 42 to 128, as said below
Outputs:
- ocean_next: float32 [2, 8, 1024, 2048], P(None, None, 'gx', ('sec', 'gy'))
- floe_next: float32 [16, 16, 4, 2048], P('gx', ('sec', 'gy'))
- arrivals: float32 [16, 16, 8, 38, 128], P('gx', ('sec', 'gy'))
Inputs may be any that keep to these rules, and one draw needn't show every extreme that they name: `contact_list`: row 0 of each slot names a block of the tile, 0 to 15; row 1 a source 0 to 8, 4 meaning the tile itself; row 2 a block of the source: 0 to 15 for source 4, else 0 to 3. Only the first contact_count slots count. `contact_count`: some tile uses all 64 slots in every draw. `move_index`: the floes named by one tile over all directions and slots are distinct. `move_count`: every tile fills all 128 slots towards at least one neighbour. `remap_cells`: Row-major index over the 1024 rows and the tile's 128 columns. The floes of tile row i lie in grid rows i * 64 - 64 // 2 to i * 64 + 64 + 64 // 2 - 1 (within the grid), and every tile has floes in the first and the last row of that band.
All inputs are finite; a program needn't handle non-finite values.
Results may differ from a plain program's by a relative error of at most 0.0003.
Values sent between devices are 32-bit elements; how exact they have to be, the bound alone decides.
No kernel may reach another device: no remote copies, remote signals or barrier semaphores. Data moves between devices by JAX's collectives and lax.ppermute only.
A program may use at most 64 MiB of HBM per device.

v0:
```python
import math

import jax
import jax.numpy as jnp
from jax import lax
from jax.sharding import PartitionSpec as P

OSTEPS = 4
GHOST = 4


SOFTEN = 0.1
STIFFNESS = 0.1
DAMPING = 0.05
VERT_MIX = 0.15
CORIOLIS = 0.1
SURFACE_GAIN = 0.25
WATER_DRAG = 0.1
AIR_GAIN = 0.2
ICE_STEP = 0.5
PLACES = (0, 1, 2, 3, 5, 6, 7, 8)


def with_halo(array, sides, width):
    for axis, dim in sides:
        size, length = (lax.axis_size(axis), array.shape[dim])
        up = [(i, (i + 1) % size) for i in range(size - 1)]
        down = [(j, i) for i, j in up]
        last = lax.slice_in_dim(array, length - width, length, axis=dim)
        leading = lax.slice_in_dim(array, 0, width, axis=dim)
        before = lax.ppermute(last, axis, up)
        after = lax.ppermute(leading, axis, down)
        array = jnp.concatenate([before, array, after], axis=dim)
    return array


def ocean_substep(flow, padded, wet, wind):
    levels_here = flow.shape[1]
    lap = (
        padded[:, :, :-2, 1:-1]
        + padded[:, :, 2:, 1:-1]
        + padded[:, :, 1:-1, :-2]
        + padded[:, :, 1:-1, 2:]
        - 4.0 * flow
    )
    depth = jnp.arange(levels_here, dtype=jnp.float32)
    horizontal = (0.15 - 0.05 * depth / levels_here)[None, :, None, None]
    flux = VERT_MIX * (flow[:, 1:] - flow[:, :-1]) * wet[None, 1:]
    empty = jnp.zeros_like(flow[:, :1])
    vert = jnp.concatenate([flux, empty], axis=1) - jnp.concatenate([empty, flux], axis=1)
    turning = jnp.stack([CORIOLIS * flow[1], -CORIOLIS * flow[0]])
    surface = jnp.concatenate([SURFACE_GAIN * wind[:, None], jnp.zeros_like(flow[:, 1:])], axis=1)
    return (flow + horizontal * lap + vert + turning + surface) * wet[None]


def pair_forces(first, second):
    delta_x = first[:, 0, :, None] - second[:, 0, None, :]
    delta_y = first[:, 1, :, None] - second[:, 1, None, :]
    distance = jnp.sqrt(delta_x * delta_x + delta_y * delta_y + SOFTEN * SOFTEN)
    reach = first[:, 4, :, None] + second[:, 4, None, :]
    intersection = jnp.maximum(reach - distance, 0.0)
    reduced = first[:, 4, :, None] * second[:, 4, None, :] / reach
    normal_x = delta_x / distance
    normal_y = delta_y / distance
    closing = (first[:, 2, :, None] - second[:, 2, None, :]) * normal_x + (
        first[:, 3, :, None] - second[:, 3, None, :]
    ) * normal_y
    magnitude = intersection * reduced * (STIFFNESS - DAMPING * closing)
    return jnp.stack(
        [jnp.sum(magnitude * normal_x, axis=2), jnp.sum(magnitude * normal_y, axis=2)], axis=1
    )


def block_table(own, ghosts):
    blocks = own.shape[1] // 128
    edge_blocks = ghosts.shape[2] // 128
    mine = own.reshape(5, blocks, 128).transpose(1, 0, 2)
    theirs = (
        ghosts.reshape(8, 5, edge_blocks, 128)
        .transpose(0, 2, 1, 3)
        .reshape(8 * edge_blocks, 5, 128)
    )
    return jnp.concatenate([mine, theirs], axis=0)


def contact_batch(table, lists, valid, blocks, edge_blocks):
    source = lists[1]
    neighbour = source - (source > 4).astype(jnp.int32)
    partner = jnp.where(source == 4, lists[2], blocks + neighbour * edge_blocks + lists[2])
    forces = pair_forces(table[lists[0]], table[partner])
    forces = jnp.where(valid[:, None, None], forces, 0.0)
    onehot = (lists[0][:, None] == jnp.arange(blocks, dtype=jnp.int32)[None, :]).astype(jnp.float32)
    return jnp.einsum("pn,pcf->ncf", onehot, forces, precision=lax.Precision.HIGHEST)


def shards(
    ocean_velocity,
    wind_stress,
    level_counts,
    floe_position,
    floe_velocity,
    floe_radius,
    floe_mass,
    floe_polygon,
    remap_cells,
    contact_count,
    contact_list,
    move_index,
    move_count,
):
    levels_here = ocean_velocity.shape[1]
    rows_here = ocean_velocity.shape[2]
    cols_here = ocean_velocity.shape[3]
    wet = (jnp.arange(levels_here, dtype=jnp.int32)[:, None, None] < level_counts[None]).astype(
        jnp.float32
    )
    flow = ocean_velocity * wet[None]
    for substep in range(OSTEPS):
        padded = with_halo(flow, (("gx", 2), (("sec", "gy"), 3)), 1)
        flow = ocean_substep(flow, padded, wet, wind_stress)
    surface = jnp.stack([flow[0, 0], flow[1, 0], wind_stress[0], wind_stress[1]])
    position = floe_position[0, 0]
    velocity = floe_velocity[0, 0]
    radius = floe_radius[0, 0]
    mass = floe_mass[0, 0]
    cells = remap_cells[0, 0]
    floes = position.shape[1]
    blocks = floes // 128
    record = jnp.concatenate([position, velocity, radius[None]], axis=0)
    edge = record[:, : GHOST * 128]
    beside_all = with_halo(edge[None, None], (("gx", 0), (("sec", "gy"), 1)), 1)
    beside_all = beside_all.reshape(9, 5, GHOST * 128)
    ghosts = jnp.concatenate([beside_all[:4], beside_all[5:]], axis=0)
    table = block_table(record, ghosts)
    margin = rows_here // 2
    near = with_halo(surface, (("gx", 1),), margin)
    first_row = lax.axis_index("gx") * rows_here - margin
    sampled = jnp.take(near.reshape(4, -1), cells - first_row * cols_here, axis=1)
    lists = contact_list[0, 0]
    count = contact_count[0, 0]
    slots = lists.shape[1]
    batch = math.gcd(slots, 32)
    rounds = (count + batch - 1) // batch

    def accumulate(turn, total):
        start = turn * batch
        group = lax.dynamic_slice_in_dim(lists, start, batch, 1)
        valid = start + jnp.arange(batch, dtype=jnp.int32) < count
        return total + contact_batch(table, group, valid, blocks, GHOST)

    contact = lax.fori_loop(0, rounds, accumulate, jnp.zeros((blocks, 2, 128), jnp.float32))
    contact = contact.transpose(1, 0, 2).reshape(2, floes)
    area = math.pi * radius * radius
    relative = sampled[0:2] - velocity
    speed = jnp.sqrt(jnp.sum(relative * relative, axis=0, keepdims=True))
    total = contact + area[None] * (WATER_DRAG * speed * relative + AIR_GAIN * sampled[2:4])
    new_velocity = velocity + ICE_STEP * total / mass[None]
    new_position = position + ICE_STEP * new_velocity
    floe_next = jnp.concatenate([new_position, new_velocity], axis=0)
    rows_all = jnp.concatenate([floe_next, radius[None], mass[None], floe_polygon[0, 0]], axis=0)
    width = rows_all.shape[0]
    leaving = move_index[0, 0]
    capacity = leaving.shape[1]
    taken = (
        jnp.take(rows_all, leaving.reshape(-1), axis=1)
        .reshape(width, 8, capacity)
        .transpose(1, 0, 2)
    )
    valid_slots = jnp.arange(capacity, dtype=jnp.int32)[None, :] < move_count[0, 0][:, None]
    outgoing = jnp.where(valid_slots[:, None, :], taken, 0.0)
    landed = with_halo(outgoing[None, None], (("gx", 0), (("sec", "gy"), 1)), 1)
    landed = landed.reshape(9, 8, width, capacity)
    arrived = [landed[8 - PLACES[way], way] for way in range(8)]
    arrivals = jnp.stack(arrived, axis=0)
    return (flow, floe_next[None, None], arrivals[None, None])


def solution(mesh):
    return jax.shard_map(
        shards,
        mesh=mesh,
        in_specs=(
            P(None, None, "gx", ("sec", "gy")),
            P(None, "gx", ("sec", "gy")),
            P("gx", ("sec", "gy")),
            P("gx", ("sec", "gy"), None, None),
            P("gx", ("sec", "gy"), None, None),
            P("gx", ("sec", "gy"), None),
            P("gx", ("sec", "gy"), None),
            P("gx", ("sec", "gy"), None, None),
            P("gx", ("sec", "gy"), None),
            P("gx", ("sec", "gy")),
            P("gx", ("sec", "gy"), None, None),
            P("gx", ("sec", "gy"), None, None),
            P("gx", ("sec", "gy"), None),
        ),
        out_specs=(
            P(None, None, "gx", ("sec", "gy")),
            P("gx", ("sec", "gy"), None, None),
            P("gx", ("sec", "gy"), None, None, None),
        ),
        check_vma=False,
    )
```

profile of v0, /device:TPU:24, one launch (start us, length us, event | category | flops | bytes accessed | tf_op | source)
XLA Modules:
  0.0 214.5 jit_solution(7060358235312906009)
XLA Ops:
  0.6 1.3 fusion.68
  2.0 3.8 %collective-permute-start.16 = (f32[1,1,5,512]{3,2,1,0:T(8,128)}, f32[1,1,5,512]{3,2,1,0:T(8,128)}, u32[]{:S(2)}, u32[]{:S(2)}) collective-permute-start(f32[1,1,5,512]{3,2,1,0:T(8,128)} %fusion.68), channel_id=1, source_target_pairs={{0,8},{8,16},{16,24},{24,32},{32,40},{40,48},{48,56},{56,64},{64,7... | collective-permute-start | bytes 30728 | tf_op jit(solution)/shard_map/ppermute | solution.py:31
  5.8 6.0 %collective-permute-start.17 = (f32[1,1,5,512]{3,2,1,0:T(8,128)}, f32[1,1,5,512]{3,2,1,0:T(8,128)}, u32[]{:S(2)}, u32[]{:S(2)}) collective-permute-start(f32[1,1,5,512]{3,2,1,0:T(8,128)} %fusion.68), channel_id=1, source_target_pairs={{8,0},{16,8},{24,16},{32,24},{40,32},{48,40},{56,48},{64,56},{72,6... | collective-permute-start | bytes 30728 | tf_op jit(solution)/shard_map/ppermute | solution.py:32
  12.6 1.4 copy_multiply_fusion
  14.1 2.1 collective-permute-start
  16.2 6.0 %collective-permute-start.1 = (f32[2,8,1,128]{3,1,2,0:T(8,128)S(1)}, f32[2,8,1,128]{3,1,2,0:T(8,128)S(1)}, u32[]{:S(2)}, u32[]{:S(2)}) collective-permute-start(f32[2,8,1,128]{3,1,2,0:T(8,128)S(1)} %get-tuple-element.123), channel_id=1, source_target_pairs={{8,0},{16,8},{24,16},{32,24},{40,32},{48,40},{56,48},{64,56},{72,6... | collective-permute-start | bytes 24584 | tf_op jit(solution)/shard_map/ppermute | solution.py:32
  27.6 1.3 copy.208
  29.3 1.4 copy.209
  32.9 1.9 collective-permute-start.2
  35.1 7.3 %collective-permute-start.3 = (f32[2,8,66,1]{2,1,3,0:T(8,128)S(1)}, f32[2,8,66,1]{2,1,3,0:T(8,128)S(1)}, u32[]{:S(2)}, u32[]{:S(2)}) collective-permute-start(f32[2,8,66,1]{2,1,3,0:T(8,128)S(1)} %copy.185), channel_id=1, source_target_pairs={{1,0},{2,1},{3,2},{4,3},{5,4},{6,5},{7,6},{128,7},{129,128},{130,1... | collective-permute-start | bytes 12680 | tf_op jit(solution)/shard_map/ppermute | solution.py:32
  42.4 1.3 copy_dynamic-update-slice_fusion.2
  43.7 1.3 copy_dynamic-update-slice_fusion.1
  45.0 1.3 copy_dynamic-update-slice_fusion
  46.4 1.9 collective-permute-start.18
  48.3 7.3 %collective-permute-start.19 = (f32[3,1,5,512]{3,1,2,0:T(1,128)}, f32[3,1,5,512]{3,1,2,0:T(1,128)}, u32[]{:S(2)}, u32[]{:S(2)}) collective-permute-start(f32[3,1,5,512]{3,1,2,0:T(1,128)} %copy_dynamic-update-slice_fusion), channel_id=1, source_target_pairs={{1,0},{2,1},{3,2},{4,3},{5,4},{6,5},{7,6},{128,7},{129,128},{130,1... | collective-permute-start | bytes 92168 | tf_op jit(solution)/shard_map/ppermute | solution.py:32
  55.9 1.1 copy.186
  57.0 2.0 fusion.20
  59.0 1.9 collective-permute-start.4
  60.9 6.0 %collective-permute-start.5 = (f32[2,8,1,128]{3,1,2,0:T(8,128)S(1)}, f32[2,8,1,128]{3,1,2,0:T(8,128)S(1)}, u32[]{:S(2)}, u32[]{:S(2)}) collective-permute-start(f32[2,8,1,128]{3,1,2,0:T(8,128)S(1)} %get-tuple-element.119), channel_id=1, source_target_pairs={{8,0},{16,8},{24,16},{32,24},{40,32},{48,40},{56,48},{64,56},{72,6... | collective-permute-start | bytes 24584 | tf_op jit(solution)/shard_map/ppermute | solution.py:32
  67.0 1.3 collective-permute-done.5
  68.3 1.0 fusion.73
  69.3 1.9 copy.187
  71.2 1.9 collective-permute-start.6
  74.0 7.2 %collective-permute-start.7 = (f32[2,8,66,1]{2,1,3,0:T(8,128)}, f32[2,8,66,1]{2,1,3,0:T(8,128)S(1)}, u32[]{:S(2)}, u32[]{:S(2)}) collective-permute-start(f32[2,8,66,1]{2,1,3,0:T(8,128)} %copy.189), channel_id=1, source_target_pairs={{1,0},{2,1},{3,2},{4,3},{5,4},{6,5},{7,6},{128,7},{129,128},{130,1... | collective-permute-start | bytes 12680 | tf_op jit(solution)/shard_map/ppermute | solution.py:32
  82.0 1.8 copy.188
  83.8 1.1 copy.190
  84.9 1.7 fusion.21
  86.6 1.9 collective-permute-start.8
  88.6 6.3 %collective-permute-start.9 = (f32[2,8,1,128]{3,1,2,0:T(8,128)S(1)}, f32[2,8,1,128]{3,1,2,0:T(8,128)S(1)}, u32[]{:S(2)}, u32[]{:S(2)}) collective-permute-start(f32[2,8,1,128]{3,1,2,0:T(8,128)S(1)} %get-tuple-element.115), channel_id=1, source_target_pairs={{8,0},{16,8},{24,16},{32,24},{40,32},{48,40},{56,48},{64,56},{72,6... | collective-permute-start | bytes 24584 | tf_op jit(solution)/shard_map/ppermute | solution.py:32
  96.3 1.2 fusion.72
  97.5 1.4 copy.191
  98.8 1.9 collective-permute-start.10
  100.7 1.3 copy.193
  102.0 7.3 %collective-permute-start.11 = (f32[2,8,66,1]{2,1,3,0:T(8,128)S(1)}, f32[2,8,66,1]{2,1,3,0:T(8,128)S(1)}, u32[]{:S(2)}, u32[]{:S(2)}) collective-permute-start(f32[2,8,66,1]{2,1,3,0:T(8,128)S(1)} %copy.193), channel_id=1, source_target_pairs={{1,0},{2,1},{3,2},{4,3},{5,4},{6,5},{7,6},{128,7},{129,128},{130,1... | collective-permute-start | bytes 12680 | tf_op jit(solution)/shard_map/ppermute | solution.py:32
  110.0 1.1 copy.192
  111.1 1.1 copy.194
  112.2 1.7 fusion.22
  115.6 2.3 %collective-permute-start.12 = (f32[2,8,1,128]{3,1,2,0:T(8,128)S(1)}, f32[2,8,1,128]{3,1,2,0:T(8,128)S(1)}, u32[]{:S(2)}, u32[]{:S(2)}) collective-permute-start(f32[2,8,1,128]{3,1,2,0:T(8,128)S(1)} %get-tuple-element.110), channel_id=1, source_target_pairs={{0,8},{8,16},{16,24},{24,32},{32,40},{40,48},{48,56},{56,64},{64,7... | collective-permute-start | bytes 24584 | tf_op jit(solution)/shard_map/ppermute | solution.py:31
  117.9 5.9 %collective-permute-start.13 = (f32[2,8,1,128]{3,1,2,0:T(8,128)S(1)}, f32[2,8,1,128]{3,1,2,0:T(8,128)S(1)}, u32[]{:S(2)}, u32[]{:S(2)}) collective-permute-start(f32[2,8,1,128]{3,1,2,0:T(8,128)S(1)} %get-tuple-element.111), channel_id=1, source_target_pairs={{8,0},{16,8},{24,16},{32,24},{40,32},{48,40},{56,48},{64,56},{72,6... | collective-permute-start | bytes 24584 | tf_op jit(solution)/shard_map/ppermute | solution.py:32
  127.8 1.9 collective-permute-start.14
  130.0 7.3 %collective-permute-start.15 = (f32[2,8,66,1]{2,1,3,0:T(8,128)S(1)}, f32[2,8,66,1]{2,1,3,0:T(8,128)}, u32[]{:S(2)}, u32[]{:S(2)}) collective-permute-start(f32[2,8,66,1]{2,1,3,0:T(8,128)S(1)} %copy.197), channel_id=1, source_target_pairs={{1,0},{2,1},{3,2},{4,3},{5,4},{6,5},{7,6},{128,7},{129,128},{130,1... | collective-permute-start | bytes 12680 | tf_op jit(solution)/shard_map/ppermute | solution.py:32
  137.3 0.9 pad_maximum_fusion.39
  138.6 1.0 copy.198
  139.6 1.8 fusion.23
  142.3 1.9 collective-permute-start.20
  144.2 6.0 %collective-permute-start.21 = (f32[4,32,128]{2,1,0:T(8,128)S(1)}, f32[4,32,128]{2,1,0:T(8,128)S(1)}, u32[]{:S(2)}, u32[]{:S(2)}) collective-permute-start(f32[4,32,128]{2,1,0:T(8,128)S(1)} %get-tuple-element.130), channel_id=1, source_target_pairs={{8,0},{16,8},{24,16},{32,24},{40,32},{48,40},{56,48},{64,56},{72,6... | collective-permute-start | bytes 196616 | tf_op jit(solution)/shard_map/ppermute | solution.py:32
  150.3 7.6 %while.10 = (s32[]{:T(128)}, f32[16,2,128]{2,0,1:T(8,128)S(1)}, s32[]{:T(128)}, s32[3,64]{1,0:T(4,128)S(1)}, s32[]{:T(128)}, /*index=5*/f32[48,5,128]{2,1,0:T(8,...) while((s32[]{:T(128)}, f32[16,2,128]{2,0,1:T(8,128)S(1)}, s32[]{:T(128)}, s32[3,64]{1,0:T(4,128)S(1)}, ...), condition=%wide.region_3.4_spmd, body=%wide.region_0.3_spmd.sunk | while | flops 15219718 | bytes 928223 | solution.py:151
  151.7 5.1 %multiply_reduce_fusion.4 = (f32[32,128]{1,0:T(8,128)S(1)}, f32[32,128]{1,0:T(8,128)S(1)}) fusion(f32[32,128]{1,0:T(8,128)S(1)} %bitcast.166, f32[32,128]{1,0:T(8,128)S(1)} %bitcast.171, f32[32,128]{1,0:T(8,128)S(1)} %bitcast.167, f32[32,128]{1,0:T(8,128)S(1)} %bitcast.172, f32[32,128]{1,0:T(8,128)S(1)} %bitcast.168, f32[32,128]{1,0:T(8,128)S(1)} %bitcast.173, ...), kind=kLoop, calls=%fused_computation.17.clone.1 | loop fusion | flops 13623296 | bytes 196608 | tf_op jit(solution)/shard_map/while/body/reduce_sum | solution.py:70
  158.0 4.7 %copy.203 = f32[4,128,128]{0,2,1:T(8,128)} copy(f32[4,128,128]{2,1,0:T(8,128)S(1)} %pad_maximum_fusion.38) | data formatting | bytes 524288 | tf_op jit(solution)/shard_map/concatenate | solution.py:33
  162.6 8.9 %gather_fusion.2 = f32[2048,4]{1,0:T(8,128)S(1)} fusion(f32[4,16384]{0,1:T(8,128)} %bitcast.154, s32[2048]{0:T(1024)S(1)} %copy-done.13), kind=kCustom, calls=%fused_computation.2 | custom fusion | bytes 73728 | tf_op jit(solution)/shard_map/jit(_take)/gather | solution.py:138
  172.1 1.4 copy.206
  173.5 1.4 copy.207
  174.8 3.4 %concatenate.178 = f32[38,2048]{0,1:T(8,128)S(1)} concatenate(f32[2,2048]{0,1:T(8,128)} %copy.206, f32[2,2048]{0,1:T(8,128)} %copy.207, f32[1,2048]{0,1:T(8,128)S(1)} %copy-done, f32[1,2048]{0,1:T(8,128)} %copy.209, f32[32,2048]{0,1:T(8,128)S(1)} %bitcast.155), dimensions={0} | concatenate | bytes 622592 | tf_op jit(solution)/shard_map/concatenate | solution.py:160
  178.3 2.8 %gather_fusion.3 = f32[1024,38]{1,0:T(8,128)S(1)} fusion(f32[38,2048]{0,1:T(8,128)S(1)} %concatenate.178, s32[1024]{0:T(1024)S(1)} %broadcast_clamp_fusion.1), kind=kCustom, calls=%fused_computation.3 | custom fusion | bytes 315392 | tf_op jit(solution)/shard_map/jit(_take)/gather | solution.py:165
  181.4 1.9 collective-permute-start.22
  183.3 6.0 %collective-permute-start.23 = (f32[1,1,8,38,128]{4,2,3,1,0:T(8,128)S(1)}, f32[1,1,8,38,128]{4,2,3,1,0:T(8,128)S(1)}, u32[]{:S(2)}, u32[]{:S(2)}) collective-permute-start(f32[1,1,8,38,128]{4,2,3,1,0:T(8,128)S(1)} %select_bitcast_fusion), channel_id=1, source_target_pairs={{8,0},{16,8},{24,16},{32,24},{40,32},{48,40},{56,48},{64,56},{72,6... | collective-permute-start | bytes 466952 | tf_op jit(solution)/shard_map/ppermute | solution.py:32
  189.4 1.3 collective-permute-done.22
  190.6 1.5 collective-permute-done.23
  192.1 1.9 collective-permute-start.24
  194.0 13.3 %collective-permute-start.25 = (f32[3,1,8,38,128]{4,2,3,1,0:T(8,128)S(1)}, f32[3,1,8,38,128]{4,2,3,1,0:T(8,128)S(1)}, u32[]{:S(2)}, u32[]{:S(2)}) collective-permute-start(f32[3,1,8,38,128]{4,2,3,1,0:T(8,128)S(1)} %pad_maximum_fusion.37), channel_id=1, source_target_pairs={{1,0},{2,1},{3,2},{4,3},{5,4},{6,5},{7,6},{128,7},{129,128},{130,1... | collective-permute-start | bytes 1400840 | tf_op jit(solution)/shard_map/ppermute | solution.py:32
  207.4 0.9 copy.218
  208.9 2.8 %collective-permute-done.24 = f32[3,1,8,38,128]{4,2,3,1,0:T(8,128)S(1)} collective-permute-done((f32[3,1,8,38,128]{4,2,3,1,0:T(8,128)S(1)}, f32[3,1,8,38,128]{4,2,3,1,0:T(8,128)S(1)}, u32[]{:S(2)}, u32[]{:S(2)}) %collective-permute-start.24) | collective-permute-done | bytes 466976 | tf_op jit(solution)/shard_map/ppermute | solution.py:31
  211.7 1.8 collective-permute-done.25
  213.7 0.9 stack.41
  (141 shorter events, 23.4 us)
Async XLA Ops:
  2.0 40.4 %collective-permute-start.16 = (f32[1,1,5,512]{3,2,1,0:T(8,128)}, f32[1,1,5,512]{3,2,1,0:T(8,128)}, u32[]{:S(2)}, u32[]{:S(2)}) collective-permute-start(f32[1,1,5,512]{3,2,1,0:T(8,128)} %fusion.68), channel_id=1, source_target_pairs={{0,8},{8,16},{16,24},{24,32},{32,40},{40,48},{48,56},{56,64},{64,7... | collective-permute-start | bytes 30728 | tf_op jit(solution)/shard_map/ppermute | solution.py:31
  5.8 39.2 %collective-permute-start.17 = (f32[1,1,5,512]{3,2,1,0:T(8,128)}, f32[1,1,5,512]{3,2,1,0:T(8,128)}, u32[]{:S(2)}, u32[]{:S(2)}) collective-permute-start(f32[1,1,5,512]{3,2,1,0:T(8,128)} %fusion.68), channel_id=1, source_target_pairs={{8,0},{16,8},{24,16},{32,24},{40,32},{48,40},{56,48},{64,56},{72,6... | collective-permute-start | bytes 30728 | tf_op jit(solution)/shard_map/ppermute | solution.py:32
  12.6 11.3 %copy-start.4 = (f32[2,64,128]{2,1,0:T(8,128)S(1)}, f32[2,64,128]{2,1,0:T(8,128)}, u32[]{:S(2)}) copy-start(f32[2,64,128]{2,1,0:T(8,128)} %param.16) | copy-start | bytes 196612
  14.0 9.9 %copy-start.19 = (s32[1,1,2048]{2,1,0:T(1,128)S(1)}, s32[1,1,2048]{2,1,0:T(1,128)}, u32[]{:S(2)}) copy-start(s32[1,1,2048]{2,1,0:T(1,128)} %param.23) | copy-start | bytes 24580
  14.0 11.0 %copy-start.18 = (s32[1,1,8,128]{3,2,1,0:T(8,128)S(1)}, s32[1,1,8,128]{3,2,1,0:T(8,128)}, u32[]{:S(2)}) copy-start(s32[1,1,8,128]{3,2,1,0:T(8,128)} %param.26) | copy-start | bytes 12292
  14.1 11.1 %copy-start.24 = (s32[1,1,8]{2,1,0:T(1,128)S(1)}, s32[1,1,8]{2,1,0:T(1,128)}, u32[]{:S(2)}) copy-start(s32[1,1,8]{2,1,0:T(1,128)} %param.27) | copy-start | bytes 100
  14.1 11.7 %copy-start.7 = (f32[1,1,2,2048]{3,2,1,0:T(2,128)S(1)}, f32[1,1,2,2048]{3,2,1,0:T(2,128)}, u32[]{:S(2)}) copy-start(f32[1,1,2,2048]{3,2,1,0:T(2,128)} %param.19) | copy-start | bytes 49156
  14.1 11.7 %copy-start.9 = (f32[1,1,2,2048]{3,2,1,0:T(2,128)S(1)}, f32[1,1,2,2048]{3,2,1,0:T(2,128)}, u32[]{:S(2)}) copy-start(f32[1,1,2,2048]{3,2,1,0:T(2,128)} %param.18) | copy-start | bytes 49156
  14.1 11.7 %copy-start.10 = (f32[1,1,2048]{2,1,0:T(1,128)S(1)}, f32[1,1,2048]{2,1,0:T(1,128)}, u32[]{:S(2)}) copy-start(f32[1,1,2048]{2,1,0:T(1,128)} %param.20) | copy-start | bytes 24580
  14.1 16.5 %collective-permute-start = (f32[2,8,1,128]{3,1,2,0:T(8,128)S(1)}, f32[2,8,1,128]{3,1,2,0:T(8,128)S(1)}, u32[]{:S(2)}, u32[]{:S(2)}) collective-permute-start(f32[2,8,1,128]{3,1,2,0:T(8,128)S(1)} %get-tuple-element.122), channel_id=1, source_target_pairs={{0,8},{8,16},{16,24},{24,32},{32,40},{40,48},{48,56},{56,64},{64,7... | collective-permute-start | bytes 24584 | tf_op jit(solution)/shard_map/ppermute | solution.py:31
  16.2 14.5 %collective-permute-start.1 = (f32[2,8,1,128]{3,1,2,0:T(8,128)S(1)}, f32[2,8,1,128]{3,1,2,0:T(8,128)S(1)}, u32[]{:S(2)}, u32[]{:S(2)}) collective-permute-start(f32[2,8,1,128]{3,1,2,0:T(8,128)S(1)} %get-tuple-element.123), channel_id=1, source_target_pairs={{8,0},{16,8},{24,16},{32,24},{40,32},{48,40},{56,48},{64,56},{72,6... | collective-permute-start | bytes 24584 | tf_op jit(solution)/shard_map/ppermute | solution.py:32
  22.3 6.7 %copy-start.23 = (s32[1,1,3,64]{3,1,2,0:T(1,128)S(1)}, s32[1,1,3,64]{3,1,2,0:T(1,128)}, u32[]{:S(2)}) copy-start(s32[1,1,3,64]{3,1,2,0:T(1,128)} %param.25) | copy-start | bytes 2308
  22.3 6.7 %copy-start.6 = (f32[1,1,32,2048]{3,2,1,0:T(8,128)S(1)}, f32[1,1,32,2048]{3,2,1,0:T(8,128)}, u32[]{:S(2)}) copy-start(f32[1,1,32,2048]{3,2,1,0:T(8,128)} %param.22) | copy-start | bytes 786436
  23.0 6.2 %copy-start.11 = (f32[1,1,2048]{2,1,0:T(1,128)S(1)}, f32[1,1,2048]{2,1,0:T(1,128)}, u32[]{:S(2)}) copy-start(f32[1,1,2048]{2,1,0:T(1,128)} %param.21) | copy-start | bytes 24580
  30.6 0.6 copy-start.14
  31.2 0.6 copy-start.15
  32.9 22.6 %collective-permute-start.2 = (f32[2,8,66,1]{2,1,3,0:T(8,128)}, f32[2,8,66,1]{2,1,3,0:T(8,128)S(1)}, u32[]{:S(2)}, u32[]{:S(2)}) collective-permute-start(f32[2,8,66,1]{2,1,3,0:T(8,128)} %copy.183), channel_id=1, source_target_pairs={{0,1},{1,2},{2,3},{3,4},{4,5},{5,6},{6,7},{7,128},{128,129},{129,1... | collective-permute-start | bytes 12680 | tf_op jit(solution)/shard_map/ppermute | solution.py:31
  35.1 20.8 %collective-permute-start.3 = (f32[2,8,66,1]{2,1,3,0:T(8,128)S(1)}, f32[2,8,66,1]{2,1,3,0:T(8,128)S(1)}, u32[]{:S(2)}, u32[]{:S(2)}) collective-permute-start(f32[2,8,66,1]{2,1,3,0:T(8,128)S(1)} %copy.185), channel_id=1, source_target_pairs={{1,0},{2,1},{3,2},{4,3},{5,4},{6,5},{7,6},{128,7},{129,128},{130,1... | collective-permute-start | bytes 12680 | tf_op jit(solution)/shard_map/ppermute | solution.py:32
  46.4 77.5 %collective-permute-start.18 = (f32[3,1,5,512]{3,1,2,0:T(1,128)}, f32[3,1,5,512]{3,1,2,0:T(1,128)}, u32[]{:S(2)}, u32[]{:S(2)}) collective-permute-start(f32[3,1,5,512]{3,1,2,0:T(1,128)} %copy_dynamic-update-slice_fusion), channel_id=1, source_target_pairs={{0,1},{1,2},{2,3},{3,4},{4,5},{5,6},{6,7},{7,128},{128,129},{129,1... | collective-permute-start | bytes 92168 | tf_op jit(solution)/shard_map/ppermute | solution.py:31
  48.3 75.6 %collective-permute-start.19 = (f32[3,1,5,512]{3,1,2,0:T(1,128)}, f32[3,1,5,512]{3,1,2,0:T(1,128)}, u32[]{:S(2)}, u32[]{:S(2)}) collective-permute-start(f32[3,1,5,512]{3,1,2,0:T(1,128)} %copy_dynamic-update-slice_fusion), channel_id=1, source_target_pairs={{1,0},{2,1},{3,2},{4,3},{5,4},{6,5},{7,6},{128,7},{129,128},{130,1... | collective-permute-start | bytes 92168 | tf_op jit(solution)/shard_map/ppermute | solution.py:32
  59.0 8.1 %collective-permute-start.4 = (f32[2,8,1,128]{3,1,2,0:T(8,128)S(1)}, f32[2,8,1,128]{3,1,2,0:T(8,128)S(1)}, u32[]{:S(2)}, u32[]{:S(2)}) collective-permute-start(f32[2,8,1,128]{3,1,2,0:T(8,128)S(1)} %get-tuple-element.118), channel_id=1, source_target_pairs={{0,8},{8,16},{16,24},{24,32},{32,40},{40,48},{48,56},{56,64},{64,7... | collective-permute-start | bytes 24584 | tf_op jit(solution)/shard_map/ppermute | solution.py:31
  60.9 7.4 %collective-permute-start.5 = (f32[2,8,1,128]{3,1,2,0:T(8,128)S(1)}, f32[2,8,1,128]{3,1,2,0:T(8,128)S(1)}, u32[]{:S(2)}, u32[]{:S(2)}) collective-permute-start(f32[2,8,1,128]{3,1,2,0:T(8,128)S(1)} %get-tuple-element.119), channel_id=1, source_target_pairs={{8,0},{16,8},{24,16},{32,24},{40,32},{48,40},{56,48},{64,56},{72,6... | collective-permute-start | bytes 24584 | tf_op jit(solution)/shard_map/ppermute | solution.py:32
  71.2 10.8 %collective-permute-start.6 = (f32[2,8,66,1]{2,1,3,0:T(8,128)}, f32[2,8,66,1]{2,1,3,0:T(8,128)}, u32[]{:S(2)}, u32[]{:S(2)}) collective-permute-start(f32[2,8,66,1]{2,1,3,0:T(8,128)} %copy.187), channel_id=1, source_target_pairs={{0,1},{1,2},{2,3},{3,4},{4,5},{5,6},{6,7},{7,128},{128,129},{129,1... | collective-permute-start | bytes 12680 | tf_op jit(solution)/shard_map/ppermute | solution.py:31
  74.0 9.8 %collective-permute-start.7 = (f32[2,8,66,1]{2,1,3,0:T(8,128)}, f32[2,8,66,1]{2,1,3,0:T(8,128)S(1)}, u32[]{:S(2)}, u32[]{:S(2)}) collective-permute-start(f32[2,8,66,1]{2,1,3,0:T(8,128)} %copy.189), channel_id=1, source_target_pairs={{1,0},{2,1},{3,2},{4,3},{5,4},{6,5},{7,6},{128,7},{129,128},{130,1... | collective-permute-start | bytes 12680 | tf_op jit(solution)/shard_map/ppermute | solution.py:32
  86.6 9.1 %collective-permute-start.8 = (f32[2,8,1,128]{3,1,2,0:T(8,128)S(1)}, f32[2,8,1,128]{3,1,2,0:T(8,128)S(1)}, u32[]{:S(2)}, u32[]{:S(2)}) collective-permute-start(f32[2,8,1,128]{3,1,2,0:T(8,128)S(1)} %get-tuple-element.114), channel_id=1, source_target_pairs={{0,8},{8,16},{16,24},{24,32},{32,40},{40,48},{48,56},{56,64},{64,7... | collective-permute-start | bytes 24584 | tf_op jit(solution)/shard_map/ppermute | solution.py:31
  88.6 7.7 %collective-permute-start.9 = (f32[2,8,1,128]{3,1,2,0:T(8,128)S(1)}, f32[2,8,1,128]{3,1,2,0:T(8,128)S(1)}, u32[]{:S(2)}, u32[]{:S(2)}) collective-permute-start(f32[2,8,1,128]{3,1,2,0:T(8,128)S(1)} %get-tuple-element.115), channel_id=1, source_target_pairs={{8,0},{16,8},{24,16},{32,24},{40,32},{48,40},{56,48},{64,56},{72,6... | collective-permute-start | bytes 24584 | tf_op jit(solution)/shard_map/ppermute | solution.py:32
  97.5 14.8 %copy-start.3 = (f32[2,7,64,128]{3,1,2,0:T(8,128)S(1)}, f32[2,7,64,128]{3,1,2,0:T(8,128)}, u32[]{:S(2)}) copy-start(f32[2,7,64,128]{3,1,2,0:T(8,128)} %fusion.33) | copy-start | bytes 1376260
  98.8 11.2 %collective-permute-start.10 = (f32[2,8,66,1]{2,1,3,0:T(8,128)S(1)}, f32[2,8,66,1]{2,1,3,0:T(8,128)S(1)}, u32[]{:S(2)}, u32[]{:S(2)}) collective-permute-start(f32[2,8,66,1]{2,1,3,0:T(8,128)S(1)} %copy.191), channel_id=1, source_target_pairs={{0,1},{1,2},{2,3},{3,4},{4,5},{5,6},{6,7},{7,128},{128,129},{129,1... | collective-permute-start | bytes 12680 | tf_op jit(solution)/shard_map/ppermute | solution.py:31
  102.0 9.1 %collective-permute-start.11 = (f32[2,8,66,1]{2,1,3,0:T(8,128)S(1)}, f32[2,8,66,1]{2,1,3,0:T(8,128)S(1)}, u32[]{:S(2)}, u32[]{:S(2)}) collective-permute-start(f32[2,8,66,1]{2,1,3,0:T(8,128)S(1)} %copy.193), channel_id=1, source_target_pairs={{1,0},{2,1},{3,2},{4,3},{5,4},{6,5},{7,6},{128,7},{129,128},{130,1... | collective-permute-start | bytes 12680 | tf_op jit(solution)/shard_map/ppermute | solution.py:32
  115.6 9.9 %collective-permute-start.12 = (f32[2,8,1,128]{3,1,2,0:T(8,128)S(1)}, f32[2,8,1,128]{3,1,2,0:T(8,128)S(1)}, u32[]{:S(2)}, u32[]{:S(2)}) collective-permute-start(f32[2,8,1,128]{3,1,2,0:T(8,128)S(1)} %get-tuple-element.110), channel_id=1, source_target_pairs={{0,8},{8,16},{16,24},{24,32},{32,40},{40,48},{48,56},{56,64},{64,7... | collective-permute-start | bytes 24584 | tf_op jit(solution)/shard_map/ppermute | solution.py:31
  117.9 7.6 %collective-permute-start.13 = (f32[2,8,1,128]{3,1,2,0:T(8,128)S(1)}, f32[2,8,1,128]{3,1,2,0:T(8,128)S(1)}, u32[]{:S(2)}, u32[]{:S(2)}) collective-permute-start(f32[2,8,1,128]{3,1,2,0:T(8,128)S(1)} %get-tuple-element.111), channel_id=1, source_target_pairs={{8,0},{16,8},{24,16},{32,24},{40,32},{48,40},{56,48},{64,56},{72,6... | collective-permute-start | bytes 24584 | tf_op jit(solution)/shard_map/ppermute | solution.py:32
  125.5 11.8 %copy-start.8 = (f32[16,5,128]{2,1,0:T(8,128)S(1)}, f32[16,5,128]{2,1,0:T(8,128)}, u32[]{:S(2)}) copy-start(f32[16,5,128]{2,1,0:T(8,128)} %maximum_bitcast_fusion) | copy-start | bytes 122884
  125.5 0.6 copy-start.16
  126.1 0.6 copy-start.17
  127.8 10.4 %collective-permute-start.14 = (f32[2,8,66,1]{2,1,3,0:T(8,128)}, f32[2,8,66,1]{2,1,3,0:T(8,128)S(1)}, u32[]{:S(2)}, u32[]{:S(2)}) collective-permute-start(f32[2,8,66,1]{2,1,3,0:T(8,128)} %copy.195), channel_id=1, source_target_pairs={{0,1},{1,2},{2,3},{3,4},{4,5},{5,6},{6,7},{7,128},{128,129},{129,1... | collective-permute-start | bytes 12680 | tf_op jit(solution)/shard_map/ppermute | solution.py:31
  130.0 8.6 %collective-permute-start.15 = (f32[2,8,66,1]{2,1,3,0:T(8,128)S(1)}, f32[2,8,66,1]{2,1,3,0:T(8,128)}, u32[]{:S(2)}, u32[]{:S(2)}) collective-permute-start(f32[2,8,66,1]{2,1,3,0:T(8,128)S(1)} %copy.197), channel_id=1, source_target_pairs={{1,0},{2,1},{3,2},{4,3},{5,4},{6,5},{7,6},{128,7},{129,128},{130,1... | collective-permute-start | bytes 12680 | tf_op jit(solution)/shard_map/ppermute | solution.py:32
  138.5 3.7 %copy-start.5 = (f32[2,64,128]{2,1,0:T(8,128)S(1)}, f32[2,64,128]{2,1,0:T(8,128)}, u32[]{:S(2)}) copy-start(f32[2,64,128]{2,1,0:T(8,128)} %param.16) | copy-start | bytes 196612
  141.4 0.8 copy-start.1
  142.3 15.6 %collective-permute-start.20 = (f32[4,32,128]{2,1,0:T(8,128)S(1)}, f32[4,32,128]{2,1,0:T(8,128)S(1)}, u32[]{:S(2)}, u32[]{:S(2)}) collective-permute-start(f32[4,32,128]{2,1,0:T(8,128)S(1)} %get-tuple-element.129), channel_id=1, source_target_pairs={{0,8},{8,16},{16,24},{24,32},{32,40},{40,48},{48,56},{56,64},{64,7... | collective-permute-start | bytes 196616 | tf_op jit(solution)/shard_map/ppermute | solution.py:31
  144.2 13.7 %collective-permute-start.21 = (f32[4,32,128]{2,1,0:T(8,128)S(1)}, f32[4,32,128]{2,1,0:T(8,128)S(1)}, u32[]{:S(2)}, u32[]{:S(2)}) collective-permute-start(f32[4,32,128]{2,1,0:T(8,128)S(1)} %get-tuple-element.130), channel_id=1, source_target_pairs={{8,0},{16,8},{24,16},{32,24},{40,32},{48,40},{56,48},{64,56},{72,6... | collective-permute-start | bytes 196616 | tf_op jit(solution)/shard_map/ppermute | solution.py:32
  157.9 4.7 %copy-start.13 = (s32[2048]{0:T(1024)S(1)}, s32[2048]{0:T(1024)}, u32[]{:S(2)}) copy-start(s32[2048]{0:T(1024)} %broadcast_clamp_fusion) | copy-start | bytes 24580
  157.9 14.0 %copy-start.20 = (pred[2048]{0:T(1024)(128)(4,1)S(1)}, pred[2048]{0:T(1024)(128)(4,1)}, u32[]{:S(2)}) copy-start(pred[2048]{0:T(1024)(128)(4,1)} %compare_and_fusion) | copy-start | bytes 6148
  157.9 14.1 %copy-start.12 = (f32[1,1,2048]{2,1,0:T(1,128)S(1)}, f32[1,1,2048]{2,1,0:T(1,128)}, u32[]{:S(2)}) copy-start(f32[1,1,2048]{2,1,0:T(1,128)} %param.21) | copy-start | bytes 24580
  162.6 12.2 %copy-start = (f32[1,2048]{0,1:T(8,128)S(1)}, f32[1,2048]{0,1:T(8,128)}, u32[]{:S(2)}) copy-start(f32[1,2048]{0,1:T(8,128)} %copy.208) | copy-start | bytes 24580
  178.3 3.1 %copy-start.21 = (pred[8,128]{1,0:T(8,128)(4,1)S(1)}, pred[8,128]{1,0:T(8,128)(4,1)}, u32[]{:S(2)}) copy-start(pred[8,128]{1,0:T(8,128)(4,1)} %get-tuple-element.133) | copy-start | bytes 3076
  178.3 3.1 %copy-start.22 = (pred[8,128]{1,0:T(8,128)(4,1)S(1)}, pred[8,128]{1,0:T(8,128)(4,1)}, u32[]{:S(2)}) copy-start(pred[8,128]{1,0:T(8,128)(4,1)} %get-tuple-element.134) | copy-start | bytes 3076
  178.3 29.0 %copy-start.2 = (f32[2,8,64,128]{3,1,2,0:T(8,128)S(1)}, f32[2,8,64,128]{3,1,2,0:T(8,128)}, u32[]{:S(2)}) copy-start(f32[2,8,64,128]{3,1,2,0:T(8,128)} %copy-done.1) | copy-start | bytes 1572868
  181.4 9.2 %collective-permute-start.22 = (f32[1,1,8,38,128]{4,2,3,1,0:T(8,128)S(1)}, f32[1,1,8,38,128]{4,2,3,1,0:T(8,128)S(1)}, u32[]{:S(2)}, u32[]{:S(2)}) collective-permute-start(f32[1,1,8,38,128]{4,2,3,1,0:T(8,128)S(1)} %select_bitcast_fusion), channel_id=1, source_target_pairs={{0,8},{8,16},{16,24},{24,32},{32,40},{40,48},{48,56},{56,64},{64,7... | collective-permute-start | bytes 466952 | tf_op jit(solution)/shard_map/ppermute | solution.py:31
  183.3 8.8 %collective-permute-start.23 = (f32[1,1,8,38,128]{4,2,3,1,0:T(8,128)S(1)}, f32[1,1,8,38,128]{4,2,3,1,0:T(8,128)S(1)}, u32[]{:S(2)}, u32[]{:S(2)}) collective-permute-start(f32[1,1,8,38,128]{4,2,3,1,0:T(8,128)S(1)} %select_bitcast_fusion), channel_id=1, source_target_pairs={{8,0},{16,8},{24,16},{32,24},{40,32},{48,40},{56,48},{64,56},{72,6... | collective-permute-start | bytes 466952 | tf_op jit(solution)/shard_map/ppermute | solution.py:32
  192.1 19.5 %collective-permute-start.24 = (f32[3,1,8,38,128]{4,2,3,1,0:T(8,128)S(1)}, f32[3,1,8,38,128]{4,2,3,1,0:T(8,128)S(1)}, u32[]{:S(2)}, u32[]{:S(2)}) collective-permute-start(f32[3,1,8,38,128]{4,2,3,1,0:T(8,128)S(1)} %pad_maximum_fusion.37), channel_id=1, source_target_pairs={{0,1},{1,2},{2,3},{3,4},{4,5},{5,6},{6,7},{7,128},{128,129},{129,1... | collective-permute-start | bytes 1400840 | tf_op jit(solution)/shard_map/ppermute | solution.py:31
  194.0 19.4 %collective-permute-start.25 = (f32[3,1,8,38,128]{4,2,3,1,0:T(8,128)S(1)}, f32[3,1,8,38,128]{4,2,3,1,0:T(8,128)S(1)}, u32[]{:S(2)}, u32[]{:S(2)}) collective-permute-start(f32[3,1,8,38,128]{4,2,3,1,0:T(8,128)S(1)} %pad_maximum_fusion.37), channel_id=1, source_target_pairs={{1,0},{2,1},{3,2},{4,3},{5,4},{6,5},{7,6},{128,7},{129,128},{130,1... | collective-permute-start | bytes 1400840 | tf_op jit(solution)/shard_map/ppermute | solution.py:32
where the time goes:
time: 219 us; the launch traced here: 215 us
  starting transfers between devices  119 us (54%)
  local copies, waits for them, and re-layouts  55.5 us (25%)
  other arithmetic  28.1 us (13%)
  waiting for transfers between devices  9.1 us (4%)
    ppermute x13, starting transfers between devices, with_halo(): after = lax.ppermute(leading, axis, down)  92 us
    ppermute x13, starting transfers between devices, with_halo(): before = lax.ppermute(last, axis, up)  27.3 us
    gather x2, local copies, waits for them, and re-layouts, shards(): jnp.take(near.reshape(4, -1), cells - first_row * cols_here, axis=1)  9.26 us
    slice x13, local copies, waits for them, and re-layouts, with_halo(): last = lax.slice_in_dim(array, length - width, length, axis=dim)  7.6 us
    mul x4, other arithmetic, ocean_substep(): return (flow + horizontal * lap + vert + turning + surface) * wet[None]  7.26 us
    unnamed x55, local copies, waits for them, and re-layouts  7.14 us
    concatenate x3, local copies, waits for them, and re-layouts, with_halo(): array = jnp.concatenate([before, array, after], axis=dim)  6.05 us
    reduce_sum x1, other arithmetic, pair_forces(): jnp.sum(magnitude * normal_x, axis=2)  5.12 us
  transfers between devices with their start and end apart: 26, of which 7 were waited for; matrix products, arithmetic and copies ran while one was open for 24% of the time, Pallas kernels for 0%

commit v1 on v0

--- a/solution.py
+++ b/solution.py
@@ -93,6 +93,15 @@
     return jnp.einsum("pn,pcf->ncf", onehot, forces, precision=lax.Precision.HIGHEST)
 
 
+def exchange(low, high, axis):
+    size = lax.axis_size(axis)
+    up = [(i, i + 1) for i in range(size - 1)]
+    down = [(i + 1, i) for i in range(size - 1)]
+    from_previous = lax.ppermute(high, axis, up)
+    from_next = lax.ppermute(low, axis, down)
+    return from_previous, from_next
+
+
 def shards(
     ocean_velocity,
     wind_stress,
@@ -108,17 +117,9 @@
     move_index,
     move_count,
 ):
-    levels_here = ocean_velocity.shape[1]
-    rows_here = ocean_velocity.shape[2]
-    cols_here = ocean_velocity.shape[3]
-    wet = (jnp.arange(levels_here, dtype=jnp.int32)[:, None, None] < level_counts[None]).astype(
-        jnp.float32
-    )
-    flow = ocean_velocity * wet[None]
-    for substep in range(OSTEPS):
-        padded = with_halo(flow, (("gx", 2), (("sec", "gy"), 3)), 1)
-        flow = ocean_substep(flow, padded, wet, wind_stress)
-    surface = jnp.stack([flow[0, 0], flow[1, 0], wind_stress[0], wind_stress[1]])
+    columns = ("sec", "gy")
+    comps, levels_here, rows_here, cols_here = ocean_velocity.shape
+    halo = OSTEPS
     position = floe_position[0, 0]
     velocity = floe_velocity[0, 0]
     radius = floe_radius[0, 0]
@@ -128,12 +129,67 @@
     blocks = floes // 128
     record = jnp.concatenate([position, velocity, radius[None]], axis=0)
     edge = record[:, : GHOST * 128]
-    beside_all = with_halo(edge[None, None], (("gx", 0), (("sec", "gy"), 1)), 1)
-    beside_all = beside_all.reshape(9, 5, GHOST * 128)
-    ghosts = jnp.concatenate([beside_all[:4], beside_all[5:]], axis=0)
+    edge_size = edge.size
+
+    fields = jnp.concatenate(
+        [
+            ocean_velocity.reshape(comps * levels_here, rows_here, cols_here),
+            wind_stress,
+            level_counts.astype(jnp.float32)[None],
+        ],
+        axis=0,
+    )
+    channels = fields.shape[0]
+    row_strip = channels * halo * cols_here
+    low = jnp.concatenate([fields[:, :halo].reshape(-1), edge.reshape(-1)])
+    high = jnp.concatenate([fields[:, -halo:].reshape(-1), edge.reshape(-1)])
+    above, below = exchange(low, high, "gx")
+    extended = jnp.concatenate(
+        [
+            above[:row_strip].reshape(channels, halo, cols_here),
+            fields,
+            below[:row_strip].reshape(channels, halo, cols_here),
+        ],
+        axis=1,
+    )
+    ghost_column = jnp.stack(
+        [above[row_strip:].reshape(edge.shape), edge, below[row_strip:].reshape(edge.shape)]
+    )
+    ext_rows = rows_here + 2 * halo
+    col_strip = channels * ext_rows * halo
+    low = jnp.concatenate([extended[:, :, :halo].reshape(-1), ghost_column.reshape(-1)])
+    high = jnp.concatenate([extended[:, :, -halo:].reshape(-1), ghost_column.reshape(-1)])
+    left, right = exchange(low, high, columns)
+    extended = jnp.concatenate(
+        [
+            left[:col_strip].reshape(channels, ext_rows, halo),
+            extended,
+            right[:col_strip].reshape(channels, ext_rows, halo),
+        ],
+        axis=2,
+    )
+    ghost_left = left[col_strip:].reshape(3, *edge.shape)
+    ghost_right = right[col_strip:].reshape(3, *edge.shape)
+    beside = [ghost_left, ghost_column, ghost_right]
+    ghosts = jnp.stack([beside[p % 3][p // 3] for p in PLACES])
+
+    ext_cols = cols_here + 2 * halo
+    counts_ext = extended[-1]
+    wet = (jnp.arange(levels_here, dtype=jnp.float32)[:, None, None] < counts_ext[None]).astype(
+        jnp.float32
+    )
+    wind_ext = extended[comps * levels_here : comps * levels_here + 2]
+    flow = extended[: comps * levels_here].reshape(comps, levels_here, ext_rows, ext_cols) * wet[None]
+    for substep in range(OSTEPS):
+        padded = jnp.pad(flow, ((0, 0), (0, 0), (1, 1), (1, 1)))
+        flow = ocean_substep(flow, padded, wet, wind_ext)
+    flow = flow[:, :, halo : halo + rows_here, halo : halo + cols_here]
+
     table = block_table(record, ghosts)
+    surface = jnp.stack([flow[0, 0], flow[1, 0], wind_stress[0], wind_stress[1]])
     margin = rows_here // 2
-    near = with_halo(surface, (("gx", 1),), margin)
+    from_above, from_below = exchange(surface[:, :margin], surface[:, -margin:], "gx")
+    near = jnp.concatenate([from_above, surface, from_below], axis=1)
     first_row = lax.axis_index("gx") * rows_here - margin
     sampled = jnp.take(near.reshape(4, -1), cells - first_row * cols_here, axis=1)
     lists = contact_list[0, 0]
@@ -168,10 +224,22 @@
     )
     valid_slots = jnp.arange(capacity, dtype=jnp.int32)[None, :] < move_count[0, 0][:, None]
     outgoing = jnp.where(valid_slots[:, None, :], taken, 0.0)
-    landed = with_halo(outgoing[None, None], (("gx", 0), (("sec", "gy"), 1)), 1)
-    landed = landed.reshape(9, 8, width, capacity)
-    arrived = [landed[8 - PLACES[way], way] for way in range(8)]
-    arrivals = jnp.stack(arrived, axis=0)
+    from_above, from_below = exchange(outgoing[0:3], outgoing[5:8], "gx")
+    heading_left = jnp.stack([from_below[0], outgoing[3], from_above[0]])
+    heading_right = jnp.stack([from_below[2], outgoing[4], from_above[2]])
+    from_left, from_right = exchange(heading_left, heading_right, columns)
+    arrivals = jnp.stack(
+        [
+            from_right[0],
+            from_below[1],
+            from_left[0],
+            from_right[1],
+            from_left[1],
+            from_right[2],
+            from_above[1],
+            from_left[2],
+        ]
+    )
     return (flow, floe_next[None, None], arrivals[None, None])
 
 

time: 219 us -> 110 us (0.50); the launches traced: 215 us -> 110 us
  starting transfers between devices: 119 us -> 32.9 us
  local copies, waits for them, and re-layouts: 55.5 us -> 34.6 us
  waiting for transfers between devices: 9.1 us -> 17.4 us
  other arithmetic: 28.1 us -> 22.8 us
    ppermute x26 -> x10, starting transfers between devices: 119 us -> 32.9 us  [the longest x5 20.8 us: exchange(): from_next = lax.ppermute(low, axis, down)]
    ppermute x26 -> x10, waiting for transfers between devices: 9.1 us -> 17.4 us  [the longest x5 15.4 us: exchange(): from_previous = lax.ppermute(high, axis, up)]
    slice x19 -> x26, local copies, waits for them, and re-layouts: 10.3 us -> 2.43 us  [the longest x1 1 us: shards(): flow = flow[:, :, halo:halo + rows_here, halo:halo + cols_here]]
    ppermute x8 -> x0, local copies, waits for them, and re-layouts: 7.77 us -> none  [the longest x4 4.28 us: with_halo(): after = lax.ppermute(leading, axis, down)]
    unnamed x55 -> x33, local copies, waits for them, and re-layouts: 7.14 us -> 0.41 us
    reduce_sum x1 -> x2, other arithmetic: 5.12 us -> 10.2 us  [pair_forces(): jnp.sum(magnitude * normal_x, axis=2)]
    mul x4, other arithmetic: 7.26 us -> 4.37 us  [ocean_substep(): return (flow + horizontal * lap + vert + turning + surface) * wet[None]]
    mul x4, other arithmetic: 2.98 us -> 0.42 us  [ocean_substep(): turning = jnp.stack([CORIOLIS * flow[1], -CORIOLIS * flow[0]])]
  transfers between devices with their start and end apart: 26 -> 10, of which waited for: 7 -> 4; matrix products, arithmetic and copies ran while one was open for 24% -> 19% of each run, Pallas kernels for 0% -> 0%
where the time goes in v1:
time: 110 us
  local copies, waits for them, and re-layouts  34.6 us (31%)
  starting transfers between devices  32.9 us (30%)
  other arithmetic  22.8 us (21%)
  waiting for transfers between devices  17.4 us (16%)
  between operations  2.12 us (2%)
    ppermute x5, starting transfers between devices, exchange(): from_next = lax.ppermute(low, axis, down)  20.8 us
    ppermute x5, waiting for transfers between devices, exchange(): from_previous = lax.ppermute(high, axis, up)  15.4 us
    ppermute x5, starting transfers between devices, exchange(): from_previous = lax.ppermute(high, axis, up)  12.1 us
    reduce_sum x2, other arithmetic, pair_forces(): jnp.sum(magnitude * normal_x, axis=2)  10.2 us
    gather x2, local copies, waits for them, and re-layouts, shards(): jnp.take(near.reshape(4, -1), cells - first_row * cols_here, axis=1)  9.17 us
    concatenate x1, local copies, waits for them, and re-layouts, shards(): near = jnp.concatenate([from_above, surface, from_below], axis=1)  4.75 us
    mul x4, other arithmetic, ocean_substep(): return (flow + horizontal * lap + vert + turning + surface) * wet[None]  4.37 us
    concatenate x1, local copies, waits for them, and re-layouts, shards(): jnp.concatenate([floe_next, radius[None], mass[None], floe_polygon[0, 0]]...  3.45 us
  transfers between devices with their start and end apart: 10, of which 4 were waited for; matrix products, arithmetic and copies ran while one was open for 19% of the time, Pallas kernels for 0%

profile of v1, /device:TPU:24, one launch (start us, length us, event | category | flops | bytes accessed | tf_op | source)
XLA Modules:
  0.0 110.5 jit_solution(2440443101484812520)
XLA Ops:
  0.7 0.8 pad_maximum_fusion.16
  1.5 0.8 convert_bitcast_fusion
  2.3 0.9 pad_maximum_fusion.15
  3.3 7.9 %collective-permute-start.1 = (f32[12288]{0:T(1024)S(1)}, f32[12288]{0:T(1024)S(1)}, u32[]{:S(2)}, u32[]{:S(2)}) collective-permute-start(f32[12288]{0:T(1024)S(1)} %get-tuple-element.120), channel_id=1, source_target_pairs={{8,0},{16,8},{24,16},{32,24},{40,32},{48,40},{56,48},{64,56},{72,6... | collective-permute-start | bytes 147464 | tf_op jit(solution)/shard_map/ppermute | solution.py:101
  11.2 1.9 %collective-permute-start = (f32[12288]{0:T(1024)S(1)}, f32[12288]{0:T(1024)S(1)}, u32[]{:S(2)}, u32[]{:S(2)}) collective-permute-start(f32[12288]{0:T(1024)S(1)} %get-tuple-element.119), channel_id=1, source_target_pairs={{0,8},{8,16},{16,24},{24,32},{32,40},{40,48},{48,56},{56,64},{64,7... | collective-permute-start | bytes 147464 | tf_op jit(solution)/shard_map/ppermute | solution.py:100
  13.4 5.9 %collective-permute-done = f32[12288]{0:T(1024)S(1)} collective-permute-done((f32[12288]{0:T(1024)S(1)}, f32[12288]{0:T(1024)S(1)}, u32[]{:S(2)}, u32[]{:S(2)}) %collective-permute-start) | collective-permute-done | bytes 49184 | tf_op jit(solution)/shard_map/ppermute | solution.py:100
  19.5 0.2 fusion.67
  19.8 0.4 reshape.318
  20.2 0.4 reshape.321
  20.6 3.0 %collective-permute-start.3 = (f32[13152]{0:T(1024)S(1)}, f32[13152]{0:T(1024)S(1)}, u32[]{:S(2)}, u32[]{:S(2)}) collective-permute-start(f32[13152]{0:T(1024)S(1)} %get-tuple-element.118), channel_id=1, source_target_pairs={{1,0},{2,1},{3,2},{4,3},{5,4},{6,5},{7,6},{128,7},{129,128},{130,1... | collective-permute-start | bytes 157832 | tf_op jit(solution)/shard_map/ppermute | solution.py:101
  23.6 1.9 %collective-permute-start.2 = (f32[13152]{0:T(1024)S(1)}, f32[13152]{0:T(1024)S(1)}, u32[]{:S(2)}, u32[]{:S(2)}) collective-permute-start(f32[13152]{0:T(1024)S(1)} %get-tuple-element.117), channel_id=1, source_target_pairs={{0,1},{1,2},{2,3},{3,4},{4,5},{5,6},{6,7},{7,128},{128,129},{129,1... | collective-permute-start | bytes 157832 | tf_op jit(solution)/shard_map/ppermute | solution.py:100
  26.2 1.4 %copy.70 = f32[1,2048]{0,1:T(8,128)} copy(f32[1,2048]{1,0:T(1,128)S(1)} %bitcast.162) | data formatting | bytes 16384 | tf_op jit(solution)/shard_map/broadcast_in_dim;squeeze | solution.py:130
  27.6 1.4 %copy.71 = f32[1,2048]{0,1:T(8,128)} copy(f32[1,2048]{1,0:T(1,128)S(1)} %bitcast.165) | data formatting | bytes 16384 | tf_op jit(solution)/shard_map/broadcast_in_dim;squeeze | solution.py:213
  29.0 0.3 copy.67
  29.3 0.7 reshape.322
  30.1 2.7 %collective-permute-done.2 = f32[13152]{0:T(1024)S(1)} collective-permute-done((f32[13152]{0:T(1024)S(1)}, f32[13152]{0:T(1024)S(1)}, u32[]{:S(2)}, u32[]{:S(2)}) %collective-permute-start.2) | collective-permute-done | bytes 52640 | tf_op jit(solution)/shard_map/ppermute | solution.py:100
  32.7 0.7 reshape.320
  33.4 0.1 fusion.61
  33.6 0.7 pad_maximum_fusion
  34.6 0.1 broadcast_multiply_fusion
  34.7 0.1 slice_multiply_fusion.7
  34.8 0.2 fusion.59
  35.0 1.1 fusion.52
  36.1 0.1 slice_multiply_fusion.5
  36.2 0.2 fusion.58
  36.4 1.1 fusion.53
  37.5 0.1 slice_multiply_fusion.3
  37.6 0.2 fusion.57
  37.7 1.1 fusion.54
  38.8 0.1 slice_multiply_fusion.1
  39.0 0.2 fusion.56
  39.1 1.1 fusion.55
  40.3 0.6 fusion.71
  41.0 1.9 %collective-permute-start.5 = (f32[4,32,128]{2,1,0:T(8,128)}, f32[4,32,128]{2,1,0:T(8,128)}, u32[]{:S(2)}, u32[]{:S(2)}) collective-permute-start(f32[4,32,128]{2,1,0:T(8,128)} %get-tuple-element.98), channel_id=1, source_target_pairs={{8,0},{16,8},{24,16},{32,24},{40,32},{48,40},{56,48},{64,56},{72,6... | collective-permute-start | bytes 196616 | tf_op jit(solution)/shard_map/ppermute | solution.py:101
  42.9 3.9 %collective-permute-start.4 = (f32[4,32,128]{2,1,0:T(8,128)S(1)}, f32[4,32,128]{2,1,0:T(8,128)}, u32[]{:S(2)}, u32[]{:S(2)}) collective-permute-start(f32[4,32,128]{2,1,0:T(8,128)S(1)} %get-tuple-element.97), channel_id=1, source_target_pairs={{0,8},{8,16},{16,24},{24,32},{32,40},{40,48},{48,56},{56,64},{64,7... | collective-permute-start | bytes 196616 | tf_op jit(solution)/shard_map/ppermute | solution.py:100
  47.2 15.0 %while.10 = (s32[]{:T(128)}, f32[16,2,128]{2,0,1:T(8,128)S(1)}, s32[]{:T(128)}, s32[3,64]{1,0:T(4,128)S(1)}, s32[]{:T(128)}, /*index=5*/f32[48,5,128]{2,1,0:T(8,...) while((s32[]{:T(128)}, f32[16,2,128]{2,0,1:T(8,128)S(1)}, s32[]{:T(128)}, s32[3,64]{1,0:T(4,128)S(1)}, ...), condition=%wide.region_3.4_spmd, body=%wide.region_0.0_spmd.sunk | while | flops 15219718 | bytes 928231 | solution.py:207
  47.4 0.6 gather_fusion
  48.0 0.6 gather_fusion.1
  48.7 5.1 %multiply_reduce_fusion.4 = (f32[32,128]{1,0:T(8,128)S(1)}, f32[32,128]{1,0:T(8,128)S(1)}) fusion(f32[32,128]{1,0:T(8,128)S(1)} %bitcast.144, f32[32,128]{1,0:T(8,128)S(1)} %bitcast.149, f32[32,128]{1,0:T(8,128)S(1)} %bitcast.145, f32[32,128]{1,0:T(8,128)S(1)} %bitcast.150, f32[32,128]{1,0:T(8,128)S(1)} %bitcast.146, f32[32,128]{1,0:T(8,128)S(1)} %bitcast.151, ...), kind=kLoop, calls=%fused_computation.17.clone.1 | loop fusion | flops 13623296 | bytes 196608 | tf_op jit(solution)/shard_map/while/body/reduce_sum | solution.py:70
  53.8 0.7 add_compare_fusion.2
  54.5 0.2 convolution_add_fusion.2
  54.8 0.6 gather_fusion
  55.5 0.6 gather_fusion.1
  56.1 5.1 %multiply_reduce_fusion.4 = (f32[32,128]{1,0:T(8,128)S(1)}, f32[32,128]{1,0:T(8,128)S(1)}) fusion(f32[32,128]{1,0:T(8,128)S(1)} %bitcast.144, f32[32,128]{1,0:T(8,128)S(1)} %bitcast.149, f32[32,128]{1,0:T(8,128)S(1)} %bitcast.145, f32[32,128]{1,0:T(8,128)S(1)} %bitcast.150, f32[32,128]{1,0:T(8,128)S(1)} %bitcast.146, f32[32,128]{1,0:T(8,128)S(1)} %bitcast.151, ...), kind=kLoop, calls=%fused_computation.17.clone.1 | loop fusion | flops 13623296 | bytes 196608 | tf_op jit(solution)/shard_map/while/body/reduce_sum | solution.py:70
  61.2 0.7 add_compare_fusion.2
  61.9 0.2 convolution_add_fusion.2
  62.3 1.0 slice.481
  63.3 0.9 pad_maximum_fusion.2
  64.2 4.7 %copy.65 = f32[4,128,128]{0,2,1:T(8,128)} copy(f32[4,128,128]{2,1,0:T(8,128)S(1)} %pad_maximum_fusion.2) | data formatting | bytes 524288 | tf_op jit(solution)/shard_map/concatenate | solution.py:192
  68.9 8.8 %gather_fusion.2 = f32[2048,4]{1,0:T(8,128)S(1)} fusion(f32[4,16384]{0,1:T(8,128)} %bitcast.137, s32[2048]{0:T(1024)S(1)} %broadcast_clamp_fusion), kind=kCustom, calls=%fused_computation.2 | custom fusion | bytes 73728 | tf_op jit(solution)/shard_map/jit(_take)/gather | solution.py:194
  77.8 0.3 copy.66
  78.2 1.4 %copy.68 = f32[2,2048]{0,1:T(8,128)} copy(f32[2,2048]{1,0:T(2,128)S(1)} %get-tuple-element.57) | data formatting | bytes 32768 | tf_op jit(solution)/shard_map/add | solution.py:214
  79.6 1.4 %copy.69 = f32[2,2048]{0,1:T(8,128)} copy(f32[2,2048]{1,0:T(2,128)S(1)} %get-tuple-element.58) | data formatting | bytes 32768 | tf_op jit(solution)/shard_map/add | solution.py:213
  81.0 3.4 %concatenate.104 = f32[38,2048]{0,1:T(8,128)S(1)} concatenate(f32[2,2048]{0,1:T(8,128)} %copy.68, f32[2,2048]{0,1:T(8,128)} %copy.69, f32[1,2048]{0,1:T(8,128)S(1)} %copy-done.1, f32[1,2048]{0,1:T(8,128)} %copy.71, f32[32,2048]{0,1:T(8,128)S(1)} %bitcast.139), dimensions={0} | concatenate | bytes 622592 | tf_op jit(solution)/shard_map/concatenate | solution.py:216
  84.4 2.8 %gather_fusion.3 = f32[1024,38]{1,0:T(8,128)S(1)} fusion(f32[38,2048]{0,1:T(8,128)S(1)} %concatenate.104, s32[1024]{0:T(1024)S(1)} %broadcast_clamp_fusion.1), kind=kCustom, calls=%fused_computation.3 | custom fusion | bytes 315392 | tf_op jit(solution)/shard_map/jit(_take)/gather | solution.py:221
  87.2 0.2 copy.72
  87.5 1.9 %collective-permute-start.7 = (f32[3,38,128]{2,0,1:T(4,128)S(1)}, f32[3,38,128]{2,0,1:T(4,128)S(1)}, u32[]{:S(2)}, u32[]{:S(2)}) collective-permute-start(f32[3,38,128]{2,0,1:T(4,128)S(1)} %get-tuple-element.92), channel_id=1, source_target_pairs={{0,8},{8,16},{16,24},{24,32},{32,40},{40,48},{48,56},{56,64},{64,7... | collective-permute-start | bytes 175112 | tf_op jit(solution)/shard_map/ppermute | solution.py:100
  89.5 0.6 maximum_bitcast_fusion.2
  90.1 6.0 %collective-permute-start.6 = (f32[3,38,128]{2,0,1:T(4,128)S(1)}, f32[3,38,128]{2,0,1:T(4,128)S(1)}, u32[]{:S(2)}, u32[]{:S(2)}) collective-permute-start(f32[3,38,128]{2,0,1:T(4,128)S(1)} %get-tuple-element.91), channel_id=1, source_target_pairs={{8,0},{16,8},{24,16},{32,24},{40,32},{48,40},{56,48},{64,56},{72,6... | collective-permute-start | bytes 175112 | tf_op jit(solution)/shard_map/ppermute | solution.py:101
  96.2 1.9 %collective-permute-done.6 = f32[3,38,128]{2,0,1:T(4,128)S(1)} collective-permute-done((f32[3,38,128]{2,0,1:T(4,128)S(1)}, f32[3,38,128]{2,0,1:T(4,128)S(1)}, u32[]{:S(2)}, u32[]{:S(2)}) %collective-permute-start.6) | collective-permute-done | bytes 58400 | tf_op jit(solution)/shard_map/ppermute | solution.py:101
  98.2 1.9 %collective-permute-start.8 = (f32[3,38,128]{2,0,1:T(4,128)S(1)}, f32[3,38,128]{2,0,1:T(4,128)S(1)}, u32[]{:S(2)}, u32[]{:S(2)}) collective-permute-start(f32[3,38,128]{2,0,1:T(4,128)S(1)} %pad_maximum_fusion.6), channel_id=1, source_target_pairs={{1,0},{2,1},{3,2},{4,3},{5,4},{6,5},{7,6},{128,7},{129,128},{130,1... | collective-permute-start | bytes 175112 | tf_op jit(solution)/shard_map/ppermute | solution.py:101
  100.2 2.4 %collective-permute-start.9 = (f32[3,38,128]{2,0,1:T(4,128)S(1)}, f32[3,38,128]{2,0,1:T(4,128)S(1)}, u32[]{:S(2)}, u32[]{:S(2)}) collective-permute-start(f32[3,38,128]{2,0,1:T(4,128)S(1)} %pad_maximum_fusion.7), channel_id=1, source_target_pairs={{0,1},{1,2},{2,3},{3,4},{4,5},{5,6},{6,7},{7,128},{128,129},{129,1... | collective-permute-start | bytes 175112 | tf_op jit(solution)/shard_map/ppermute | solution.py:100
  102.7 6.9 %collective-permute-done.9 = f32[3,38,128]{2,0,1:T(4,128)S(1)} collective-permute-done((f32[3,38,128]{2,0,1:T(4,128)S(1)}, f32[3,38,128]{2,0,1:T(4,128)S(1)}, u32[]{:S(2)}, u32[]{:S(2)}) %collective-permute-start.9) | collective-permute-done | bytes 58400 | tf_op jit(solution)/shard_map/ppermute | solution.py:100
  109.6 0.9 stack.61
  (109 shorter events, 2.1 us)
Async XLA Ops:
  0.6 12.7 %copy-start.6 = (f32[1,1,2048]{2,1,0:T(1,128)S(1)}, f32[1,1,2048]{2,1,0:T(1,128)}, u32[]{:S(2)}) copy-start(f32[1,1,2048]{2,1,0:T(1,128)} %param.20) | copy-start | bytes 24580
  0.6 12.7 %copy-start.4 = (f32[1,1,2,2048]{3,2,1,0:T(2,128)S(1)}, f32[1,1,2,2048]{3,2,1,0:T(2,128)}, u32[]{:S(2)}) copy-start(f32[1,1,2,2048]{3,2,1,0:T(2,128)} %param.19) | copy-start | bytes 49156
  0.7 12.7 %copy-start.5 = (f32[1,1,2,2048]{3,2,1,0:T(2,128)S(1)}, f32[1,1,2,2048]{3,2,1,0:T(2,128)}, u32[]{:S(2)}) copy-start(f32[1,1,2,2048]{3,2,1,0:T(2,128)} %param.18) | copy-start | bytes 49156
  0.7 18.8 %copy-start.2 = (f32[2,64,128]{2,1,0:T(8,128)S(1)}, f32[2,64,128]{2,1,0:T(8,128)}, u32[]{:S(2)}) copy-start(f32[2,64,128]{2,1,0:T(8,128)} %param.16) | copy-start | bytes 196612
  0.7 18.8 %copy-start = (f32[2,8,64,128]{3,2,1,0:T(8,128)S(1)}, f32[2,8,64,128]{3,2,1,0:T(8,128)}, u32[]{:S(2)}) copy-start(f32[2,8,64,128]{3,2,1,0:T(8,128)} %param.15) | copy-start | bytes 1572868
  0.7 12.5 %copy-start.9 = (s32[1,1,2048]{2,1,0:T(1,128)S(1)}, s32[1,1,2048]{2,1,0:T(1,128)}, u32[]{:S(2)}) copy-start(s32[1,1,2048]{2,1,0:T(1,128)} %param.23) | copy-start | bytes 24580
  0.7 12.5 %copy-start.8 = (s32[1,1,8,128]{3,2,1,0:T(8,128)S(1)}, s32[1,1,8,128]{3,2,1,0:T(8,128)}, u32[]{:S(2)}) copy-start(s32[1,1,8,128]{3,2,1,0:T(8,128)} %param.26) | copy-start | bytes 12292
  0.7 12.6 %copy-start.11 = (s32[1,1,8]{2,1,0:T(1,128)S(1)}, s32[1,1,8]{2,1,0:T(1,128)}, u32[]{:S(2)}) copy-start(s32[1,1,8]{2,1,0:T(1,128)} %param.27) | copy-start | bytes 100
  3.3 10.1 %collective-permute-start.1 = (f32[12288]{0:T(1024)S(1)}, f32[12288]{0:T(1024)S(1)}, u32[]{:S(2)}, u32[]{:S(2)}) collective-permute-start(f32[12288]{0:T(1024)S(1)} %get-tuple-element.120), channel_id=1, source_target_pairs={{8,0},{16,8},{24,16},{32,24},{40,32},{48,40},{56,48},{64,56},{72,6... | collective-permute-start | bytes 147464 | tf_op jit(solution)/shard_map/ppermute | solution.py:101
  11.2 8.1 %collective-permute-start = (f32[12288]{0:T(1024)S(1)}, f32[12288]{0:T(1024)S(1)}, u32[]{:S(2)}, u32[]{:S(2)}) collective-permute-start(f32[12288]{0:T(1024)S(1)} %get-tuple-element.119), channel_id=1, source_target_pairs={{0,8},{8,16},{16,24},{24,32},{32,40},{40,48},{48,56},{56,64},{64,7... | collective-permute-start | bytes 147464 | tf_op jit(solution)/shard_map/ppermute | solution.py:100
  20.1 7.5 %copy-start.10 = (s32[1,1,3,64]{3,1,2,0:T(1,128)S(1)}, s32[1,1,3,64]{3,1,2,0:T(1,128)}, u32[]{:S(2)}) copy-start(s32[1,1,3,64]{3,1,2,0:T(1,128)} %param.25) | copy-start | bytes 2308
  20.1 7.5 %copy-start.7 = (f32[1,1,2048]{2,1,0:T(1,128)S(1)}, f32[1,1,2048]{2,1,0:T(1,128)}, u32[]{:S(2)}) copy-start(f32[1,1,2048]{2,1,0:T(1,128)} %param.21) | copy-start | bytes 24580
  20.5 8.5 %copy-start.3 = (f32[1,1,32,2048]{3,2,1,0:T(8,128)S(1)}, f32[1,1,32,2048]{3,2,1,0:T(8,128)}, u32[]{:S(2)}) copy-start(f32[1,1,32,2048]{3,2,1,0:T(8,128)} %param.22) | copy-start | bytes 786436
  20.6 8.7 %collective-permute-start.3 = (f32[13152]{0:T(1024)S(1)}, f32[13152]{0:T(1024)S(1)}, u32[]{:S(2)}, u32[]{:S(2)}) collective-permute-start(f32[13152]{0:T(1024)S(1)} %get-tuple-element.118), channel_id=1, source_target_pairs={{1,0},{2,1},{3,2},{4,3},{5,4},{6,5},{7,6},{128,7},{129,128},{130,1... | collective-permute-start | bytes 157832 | tf_op jit(solution)/shard_map/ppermute | solution.py:101
  23.6 9.1 %collective-permute-start.2 = (f32[13152]{0:T(1024)S(1)}, f32[13152]{0:T(1024)S(1)}, u32[]{:S(2)}, u32[]{:S(2)}) collective-permute-start(f32[13152]{0:T(1024)S(1)} %get-tuple-element.117), channel_id=1, source_target_pairs={{0,1},{1,2},{2,3},{3,4},{4,5},{5,6},{6,7},{7,128},{128,129},{129,1... | collective-permute-start | bytes 157832 | tf_op jit(solution)/shard_map/ppermute | solution.py:100
  41.0 22.3 %collective-permute-start.5 = (f32[4,32,128]{2,1,0:T(8,128)}, f32[4,32,128]{2,1,0:T(8,128)}, u32[]{:S(2)}, u32[]{:S(2)}) collective-permute-start(f32[4,32,128]{2,1,0:T(8,128)} %get-tuple-element.98), channel_id=1, source_target_pairs={{8,0},{16,8},{24,16},{32,24},{40,32},{48,40},{56,48},{64,56},{72,6... | collective-permute-start | bytes 196616 | tf_op jit(solution)/shard_map/ppermute | solution.py:101
  42.9 20.4 %collective-permute-start.4 = (f32[4,32,128]{2,1,0:T(8,128)S(1)}, f32[4,32,128]{2,1,0:T(8,128)}, u32[]{:S(2)}, u32[]{:S(2)}) collective-permute-start(f32[4,32,128]{2,1,0:T(8,128)S(1)} %get-tuple-element.97), channel_id=1, source_target_pairs={{0,8},{8,16},{16,24},{24,32},{32,40},{40,48},{48,56},{56,64},{64,7... | collective-permute-start | bytes 196616 | tf_op jit(solution)/shard_map/ppermute | solution.py:100
  78.1 2.9 %copy-start.1 = (f32[1,2048]{0,1:T(8,128)S(1)}, f32[1,2048]{0,1:T(8,128)}, u32[]{:S(2)}) copy-start(f32[1,2048]{0,1:T(8,128)} %copy.70) | copy-start | bytes 24580
  87.5 8.6 %collective-permute-start.7 = (f32[3,38,128]{2,0,1:T(4,128)S(1)}, f32[3,38,128]{2,0,1:T(4,128)S(1)}, u32[]{:S(2)}, u32[]{:S(2)}) collective-permute-start(f32[3,38,128]{2,0,1:T(4,128)S(1)} %get-tuple-element.92), channel_id=1, source_target_pairs={{0,8},{8,16},{16,24},{24,32},{32,40},{40,48},{48,56},{56,64},{64,7... | collective-permute-start | bytes 175112 | tf_op jit(solution)/shard_map/ppermute | solution.py:100
  90.1 8.0 %collective-permute-start.6 = (f32[3,38,128]{2,0,1:T(4,128)S(1)}, f32[3,38,128]{2,0,1:T(4,128)S(1)}, u32[]{:S(2)}, u32[]{:S(2)}) collective-permute-start(f32[3,38,128]{2,0,1:T(4,128)S(1)} %get-tuple-element.91), channel_id=1, source_target_pairs={{8,0},{16,8},{24,16},{32,24},{40,32},{48,40},{56,48},{64,56},{72,6... | collective-permute-start | bytes 175112 | tf_op jit(solution)/shard_map/ppermute | solution.py:101
  98.2 4.4 %collective-permute-start.8 = (f32[3,38,128]{2,0,1:T(4,128)S(1)}, f32[3,38,128]{2,0,1:T(4,128)S(1)}, u32[]{:S(2)}, u32[]{:S(2)}) collective-permute-start(f32[3,38,128]{2,0,1:T(4,128)S(1)} %pad_maximum_fusion.6), channel_id=1, source_target_pairs={{1,0},{2,1},{3,2},{4,3},{5,4},{6,5},{7,6},{128,7},{129,128},{130,1... | collective-permute-start | bytes 175112 | tf_op jit(solution)/shard_map/ppermute | solution.py:101
  100.2 9.3 %collective-permute-start.9 = (f32[3,38,128]{2,0,1:T(4,128)S(1)}, f32[3,38,128]{2,0,1:T(4,128)S(1)}, u32[]{:S(2)}, u32[]{:S(2)}) collective-permute-start(f32[3,38,128]{2,0,1:T(4,128)S(1)} %pad_maximum_fusion.7), channel_id=1, source_target_pairs={{0,1},{1,2},{2,3},{3,4},{4,5},{5,6},{6,7},{7,128},{128,129},{129,1... | collective-permute-start | bytes 175112 | tf_op jit(solution)/shard_map/ppermute | solution.py:100

commit v2 on v1

--- a/solution.py
+++ b/solution.py
@@ -3,6 +3,8 @@
 import jax
 import jax.numpy as jnp
 from jax import lax
+from jax.experimental import pallas as pl
+from jax.experimental.pallas import tpu as pltpu
 from jax.sharding import PartitionSpec as P
 
 OSTEPS = 4
@@ -91,6 +93,67 @@
     forces = jnp.where(valid[:, None, None], forces, 0.0)
     onehot = (lists[0][:, None] == jnp.arange(blocks, dtype=jnp.int32)[None, :]).astype(jnp.float32)
     return jnp.einsum("pn,pcf->ncf", onehot, forces, precision=lax.Precision.HIGHEST)
+
+
+def split_three(x):
+    high = x.astype(jnp.bfloat16)
+    rest = x - high.astype(jnp.float32)
+    middle = rest.astype(jnp.bfloat16)
+    low = (rest - middle.astype(jnp.float32)).astype(jnp.bfloat16)
+    return high, middle, low
+
+
+def exact_select(parts, onehot):
+    high, middle, low = (jnp.dot(p, onehot, preferred_element_type=jnp.float32) for p in parts)
+    return (high + middle) + low
+
+
+def sample_kernel(window_ref, rows_ref, cols_ref, out_ref):
+    window_rows, window_cols = window_ref.shape[1:]
+    floes = rows_ref.shape[1]
+    onehot = (
+        lax.broadcasted_iota(jnp.int32, (window_rows, floes), 0) == rows_ref[...]
+    ).astype(jnp.bfloat16)
+    pick = lax.broadcasted_iota(jnp.int32, (window_cols, floes), 0) == cols_ref[...]
+    for channel in range(window_ref.shape[0]):
+        picked = exact_select(split_three(window_ref[channel].T), onehot)
+        out_ref[channel : channel + 1, :] = jnp.sum(
+            jnp.where(pick, picked, 0.0), axis=0, keepdims=True
+        )
+
+
+def sample_surface(window, rows, cols):
+    return pl.pallas_call(
+        sample_kernel,
+        out_shape=jax.ShapeDtypeStruct((window.shape[0], rows.shape[1]), jnp.float32),
+    )(window, rows, cols)
+
+
+def gather_kernel(state_ref, radius_ref, mass_ref, polygon_ref, index_ref, out_ref, head_ref):
+    floes = state_ref.shape[1]
+    slots = index_ref.shape[1]
+    head_ref[...] = jnp.zeros_like(head_ref)
+    head_ref[0:4, :] = state_ref[...]
+    head_ref[4:5, :] = radius_ref[...]
+    head_ref[5:6, :] = mass_ref[...]
+    head = split_three(head_ref[...])
+    polygon = split_three(polygon_ref[...])
+    rows = head_ref.shape[0]
+    for way in range(index_ref.shape[0]):
+        onehot = (
+            lax.broadcasted_iota(jnp.int32, (floes, slots), 0) == index_ref[way : way + 1, :]
+        ).astype(jnp.bfloat16)
+        out_ref[way, 0:rows, :] = exact_select(head, onehot)
+        out_ref[way, rows:, :] = exact_select(polygon, onehot)
+
+
+def gather_records(state, radius, mass, polygon, index):
+    rows = 8 + polygon.shape[0]
+    return pl.pallas_call(
+        gather_kernel,
+        out_shape=jax.ShapeDtypeStruct((index.shape[0], rows, index.shape[1]), jnp.float32),
+        scratch_shapes=[pltpu.VMEM((8, state.shape[1]), jnp.float32)],
+    )(state, radius, mass, polygon, index)
 
 
 def exchange(low, high, axis):
@@ -191,7 +254,11 @@
     from_above, from_below = exchange(surface[:, :margin], surface[:, -margin:], "gx")
     near = jnp.concatenate([from_above, surface, from_below], axis=1)
     first_row = lax.axis_index("gx") * rows_here - margin
-    sampled = jnp.take(near.reshape(4, -1), cells - first_row * cols_here, axis=1)
+    sampled = sample_surface(
+        near,
+        (cells // cols_here - first_row)[None],
+        (cells % cols_here)[None],
+    )
     lists = contact_list[0, 0]
     count = contact_count[0, 0]
     slots = lists.shape[1]
@@ -213,17 +280,12 @@
     new_velocity = velocity + ICE_STEP * total / mass[None]
     new_position = position + ICE_STEP * new_velocity
     floe_next = jnp.concatenate([new_position, new_velocity], axis=0)
-    rows_all = jnp.concatenate([floe_next, radius[None], mass[None], floe_polygon[0, 0]], axis=0)
-    width = rows_all.shape[0]
     leaving = move_index[0, 0]
     capacity = leaving.shape[1]
-    taken = (
-        jnp.take(rows_all, leaving.reshape(-1), axis=1)
-        .reshape(width, 8, capacity)
-        .transpose(1, 0, 2)
-    )
     valid_slots = jnp.arange(capacity, dtype=jnp.int32)[None, :] < move_count[0, 0][:, None]
-    outgoing = jnp.where(valid_slots[:, None, :], taken, 0.0)
+    outgoing = gather_records(
+        floe_next, radius[None], mass[None], floe_polygon[0, 0], jnp.where(valid_slots, leaving, -1)
+    )
     from_above, from_below = exchange(outgoing[0:3], outgoing[5:8], "gx")
     heading_left = jnp.stack([from_below[0], outgoing[3], from_above[0]])
     heading_right = jnp.stack([from_below[2], outgoing[4], from_above[2]])
@@ -240,6 +302,7 @@
             from_left[2],
         ]
     )
+    arrivals = jnp.concatenate([arrivals[:, 0:6], arrivals[:, 8:]], axis=1)
     return (flow, floe_next[None, None], arrivals[None, None])
 
 

time: 110 us -> 100 us (0.909)
  the two profiles are of different devices: /device:TPU:24 before, /device:TPU:144 now
where the time goes in v2:
time: 100 us; the launch traced here: 99.1 us
  starting transfers between devices  43.3 us (43%)
  other arithmetic  23.5 us (24%)
  waiting for transfers between devices  10.8 us (11%)
  local copies, waits for them, and re-layouts  10.1 us (10%)
  Pallas kernels  8.92 us (9%)
  between operations  2.2 us (2%)
    ppermute x5, starting transfers between devices, exchange(): from_next = lax.ppermute(low, axis, down)  31.5 us
    ppermute x5, starting transfers between devices, exchange(): from_previous = lax.ppermute(high, axis, up)  11.8 us
    ppermute x5, waiting for transfers between devices, exchange(): from_previous = lax.ppermute(high, axis, up)  8.43 us
    mul x4, other arithmetic, ocean_substep(): return (flow + horizontal * lap + vert + turning + surface) * wet[None]  5.52 us
    pallas_call x1, Pallas kernels, gather_records(): pl.pallas_call(gather_kernel, out_shape=jax.ShapeDtypeStruct((index.shape...  5.33 us
    reduce_sum x1, other arithmetic, pair_forces(): jnp.sum(magnitude * normal_x, axis=2)  5.12 us
    pallas_call x1, Pallas kernels, sample_surface(): pl.pallas_call(sample_kernel, out_shape=jax.ShapeDtypeStruct((window.shap...  3.59 us
    ppermute x5, waiting for transfers between devices, exchange(): from_next = lax.ppermute(low, axis, down)  2.33 us
  transfers between devices with their start and end apart: 10, of which 4 were waited for; matrix products, arithmetic and copies ran while one was open for 15% of the time, Pallas kernels for 0%

profile of v2, /device:TPU:144, one launch (start us, length us, event | category | flops | bytes accessed | tf_op | source)
XLA Modules:
  0.0 99.1 jit_solution(9229443542673920850)
XLA Ops:
  0.7 0.8 pad_maximum_fusion.17
  1.5 0.8 convert_bitcast_fusion
  2.3 0.9 pad_maximum_fusion.15
  3.3 2.9 %collective-permute-start = (f32[12288]{0:T(1024)S(1)}, f32[12288]{0:T(1024)S(1)}, u32[]{:S(2)}, u32[]{:S(2)}) collective-permute-start(f32[12288]{0:T(1024)S(1)} %get-tuple-element.116), channel_id=1, source_target_pairs={{0,8},{8,16},{16,24},{24,32},{32,40},{40,48},{48,56},{56,64},{64,7... | collective-permute-start | bytes 147464 | tf_op jit(solution)/shard_map/ppermute | solution.py:163
  6.2 4.1 %collective-permute-start.1 = (f32[12288]{0:T(1024)S(1)}, f32[12288]{0:T(1024)S(1)}, u32[]{:S(2)}, u32[]{:S(2)}) collective-permute-start(f32[12288]{0:T(1024)S(1)} %get-tuple-element.117), channel_id=1, source_target_pairs={{8,0},{16,8},{24,16},{32,24},{40,32},{48,40},{56,48},{64,56},{72,6... | collective-permute-start | bytes 147464 | tf_op jit(solution)/shard_map/ppermute | solution.py:164
  10.4 0.6 multiply_multiply_fusion
  11.0 0.6 and_select_fusion
  11.6 0.7 bitcast_select_fusion.index_ref
  12.2 0.6 fusion.65.rows_ref
  12.9 0.7 maximum_bitcast_fusion.2
  13.8 0.2 fusion.69
  14.1 0.1 copy-done.9
  14.3 0.4 reshape.331
  14.6 0.4 reshape.334
  15.1 1.9 %collective-permute-start.2 = (f32[13152]{0:T(1024)S(1)}, f32[13152]{0:T(1024)S(1)}, u32[]{:S(2)}, u32[]{:S(2)}) collective-permute-start(f32[13152]{0:T(1024)S(1)} %get-tuple-element.114), channel_id=1, source_target_pairs={{0,1},{1,2},{2,3},{3,4},{4,5},{5,6},{6,7},{7,128},{128,129},{129,1... | collective-permute-start | bytes 157832 | tf_op jit(solution)/shard_map/ppermute | solution.py:163
  17.0 7.3 %collective-permute-start.3 = (f32[13152]{0:T(1024)S(1)}, f32[13152]{0:T(1024)S(1)}, u32[]{:S(2)}, u32[]{:S(2)}) collective-permute-start(f32[13152]{0:T(1024)S(1)} %get-tuple-element.115), channel_id=1, source_target_pairs={{1,0},{2,1},{3,2},{4,3},{5,4},{6,5},{7,6},{128,7},{129,128},{130,1... | collective-permute-start | bytes 157832 | tf_op jit(solution)/shard_map/ppermute | solution.py:164
  24.9 0.6 copy.28
  25.5 0.5 collective-permute-done.3
  26.0 0.7 reshape.335
  26.8 0.7 reshape.333
  27.5 0.1 maximum_bitcast_fusion.1
  27.6 0.1 fusion.61
  27.8 0.7 pad_maximum_fusion
  28.7 0.1 broadcast_multiply_fusion
  28.8 0.1 slice_multiply_fusion.7
  28.9 0.2 fusion.59
  29.1 1.1 %fusion.52 = f32[2,8,72,136]{3,2,1,0:T(8,128)S(1)} fusion(f32[2,1,72,136]{3,2,1,0:T(8,128)S(1)} %fusion.61, f32[1,8,72,136]{3,2,1,0:T(8,128)S(1)} %get-tuple-element.87, f32[1,8,72,136]{3,2,1,0:T(8,128)S(1)} %get-tuple-element.86, f32[2,7,72,136]{3,2,1,0:T(8,128)S(1)} %fusion.59, f32[2,8,72,136]{3,2,1,0:T(8,128)S(1)} %broadcast_multiply_fusion, ...), kind=kLoop, calls=%fused_computation.94 | loop fusion | flops 2036736 | bytes 2820128 | tf_op jit(solution)/shard_map/mul | solution.py:55
  30.2 0.2 fusion.58
  30.3 0.1 slice_multiply_fusion.5
  30.4 1.1 %fusion.53 = f32[2,8,72,136]{3,2,1,0:T(8,128)S(1)} fusion(f32[2,1,72,136]{3,2,1,0:T(8,128)S(1)} %fusion.61, f32[1,8,72,136]{3,2,1,0:T(8,128)S(1)} %get-tuple-element.85, f32[1,8,72,136]{3,2,1,0:T(8,128)S(1)} %get-tuple-element.84, f32[2,7,72,136]{3,2,1,0:T(8,128)S(1)} %fusion.58, f32[2,8,72,136]{3,2,1,0:T(8,128)S(1)} %fusion.52, ...), kind=kLoop, calls=%fused_computation.95 | loop fusion | flops 2036736 | bytes 2820128 | tf_op jit(solution)/shard_map/mul | solution.py:55
  31.5 0.2 fusion.57
  31.7 0.1 slice_multiply_fusion.3
  31.8 1.1 %fusion.54 = f32[2,8,72,136]{3,2,1,0:T(8,128)S(1)} fusion(f32[2,1,72,136]{3,2,1,0:T(8,128)S(1)} %fusion.61, f32[1,8,72,136]{3,2,1,0:T(8,128)S(1)} %get-tuple-element.83, f32[1,8,72,136]{3,2,1,0:T(8,128)S(1)} %get-tuple-element.82, f32[2,7,72,136]{3,2,1,0:T(8,128)S(1)} %fusion.57, f32[2,8,72,136]{3,2,1,0:T(8,128)S(1)} %fusion.53, ...), kind=kLoop, calls=%fused_computation.96 | loop fusion | flops 2036736 | bytes 2820128 | tf_op jit(solution)/shard_map/mul | solution.py:55
  32.9 0.1 fusion.56
  33.1 1.2 %slice_multiply_fusion.1 = (f32[1,8,72,136]{3,2,1,0:T(8,128)}, f32[1,8,72,136]{3,2,1,0:T(8,128)}) fusion(f32[2,8,72,136]{3,2,1,0:T(8,128)S(1)} %fusion.54), kind=kLoop, calls=%fused_computation.108 | loop fusion | flops 156672 | bytes 1253376 | tf_op jit(solution)/shard_map/mul | solution.py:53
  34.4 0.1 fusion.76
  34.7 0.2 copy-done.21
  34.9 2.2 %fusion.55 = f32[2,8,72,136]{3,2,1,0:T(8,128)S(1)} fusion(f32[2,1,72,136]{3,2,1,0:T(8,128)S(1)} %fusion.61, f32[1,8,72,136]{3,2,1,0:T(8,128)} %get-tuple-element.81, f32[1,8,72,136]{3,2,1,0:T(8,128)} %get-tuple-element.80, f32[2,7,72,136]{3,2,1,0:T(8,128)S(1)} %fusion.56, f32[2,8,72,136]{3,2,1,0:T(8,128)S(1)} %fusion.54, f32[8]{0:T(128)S(1)} %copy-done.21, ...), kind=kLoop, calls=%fused_computation.97 | loop fusion | flops 2036736 | bytes 2820128 | tf_op jit(solution)/shard_map/mul | solution.py:55
  37.2 0.1 slice_bitcast_fusion.2
  37.3 1.9 %collective-permute-start.4 = (f32[4,32,128]{2,1,0:T(8,128)S(1)}, f32[4,32,128]{2,1,0:T(8,128)S(1)}, u32[]{:S(2)}, u32[]{:S(2)}) collective-permute-start(f32[4,32,128]{2,1,0:T(8,128)S(1)} %get-tuple-element.100), channel_id=1, source_target_pairs={{0,8},{8,16},{16,24},{24,32},{32,40},{40,48},{48,56},{56,64},{64,7... | collective-permute-start | bytes 196616 | tf_op jit(solution)/shard_map/ppermute | solution.py:163
  39.2 5.1 %collective-permute-start.5 = (f32[4,32,128]{2,1,0:T(8,128)S(1)}, f32[4,32,128]{2,1,0:T(8,128)S(1)}, u32[]{:S(2)}, u32[]{:S(2)}) collective-permute-start(f32[4,32,128]{2,1,0:T(8,128)S(1)} %get-tuple-element.101), channel_id=1, source_target_pairs={{8,0},{16,8},{24,16},{32,24},{40,32},{48,40},{56,48},{64,56},{72,6... | collective-permute-start | bytes 196616 | tf_op jit(solution)/shard_map/ppermute | solution.py:164
  44.5 7.6 %while.10 = (s32[]{:T(128)}, f32[16,2,128]{2,0,1:T(8,128)S(1)}, s32[]{:T(128)}, s32[3,64]{1,0:T(4,128)S(1)}, s32[]{:T(128)}, /*index=5*/f32[48,5,128]{2,1,0:T(8,...) while((s32[]{:T(128)}, f32[16,2,128]{2,0,1:T(8,128)S(1)}, s32[]{:T(128)}, s32[3,64]{1,0:T(4,128)S(1)}, ...), condition=%wide.region_3.4_spmd, body=%wide.region_0.3_spmd.sunk | while | flops 15219718 | bytes 928223 | solution.py:274
  44.5 0.7 add_compare_fusion.2
  45.3 0.6 gather_fusion
  45.9 0.6 gather_fusion.1
  46.6 5.1 %multiply_reduce_fusion.4 = (f32[32,128]{1,0:T(8,128)S(1)}, f32[32,128]{1,0:T(8,128)S(1)}) fusion(f32[32,128]{1,0:T(8,128)S(1)} %bitcast.140, f32[32,128]{1,0:T(8,128)S(1)} %bitcast.145, f32[32,128]{1,0:T(8,128)S(1)} %bitcast.141, f32[32,128]{1,0:T(8,128)S(1)} %bitcast.146, f32[32,128]{1,0:T(8,128)S(1)} %bitcast.142, f32[32,128]{1,0:T(8,128)S(1)} %bitcast.147, ...), kind=kLoop, calls=%fused_computation.15.clone.1 | loop fusion | flops 13623296 | bytes 196608 | tf_op jit(solution)/shard_map/while/body/reduce_sum | solution.py:72
  51.7 0.2 convolution_add_fusion.2
  52.1 0.7 pad_maximum_fusion.2.window_ref
  52.8 3.6 %shard_map.148 = f32[4,2048]{1,0:T(4,128)} custom-call(f32[4,128,128]{2,1,0:T(8,128)} %pad_maximum_fusion.2.window_ref, s32[1,2048]{1,0:T(1,128)} %fusion.65.rows_ref, s32[1,2048]{1,0:T(1,128)} %get-tuple-element.62.cols_ref), custom_call_target="tpu_custom_call" | custom-call | tf_op jit(solution)/shard_map/pallas_call | solution.py:126
  56.4 0.8 multiply_reduce_fusion.2
  57.2 0.9 multiply_add_fusion
  58.1 0.6 pad_maximum_fusion.16
  58.8 5.3 %shard_map.149 = f32[8,40,128]{2,1,0:T(8,128)} custom-call(f32[4,2048]{1,0:T(4,128)} %get-tuple-element.112.state_ref, f32[1,2048]{1,0:T(1,128)} %bitcast.157, f32[1,2048]{1,0:T(1,128)} %bitcast.161, f32[32,2048]{1,0:T(8,128)} %bitcast.152, s32[8,128]{1,0:T(8,128)} %bitcast_select_fusion.index_ref), custom_call_target="tpu_custom_call" | custom-call | tf_op jit(solution)/shard_map/pallas_call | solution.py:152
  64.1 0.9 fusion.71
  65.0 2.7 %collective-permute-start.6 = (f32[3,40,128]{2,1,0:T(8,128)S(1)}, f32[3,40,128]{2,1,0:T(8,128)S(1)}, u32[]{:S(2)}, u32[]{:S(2)}) collective-permute-start(f32[3,40,128]{2,1,0:T(8,128)S(1)} %get-tuple-element.94), channel_id=1, source_target_pairs={{8,0},{16,8},{24,16},{32,24},{40,32},{48,40},{56,48},{64,56},{72,6... | collective-permute-start | bytes 184328 | tf_op jit(solution)/shard_map/ppermute | solution.py:164
  67.7 3.1 %collective-permute-start.7 = (f32[3,40,128]{2,1,0:T(8,128)S(1)}, f32[3,40,128]{2,1,0:T(8,128)S(1)}, u32[]{:S(2)}, u32[]{:S(2)}) collective-permute-start(f32[3,40,128]{2,1,0:T(8,128)S(1)} %get-tuple-element.95), channel_id=1, source_target_pairs={{0,8},{8,16},{16,24},{24,32},{32,40},{40,48},{48,56},{56,64},{64,7... | collective-permute-start | bytes 184328 | tf_op jit(solution)/shard_map/ppermute | solution.py:163
  70.8 0.8 fusion.70
  71.6 3.4 %collective-permute-done.7 = f32[3,40,128]{2,1,0:T(8,128)S(1)} collective-permute-done((f32[3,40,128]{2,1,0:T(8,128)S(1)}, f32[3,40,128]{2,1,0:T(8,128)S(1)}, u32[]{:S(2)}, u32[]{:S(2)}) %collective-permute-start.7) | collective-permute-done | bytes 61472 | tf_op jit(solution)/shard_map/ppermute | solution.py:163
  75.0 12.2 %collective-permute-start.8 = (f32[3,40,128]{2,1,0:T(8,128)S(1)}, f32[3,40,128]{2,1,0:T(8,128)S(1)}, u32[]{:S(2)}, u32[]{:S(2)}) collective-permute-start(f32[3,40,128]{2,1,0:T(8,128)S(1)} %pad_maximum_fusion.8), channel_id=1, source_target_pairs={{1,0},{2,1},{3,2},{4,3},{5,4},{6,5},{7,6},{128,7},{129,128},{130,1... | collective-permute-start | bytes 184328 | tf_op jit(solution)/shard_map/ppermute | solution.py:164
  87.3 1.8 %collective-permute-done.8 = f32[3,40,128]{2,1,0:T(8,128)S(1)} collective-permute-done((f32[3,40,128]{2,1,0:T(8,128)S(1)}, f32[3,40,128]{2,1,0:T(8,128)S(1)}, u32[]{:S(2)}, u32[]{:S(2)}) %collective-permute-start.8) | collective-permute-done | bytes 61472 | tf_op jit(solution)/shard_map/ppermute | solution.py:164
  89.1 1.9 %collective-permute-start.9 = (f32[3,40,128]{2,1,0:T(8,128)S(1)}, f32[3,40,128]{2,1,0:T(8,128)S(1)}, u32[]{:S(2)}, u32[]{:S(2)}) collective-permute-start(f32[3,40,128]{2,1,0:T(8,128)S(1)} %pad_maximum_fusion.9), channel_id=1, source_target_pairs={{0,1},{1,2},{2,3},{3,4},{4,5},{5,6},{6,7},{7,128},{128,129},{129,1... | collective-permute-start | bytes 184328 | tf_op jit(solution)/shard_map/ppermute | solution.py:163
  91.1 2.3 %slice.485 = f32[2,8,64,128]{3,2,1,0:T(8,128)} slice(f32[2,8,72,136]{3,2,1,0:T(8,128)} %copy-done.2), slice={[0:2], [0:8], [4:68], [4:132]} | slice | bytes 1048576 | tf_op jit(solution)/shard_map/slice | solution.py:249
  93.3 5.0 %collective-permute-done.9 = f32[3,40,128]{2,1,0:T(8,128)S(1)} collective-permute-done((f32[3,40,128]{2,1,0:T(8,128)S(1)}, f32[3,40,128]{2,1,0:T(8,128)S(1)}, u32[]{:S(2)}, u32[]{:S(2)}) %collective-permute-start.9) | collective-permute-done | bytes 61472 | tf_op jit(solution)/shard_map/ppermute | solution.py:163
  98.4 0.7 copy.18
  (120 shorter events, 1.2 us)
Async XLA Ops:
  0.6 9.7 %copy-start.11 = (f32[1,1,2048]{2,1,0:T(1,128)S(1)}, f32[1,1,2048]{2,1,0:T(1,128)}, u32[]{:S(2)}) copy-start(f32[1,1,2048]{2,1,0:T(1,128)} %param.20) | copy-start | bytes 24580
  0.6 12.2 %copy-start.5 = (f32[1,1,2,2048]{3,2,1,0:T(2,128)S(1)}, f32[1,1,2,2048]{3,2,1,0:T(2,128)}, u32[]{:S(2)}) copy-start(f32[1,1,2,2048]{3,2,1,0:T(2,128)} %param.18) | copy-start | bytes 49156
  0.7 12.2 %copy-start.3 = (f32[1,1,2,2048]{3,2,1,0:T(2,128)S(1)}, f32[1,1,2,2048]{3,2,1,0:T(2,128)}, u32[]{:S(2)}) copy-start(f32[1,1,2,2048]{3,2,1,0:T(2,128)} %param.19) | copy-start | bytes 49156
  0.7 13.0 %copy-start.1 = (f32[2,64,128]{2,1,0:T(8,128)S(1)}, f32[2,64,128]{2,1,0:T(8,128)}, u32[]{:S(2)}) copy-start(f32[2,64,128]{2,1,0:T(8,128)} %param.16) | copy-start | bytes 196612
  0.7 13.0 %copy-start = (f32[2,8,64,128]{3,2,1,0:T(8,128)S(1)}, f32[2,8,64,128]{3,2,1,0:T(8,128)}, u32[]{:S(2)}) copy-start(f32[2,8,64,128]{3,2,1,0:T(8,128)} %param.15) | copy-start | bytes 1572868
  0.7 10.3 %copy-start.17 = (s32[1,1,2048]{2,1,0:T(1,128)S(1)}, s32[1,1,2048]{2,1,0:T(1,128)}, u32[]{:S(2)}) copy-start(s32[1,1,2048]{2,1,0:T(1,128)} %param.23) | copy-start | bytes 24580
  0.7 10.9 %copy-start.24 = (s32[1,1,8]{2,1,0:T(1,128)S(1)}, s32[1,1,8]{2,1,0:T(1,128)}, u32[]{:S(2)}) copy-start(s32[1,1,8]{2,1,0:T(1,128)} %param.27) | copy-start | bytes 100
  0.7 10.9 %copy-start.22 = (s32[1,1,8,128]{3,2,1,0:T(8,128)S(1)}, s32[1,1,8,128]{3,2,1,0:T(8,128)}, u32[]{:S(2)}) copy-start(s32[1,1,8,128]{3,2,1,0:T(8,128)} %param.26) | copy-start | bytes 12292
  3.3 10.3 %collective-permute-start = (f32[12288]{0:T(1024)S(1)}, f32[12288]{0:T(1024)S(1)}, u32[]{:S(2)}, u32[]{:S(2)}) collective-permute-start(f32[12288]{0:T(1024)S(1)} %get-tuple-element.116), channel_id=1, source_target_pairs={{0,8},{8,16},{16,24},{24,32},{32,40},{40,48},{48,56},{56,64},{64,7... | collective-permute-start | bytes 147464 | tf_op jit(solution)/shard_map/ppermute | solution.py:163
  6.2 7.4 %collective-permute-start.1 = (f32[12288]{0:T(1024)S(1)}, f32[12288]{0:T(1024)S(1)}, u32[]{:S(2)}, u32[]{:S(2)}) collective-permute-start(f32[12288]{0:T(1024)S(1)} %get-tuple-element.117), channel_id=1, source_target_pairs={{8,0},{16,8},{24,16},{32,24},{40,32},{48,40},{56,48},{64,56},{72,6... | collective-permute-start | bytes 147464 | tf_op jit(solution)/shard_map/ppermute | solution.py:164
  13.6 0.6 copy-start.9
  13.7 0.6 copy-start.7
  14.3 10.7 %copy-start.23 = (s32[1,1,3,64]{3,1,2,0:T(1,128)S(1)}, s32[1,1,3,64]{3,1,2,0:T(1,128)}, u32[]{:S(2)}) copy-start(s32[1,1,3,64]{3,1,2,0:T(1,128)} %param.25) | copy-start | bytes 2308
  15.1 11.7 %collective-permute-start.2 = (f32[13152]{0:T(1024)S(1)}, f32[13152]{0:T(1024)S(1)}, u32[]{:S(2)}, u32[]{:S(2)}) collective-permute-start(f32[13152]{0:T(1024)S(1)} %get-tuple-element.114), channel_id=1, source_target_pairs={{0,1},{1,2},{2,3},{3,4},{4,5},{5,6},{6,7},{7,128},{128,129},{129,1... | collective-permute-start | bytes 157832 | tf_op jit(solution)/shard_map/ppermute | solution.py:163
  17.0 9.0 %collective-permute-start.3 = (f32[13152]{0:T(1024)S(1)}, f32[13152]{0:T(1024)S(1)}, u32[]{:S(2)}, u32[]{:S(2)}) collective-permute-start(f32[13152]{0:T(1024)S(1)} %get-tuple-element.115), channel_id=1, source_target_pairs={{1,0},{2,1},{3,2},{4,3},{5,4},{6,5},{7,6},{128,7},{129,128},{130,1... | collective-permute-start | bytes 157832 | tf_op jit(solution)/shard_map/ppermute | solution.py:164
  24.3 7.6 %copy-start.20 = (f32[8]{0:T(128)}, f32[8]{0:T(128)S(1)}, u32[]{:S(2)}) copy-start(f32[8]{0:T(128)S(1)} %multiply_subtract_fusion) | copy-start | bytes 100
  26.0 1.6 %copy-start.13 = (f32[13152]{0:T(1024)}, f32[13152]{0:T(1024)S(1)}, u32[]{:S(2)}) copy-start(f32[13152]{0:T(1024)S(1)} %collective-permute-done.3) | copy-start | bytes 157828
  26.8 0.7 copy-start.15
  33.0 1.2 %copy-start.16 = (f32[13152]{0:T(1024)S(1)}, f32[13152]{0:T(1024)}, u32[]{:S(2)}) copy-start(f32[13152]{0:T(1024)} %copy-done.15) | copy-start | bytes 157828
  33.1 1.3 %copy-start.14 = (f32[13152]{0:T(1024)S(1)}, f32[13152]{0:T(1024)}, u32[]{:S(2)}) copy-start(f32[13152]{0:T(1024)} %copy-done.13) | copy-start | bytes 157828
  33.1 1.4 %copy-start.10 = (f32[1,5,512]{2,1,0:T(8,128)S(1)}, f32[1,5,512]{2,1,0:T(8,128)}, u32[]{:S(2)}) copy-start(f32[1,5,512]{2,1,0:T(8,128)} %copy-done.9) | copy-start | bytes 30724
  33.1 1.5 %copy-start.8 = (f32[1,5,512]{2,1,0:T(8,128)S(1)}, f32[1,5,512]{2,1,0:T(8,128)}, u32[]{:S(2)}) copy-start(f32[1,5,512]{2,1,0:T(8,128)} %copy-done.7) | copy-start | bytes 30724
  34.2 0.7 copy-start.21
  34.9 9.5 %copy-start.4 = (f32[16,5,128]{2,1,0:T(8,128)S(1)}, f32[16,5,128]{2,1,0:T(8,128)}, u32[]{:S(2)}) copy-start(f32[16,5,128]{2,1,0:T(8,128)} %maximum_bitcast_fusion.2) | copy-start | bytes 122884
  34.9 9.5 %copy-start.12 = (s32[1,1,3,64]{3,2,1,0:T(4,128)S(1)}, s32[1,1,3,64]{3,2,1,0:T(4,128)}, u32[]{:S(2)}) copy-start(s32[1,1,3,64]{3,2,1,0:T(4,128)} %copy.28) | copy-start | bytes 2308
  37.2 2.1 %copy-start.2 = (f32[2,8,72,136]{3,2,1,0:T(8,128)}, f32[2,8,72,136]{3,2,1,0:T(8,128)S(1)}, u32[]{:S(2)}) copy-start(f32[2,8,72,136]{3,2,1,0:T(8,128)S(1)} %fusion.55) | copy-start | bytes 1880068
  37.3 14.8 %collective-permute-start.4 = (f32[4,32,128]{2,1,0:T(8,128)S(1)}, f32[4,32,128]{2,1,0:T(8,128)S(1)}, u32[]{:S(2)}, u32[]{:S(2)}) collective-permute-start(f32[4,32,128]{2,1,0:T(8,128)S(1)} %get-tuple-element.100), channel_id=1, source_target_pairs={{0,8},{8,16},{16,24},{24,32},{32,40},{40,48},{48,56},{56,64},{64,7... | collective-permute-start | bytes 196616 | tf_op jit(solution)/shard_map/ppermute | solution.py:163
  39.2 12.8 %collective-permute-start.5 = (f32[4,32,128]{2,1,0:T(8,128)S(1)}, f32[4,32,128]{2,1,0:T(8,128)S(1)}, u32[]{:S(2)}, u32[]{:S(2)}) collective-permute-start(f32[4,32,128]{2,1,0:T(8,128)S(1)} %get-tuple-element.101), channel_id=1, source_target_pairs={{8,0},{16,8},{24,16},{32,24},{40,32},{48,40},{56,48},{64,56},{72,6... | collective-permute-start | bytes 196616 | tf_op jit(solution)/shard_map/ppermute | solution.py:164
  44.4 12.8 %copy-start.6 = (f32[1,1,2,2048]{3,2,1,0:T(2,128)S(1)}, f32[1,1,2,2048]{3,2,1,0:T(2,128)}, u32[]{:S(2)}) copy-start(f32[1,1,2,2048]{3,2,1,0:T(2,128)} %param.18) | copy-start | bytes 49156
  44.5 12.8 %copy-start.18 = (f32[2048]{0:T(1024)S(1)}, f32[2048]{0:T(1024)}, u32[]{:S(2)}) copy-start(f32[2048]{0:T(1024)} %multiply_multiply_fusion) | copy-start | bytes 24580
  44.5 12.8 %copy-start.19 = (f32[1,1,2048]{2,1,0:T(1,128)S(1)}, f32[1,1,2048]{2,1,0:T(1,128)}, u32[]{:S(2)}) copy-start(f32[1,1,2048]{2,1,0:T(1,128)} %param.21) | copy-start | bytes 24580
  65.0 6.6 %collective-permute-start.6 = (f32[3,40,128]{2,1,0:T(8,128)S(1)}, f32[3,40,128]{2,1,0:T(8,128)S(1)}, u32[]{:S(2)}, u32[]{:S(2)}) collective-permute-start(f32[3,40,128]{2,1,0:T(8,128)S(1)} %get-tuple-element.94), channel_id=1, source_target_pairs={{8,0},{16,8},{24,16},{32,24},{40,32},{48,40},{56,48},{64,56},{72,6... | collective-permute-start | bytes 184328 | tf_op jit(solution)/shard_map/ppermute | solution.py:164
  67.7 7.3 %collective-permute-start.7 = (f32[3,40,128]{2,1,0:T(8,128)S(1)}, f32[3,40,128]{2,1,0:T(8,128)S(1)}, u32[]{:S(2)}, u32[]{:S(2)}) collective-permute-start(f32[3,40,128]{2,1,0:T(8,128)S(1)} %get-tuple-element.95), channel_id=1, source_target_pairs={{0,8},{8,16},{16,24},{24,32},{32,40},{40,48},{48,56},{56,64},{64,7... | collective-permute-start | bytes 184328 | tf_op jit(solution)/shard_map/ppermute | solution.py:163
  75.0 14.1 %collective-permute-start.8 = (f32[3,40,128]{2,1,0:T(8,128)S(1)}, f32[3,40,128]{2,1,0:T(8,128)S(1)}, u32[]{:S(2)}, u32[]{:S(2)}) collective-permute-start(f32[3,40,128]{2,1,0:T(8,128)S(1)} %pad_maximum_fusion.8), channel_id=1, source_target_pairs={{1,0},{2,1},{3,2},{4,3},{5,4},{6,5},{7,6},{128,7},{129,128},{130,1... | collective-permute-start | bytes 184328 | tf_op jit(solution)/shard_map/ppermute | solution.py:164
  89.1 9.2 %collective-permute-start.9 = (f32[3,40,128]{2,1,0:T(8,128)S(1)}, f32[3,40,128]{2,1,0:T(8,128)S(1)}, u32[]{:S(2)}, u32[]{:S(2)}) collective-permute-start(f32[3,40,128]{2,1,0:T(8,128)S(1)} %pad_maximum_fusion.9), channel_id=1, source_target_pairs={{0,1},{1,2},{2,3},{3,4},{4,5},{5,6},{6,7},{7,128},{128,129},{129,1... | collective-permute-start | bytes 184328 | tf_op jit(solution)/shard_map/ppermute | solution.py:163

commit v3 on v2

--- a/solution.py
+++ b/solution.py
@@ -56,20 +56,21 @@
 
 
 def pair_forces(first, second):
-    delta_x = first[:, 0, :, None] - second[:, 0, None, :]
-    delta_y = first[:, 1, :, None] - second[:, 1, None, :]
-    distance = jnp.sqrt(delta_x * delta_x + delta_y * delta_y + SOFTEN * SOFTEN)
-    reach = first[:, 4, :, None] + second[:, 4, None, :]
+    own = first[:, :, None, :]
+    other = second[:, :, :, None]
+    delta_x = own[:, 0] - other[:, 0]
+    delta_y = own[:, 1] - other[:, 1]
+    inverse = lax.rsqrt(delta_x * delta_x + delta_y * delta_y + SOFTEN * SOFTEN)
+    distance = (delta_x * delta_x + delta_y * delta_y + SOFTEN * SOFTEN) * inverse
+    reach = own[:, 4] + other[:, 4]
     intersection = jnp.maximum(reach - distance, 0.0)
-    reduced = first[:, 4, :, None] * second[:, 4, None, :] / reach
-    normal_x = delta_x / distance
-    normal_y = delta_y / distance
-    closing = (first[:, 2, :, None] - second[:, 2, None, :]) * normal_x + (
-        first[:, 3, :, None] - second[:, 3, None, :]
-    ) * normal_y
+    reduced = own[:, 4] * other[:, 4] / reach
+    normal_x = delta_x * inverse
+    normal_y = delta_y * inverse
+    closing = (own[:, 2] - other[:, 2]) * normal_x + (own[:, 3] - other[:, 3]) * normal_y
     magnitude = intersection * reduced * (STIFFNESS - DAMPING * closing)
     return jnp.stack(
-        [jnp.sum(magnitude * normal_x, axis=2), jnp.sum(magnitude * normal_y, axis=2)], axis=1
+        [jnp.sum(magnitude * normal_x, axis=1), jnp.sum(magnitude * normal_y, axis=1)], axis=1
     )
 
 
@@ -261,17 +262,8 @@
     )
     lists = contact_list[0, 0]
     count = contact_count[0, 0]
-    slots = lists.shape[1]
-    batch = math.gcd(slots, 32)
-    rounds = (count + batch - 1) // batch
-
-    def accumulate(turn, total):
-        start = turn * batch
-        group = lax.dynamic_slice_in_dim(lists, start, batch, 1)
-        valid = start + jnp.arange(batch, dtype=jnp.int32) < count
-        return total + contact_batch(table, group, valid, blocks, GHOST)
-
-    contact = lax.fori_loop(0, rounds, accumulate, jnp.zeros((blocks, 2, 128), jnp.float32))
+    valid = jnp.arange(lists.shape[1], dtype=jnp.int32) < count
+    contact = contact_batch(table, lists, valid, blocks, GHOST)
     contact = contact.transpose(1, 0, 2).reshape(2, floes)
     area = math.pi * radius * radius
     relative = sampled[0:2] - velocity

time: 100 us -> 102 us (1.020)
  the two profiles are of different devices: /device:TPU:144 before, /device:TPU:24 now
where the time goes in v3:
time: 102 us; the launch traced here: 101 us
  starting transfers between devices  40.7 us (40%)
  other arithmetic  26 us (25%)
  waiting for transfers between devices  11.6 us (11%)
  local copies, waits for them, and re-layouts  11.2 us (11%)
  Pallas kernels  8.93 us (9%)
  between operations  2.27 us (2%)
    ppermute x5, starting transfers between devices, exchange(): from_next = lax.ppermute(low, axis, down)  27.2 us
    ppermute x5, starting transfers between devices, exchange(): from_previous = lax.ppermute(high, axis, up)  13.5 us
    ppermute x5, waiting for transfers between devices, exchange(): from_previous = lax.ppermute(high, axis, up)  8.55 us
    reduce_sum x1, other arithmetic, pair_forces(): jnp.sum(magnitude * normal_x, axis=1)  7.06 us
    mul x4, other arithmetic, ocean_substep(): return (flow + horizontal * lap + vert + turning + surface) * wet[None]  5.52 us
    pallas_call x1, Pallas kernels, gather_records(): pl.pallas_call(gather_kernel, out_shape=jax.ShapeDtypeStruct((index.shape...  5.33 us
    pallas_call x1, Pallas kernels, sample_surface(): pl.pallas_call(sample_kernel, out_shape=jax.ShapeDtypeStruct((window.shap...  3.6 us
    ppermute x5, waiting for transfers between devices, exchange(): from_next = lax.ppermute(low, axis, down)  3.04 us
  transfers between devices with their start and end apart: 10, of which 4 were waited for; matrix products, arithmetic and copies ran while one was open for 16% of the time, Pallas kernels for 0%

profile of v3, /device:TPU:24, one launch (start us, length us, event | category | flops | bytes accessed | tf_op | source)
XLA Modules:
  0.0 100.9 jit_solution(14908904584997352727)
XLA Ops:
  0.7 0.8 pad_maximum_fusion.17
  1.5 0.8 convert_bitcast_fusion
  2.3 0.9 pad_maximum_fusion.15
  3.3 3.8 %collective-permute-start = (f32[12288]{0:T(1024)S(1)}, f32[12288]{0:T(1024)S(1)}, u32[]{:S(2)}, u32[]{:S(2)}) collective-permute-start(f32[12288]{0:T(1024)S(1)} %get-tuple-element.66), channel_id=1, source_target_pairs={{0,8},{8,16},{16,24},{24,32},{32,40},{40,48},{48,56},{56,64},{64,7... | collective-permute-start | bytes 147464 | tf_op jit(solution)/shard_map/ppermute | solution.py:164
  7.1 6.0 %collective-permute-start.1 = (f32[12288]{0:T(1024)S(1)}, f32[12288]{0:T(1024)S(1)}, u32[]{:S(2)}, u32[]{:S(2)}) collective-permute-start(f32[12288]{0:T(1024)S(1)} %get-tuple-element.67), channel_id=1, source_target_pairs={{8,0},{16,8},{24,16},{32,24},{40,32},{48,40},{56,48},{64,56},{72,6... | collective-permute-start | bytes 147464 | tf_op jit(solution)/shard_map/ppermute | solution.py:165
  13.2 0.6 slice_bitcast_fusion.2
  13.8 0.6 multiply_multiply_fusion
  14.4 0.6 and_select_fusion
  15.0 0.6 bitcast_select_fusion.index_ref
  15.6 0.6 pad_clamp_fusion
  16.2 0.6 fusion.56.rows_ref
  16.9 0.7 maximum_bitcast_fusion.2
  18.5 0.2 fusion.66
  18.7 0.1 copy-done.9
  18.9 0.4 reshape.342
  19.3 0.4 reshape.345
  19.7 1.9 %collective-permute-start.2 = (f32[13152]{0:T(1024)S(1)}, f32[13152]{0:T(1024)S(1)}, u32[]{:S(2)}, u32[]{:S(2)}) collective-permute-start(f32[13152]{0:T(1024)S(1)} %get-tuple-element.64), channel_id=1, source_target_pairs={{0,1},{1,2},{2,3},{3,4},{4,5},{5,6},{6,7},{7,128},{128,129},{129,1... | collective-permute-start | bytes 157832 | tf_op jit(solution)/shard_map/ppermute | solution.py:164
  21.7 7.3 %collective-permute-start.3 = (f32[13152]{0:T(1024)S(1)}, f32[13152]{0:T(1024)S(1)}, u32[]{:S(2)}, u32[]{:S(2)}) collective-permute-start(f32[13152]{0:T(1024)S(1)} %get-tuple-element.65), channel_id=1, source_target_pairs={{1,0},{2,1},{3,2},{4,3},{5,4},{6,5},{7,6},{128,7},{129,128},{130,1... | collective-permute-start | bytes 157832 | tf_op jit(solution)/shard_map/ppermute | solution.py:165
  28.9 0.6 iota_compare_fusion.3
  29.5 1.2 %collective-permute-done.3 = f32[13152]{0:T(1024)S(1)} collective-permute-done((f32[13152]{0:T(1024)S(1)}, f32[13152]{0:T(1024)S(1)}, u32[]{:S(2)}, u32[]{:S(2)}) %collective-permute-start.3) | collective-permute-done | bytes 52640 | tf_op jit(solution)/shard_map/ppermute | solution.py:165
  30.7 0.7 reshape.346
  31.5 0.7 reshape.344
  32.2 0.1 maximum_bitcast_fusion.1
  32.3 0.1 fusion.46
  32.4 0.7 pad_maximum_fusion
  33.4 0.1 broadcast_multiply_fusion
  33.5 0.1 slice_multiply_fusion.7
  33.6 0.2 fusion.44
  33.7 1.1 %fusion.37 = f32[2,8,72,136]{3,2,1,0:T(8,128)S(1)} fusion(f32[2,1,72,136]{3,2,1,0:T(8,128)S(1)} %fusion.46, f32[1,8,72,136]{3,2,1,0:T(8,128)S(1)} %get-tuple-element.27, f32[1,8,72,136]{3,2,1,0:T(8,128)S(1)} %get-tuple-element.26, f32[2,7,72,136]{3,2,1,0:T(8,128)S(1)} %fusion.44, f32[2,8,72,136]{3,2,1,0:T(8,128)S(1)} %broadcast_multiply_fusion, ...), kind=kLoop, calls=%fused_computation.69 | loop fusion | flops 2036736 | bytes 2820128 | tf_op jit(solution)/shard_map/mul | solution.py:55
  34.8 0.2 fusion.43
  35.0 0.1 slice_multiply_fusion.5
  35.1 1.1 %fusion.38 = f32[2,8,72,136]{3,2,1,0:T(8,128)S(1)} fusion(f32[2,1,72,136]{3,2,1,0:T(8,128)S(1)} %fusion.46, f32[1,8,72,136]{3,2,1,0:T(8,128)S(1)} %get-tuple-element.25, f32[1,8,72,136]{3,2,1,0:T(8,128)S(1)} %get-tuple-element.24, f32[2,7,72,136]{3,2,1,0:T(8,128)S(1)} %fusion.43, f32[2,8,72,136]{3,2,1,0:T(8,128)S(1)} %fusion.37, ...), kind=kLoop, calls=%fused_computation.70 | loop fusion | flops 2036736 | bytes 2820128 | tf_op jit(solution)/shard_map/mul | solution.py:55
  36.2 0.2 fusion.42
  36.4 0.1 slice_multiply_fusion.3
  36.5 1.1 %fusion.39 = f32[2,8,72,136]{3,2,1,0:T(8,128)S(1)} fusion(f32[2,1,72,136]{3,2,1,0:T(8,128)S(1)} %fusion.46, f32[1,8,72,136]{3,2,1,0:T(8,128)S(1)} %get-tuple-element.23, f32[1,8,72,136]{3,2,1,0:T(8,128)S(1)} %get-tuple-element.22, f32[2,7,72,136]{3,2,1,0:T(8,128)S(1)} %fusion.42, f32[2,8,72,136]{3,2,1,0:T(8,128)S(1)} %fusion.38, ...), kind=kLoop, calls=%fused_computation.71 | loop fusion | flops 2036736 | bytes 2820128 | tf_op jit(solution)/shard_map/mul | solution.py:55
  37.6 0.1 fusion.41
  37.8 1.2 %slice_multiply_fusion.1 = (f32[1,8,72,136]{3,2,1,0:T(8,128)}, f32[1,8,72,136]{3,2,1,0:T(8,128)}) fusion(f32[2,8,72,136]{3,2,1,0:T(8,128)S(1)} %fusion.39), kind=kLoop, calls=%fused_computation.84 | loop fusion | flops 156672 | bytes 1253376 | tf_op jit(solution)/shard_map/mul | solution.py:53
  39.4 0.4 copy-done.4
  39.8 0.8 gather_fusion.1
  40.6 0.7 fusion.68
  41.3 0.8 gather_fusion
  42.1 0.1 fusion.67
  42.2 2.2 %fusion.40 = f32[2,8,72,136]{3,2,1,0:T(8,128)S(1)} fusion(f32[2,1,72,136]{3,2,1,0:T(8,128)S(1)} %fusion.46, f32[1,8,72,136]{3,2,1,0:T(8,128)} %get-tuple-element.21, f32[1,8,72,136]{3,2,1,0:T(8,128)} %get-tuple-element.20, f32[2,7,72,136]{3,2,1,0:T(8,128)S(1)} %fusion.41, f32[2,8,72,136]{3,2,1,0:T(8,128)S(1)} %fusion.39, f32[8]{0:T(128)} %copy-done.22, ...), kind=kLoop, calls=%fused_computation.72 | loop fusion | flops 2036736 | bytes 2820128 | tf_op jit(solution)/shard_map/mul | solution.py:55
  44.6 1.9 %collective-permute-start.4 = (f32[4,32,128]{2,1,0:T(8,128)S(1)}, f32[4,32,128]{2,1,0:T(8,128)S(1)}, u32[]{:S(2)}, u32[]{:S(2)}) collective-permute-start(f32[4,32,128]{2,1,0:T(8,128)S(1)} %get-tuple-element.50), channel_id=1, source_target_pairs={{0,8},{8,16},{16,24},{24,32},{32,40},{40,48},{48,56},{56,64},{64,7... | collective-permute-start | bytes 196616 | tf_op jit(solution)/shard_map/ppermute | solution.py:164
  46.6 6.2 %collective-permute-start.5 = (f32[4,32,128]{2,1,0:T(8,128)S(1)}, f32[4,32,128]{2,1,0:T(8,128)S(1)}, u32[]{:S(2)}, u32[]{:S(2)}) collective-permute-start(f32[4,32,128]{2,1,0:T(8,128)S(1)} %get-tuple-element.51), channel_id=1, source_target_pairs={{8,0},{16,8},{24,16},{32,24},{40,32},{48,40},{56,48},{64,56},{72,6... | collective-permute-start | bytes 196616 | tf_op jit(solution)/shard_map/ppermute | solution.py:165
  52.9 7.1 %multiply_reduce_fusion.1 = (f32[64,128]{1,0:T(8,128)S(1)}, f32[64,128]{1,0:T(8,128)S(1)}) fusion(f32[64,128]{1,0:T(8,128)S(1)} %bitcast.120, f32[64,128]{1,0:T(8,128)S(1)} %bitcast.125, f32[64,128]{1,0:T(8,128)S(1)} %bitcast.121, f32[64,128]{1,0:T(8,128)S(1)} %bitcast.126, f32[64,128]{1,0:T(8,128)S(1)} %bitcast.118, f32[64,128]{1,0:T(8,128)S(1)} %bitcast.123, ...), kind=kLoop, calls=%fused_computation.15 | loop fusion | flops 28295168 | bytes 393216 | tf_op jit(solution)/shard_map/reduce_sum | solution.py:73
  60.0 0.2 convolution_bitcast_fusion
  60.2 0.7 pad_maximum_fusion.2.window_ref
  60.9 3.6 %shard_map.148 = f32[4,2048]{1,0:T(4,128)} custom-call(f32[4,128,128]{2,1,0:T(8,128)} %pad_maximum_fusion.2.window_ref, s32[1,2048]{1,0:T(1,128)} %fusion.56.rows_ref, s32[1,2048]{1,0:T(1,128)} %get-tuple-element.16.cols_ref), custom_call_target="tpu_custom_call" | custom-call | tf_op jit(solution)/shard_map/pallas_call | solution.py:127
  64.5 0.8 multiply_reduce_fusion.2
  65.4 0.9 multiply_add_fusion
  66.2 0.6 pad_maximum_fusion.16
  66.9 5.3 %shard_map.149 = f32[8,40,128]{2,1,0:T(8,128)} custom-call(f32[4,2048]{1,0:T(4,128)} %get-tuple-element.62.state_ref, f32[1,2048]{1,0:T(1,128)} %bitcast.114, f32[1,2048]{1,0:T(1,128)} %bitcast.127, f32[32,2048]{1,0:T(8,128)} %bitcast.109, s32[8,128]{1,0:T(8,128)} %bitcast_select_fusion.index_ref), custom_call_target="tpu_custom_call" | custom-call | tf_op jit(solution)/shard_map/pallas_call | solution.py:153
  72.2 0.9 fusion.70
  73.1 1.9 %collective-permute-start.6 = (f32[3,40,128]{2,1,0:T(8,128)S(1)}, f32[3,40,128]{2,1,0:T(8,128)S(1)}, u32[]{:S(2)}, u32[]{:S(2)}) collective-permute-start(f32[3,40,128]{2,1,0:T(8,128)S(1)} %get-tuple-element.44), channel_id=1, source_target_pairs={{8,0},{16,8},{24,16},{32,24},{40,32},{48,40},{56,48},{64,56},{72,6... | collective-permute-start | bytes 184328 | tf_op jit(solution)/shard_map/ppermute | solution.py:165
  75.0 3.9 %collective-permute-start.7 = (f32[3,40,128]{2,1,0:T(8,128)S(1)}, f32[3,40,128]{2,1,0:T(8,128)S(1)}, u32[]{:S(2)}, u32[]{:S(2)}) collective-permute-start(f32[3,40,128]{2,1,0:T(8,128)S(1)} %get-tuple-element.45), channel_id=1, source_target_pairs={{0,8},{8,16},{16,24},{24,32},{32,40},{40,48},{48,56},{56,64},{64,7... | collective-permute-start | bytes 184328 | tf_op jit(solution)/shard_map/ppermute | solution.py:164
  78.9 0.8 fusion.69
  79.7 3.5 %collective-permute-done.7 = f32[3,40,128]{2,1,0:T(8,128)S(1)} collective-permute-done((f32[3,40,128]{2,1,0:T(8,128)S(1)}, f32[3,40,128]{2,1,0:T(8,128)S(1)}, u32[]{:S(2)}, u32[]{:S(2)}) %collective-permute-start.7) | collective-permute-done | bytes 61472 | tf_op jit(solution)/shard_map/ppermute | solution.py:164
  83.2 5.8 %collective-permute-start.8 = (f32[3,40,128]{2,1,0:T(8,128)S(1)}, f32[3,40,128]{2,1,0:T(8,128)S(1)}, u32[]{:S(2)}, u32[]{:S(2)}) collective-permute-start(f32[3,40,128]{2,1,0:T(8,128)S(1)} %pad_maximum_fusion.8), channel_id=1, source_target_pairs={{1,0},{2,1},{3,2},{4,3},{5,4},{6,5},{7,6},{128,7},{129,128},{130,1... | collective-permute-start | bytes 184328 | tf_op jit(solution)/shard_map/ppermute | solution.py:165
  89.0 1.8 %collective-permute-done.8 = f32[3,40,128]{2,1,0:T(8,128)S(1)} collective-permute-done((f32[3,40,128]{2,1,0:T(8,128)S(1)}, f32[3,40,128]{2,1,0:T(8,128)S(1)}, u32[]{:S(2)}, u32[]{:S(2)}) %collective-permute-start.8) | collective-permute-done | bytes 61472 | tf_op jit(solution)/shard_map/ppermute | solution.py:165
  90.9 1.9 %collective-permute-start.9 = (f32[3,40,128]{2,1,0:T(8,128)S(1)}, f32[3,40,128]{2,1,0:T(8,128)S(1)}, u32[]{:S(2)}, u32[]{:S(2)}) collective-permute-start(f32[3,40,128]{2,1,0:T(8,128)S(1)} %pad_maximum_fusion.9), channel_id=1, source_target_pairs={{0,1},{1,2},{2,3},{3,4},{4,5},{5,6},{6,7},{7,128},{128,129},{129,1... | collective-permute-start | bytes 184328 | tf_op jit(solution)/shard_map/ppermute | solution.py:164
  92.8 2.3 %slice.491 = f32[2,8,64,128]{3,2,1,0:T(8,128)} slice(f32[2,8,72,136]{3,2,1,0:T(8,128)} %copy-done.2), slice={[0:2], [0:8], [4:68], [4:132]} | slice | bytes 1048576 | tf_op jit(solution)/shard_map/slice | solution.py:250
  95.1 5.0 %collective-permute-done.9 = f32[3,40,128]{2,1,0:T(8,128)S(1)} collective-permute-done((f32[3,40,128]{2,1,0:T(8,128)S(1)}, f32[3,40,128]{2,1,0:T(8,128)S(1)}, u32[]{:S(2)}, u32[]{:S(2)}) %collective-permute-start.9) | collective-permute-done | bytes 61472 | tf_op jit(solution)/shard_map/ppermute | solution.py:164
  100.2 0.7 copy.21
  (122 shorter events, 1.2 us)
Async XLA Ops:
  0.6 13.1 %copy-start.11 = (f32[1,1,2048]{2,1,0:T(1,128)S(1)}, f32[1,1,2048]{2,1,0:T(1,128)}, u32[]{:S(2)}) copy-start(f32[1,1,2048]{2,1,0:T(1,128)} %param.18) | copy-start | bytes 24580
  0.6 16.2 %copy-start.5 = (f32[1,1,2,2048]{3,2,1,0:T(2,128)S(1)}, f32[1,1,2,2048]{3,2,1,0:T(2,128)}, u32[]{:S(2)}) copy-start(f32[1,1,2,2048]{3,2,1,0:T(2,128)} %param.16) | copy-start | bytes 49156
  0.7 16.2 %copy-start.3 = (f32[1,1,2,2048]{3,2,1,0:T(2,128)S(1)}, f32[1,1,2,2048]{3,2,1,0:T(2,128)}, u32[]{:S(2)}) copy-start(f32[1,1,2,2048]{3,2,1,0:T(2,128)} %param.17) | copy-start | bytes 49156
  0.7 17.7 %copy-start.1 = (f32[2,64,128]{2,1,0:T(8,128)S(1)}, f32[2,64,128]{2,1,0:T(8,128)}, u32[]{:S(2)}) copy-start(f32[2,64,128]{2,1,0:T(8,128)} %param.14) | copy-start | bytes 196612
  0.7 17.7 %copy-start = (f32[2,8,64,128]{3,2,1,0:T(8,128)S(1)}, f32[2,8,64,128]{3,2,1,0:T(8,128)}, u32[]{:S(2)}) copy-start(f32[2,8,64,128]{3,2,1,0:T(8,128)} %param.13) | copy-start | bytes 1572868
  0.7 12.5 %copy-start.24 = (s32[1,1,3,64]{3,1,2,0:T(1,128)S(1)}, s32[1,1,3,64]{3,1,2,0:T(1,128)}, u32[]{:S(2)}) copy-start(s32[1,1,3,64]{3,1,2,0:T(1,128)} %param.23) | copy-start | bytes 2308
  0.7 13.7 %copy-start.19 = (s32[1,1,2048]{2,1,0:T(1,128)S(1)}, s32[1,1,2048]{2,1,0:T(1,128)}, u32[]{:S(2)}) copy-start(s32[1,1,2048]{2,1,0:T(1,128)} %param.21) | copy-start | bytes 24580
  0.7 14.3 %copy-start.25 = (s32[1,1,8]{2,1,0:T(1,128)S(1)}, s32[1,1,8]{2,1,0:T(1,128)}, u32[]{:S(2)}) copy-start(s32[1,1,8]{2,1,0:T(1,128)} %param.25) | copy-start | bytes 100
  0.7 14.3 %copy-start.23 = (s32[1,1,8,128]{3,2,1,0:T(8,128)S(1)}, s32[1,1,8,128]{3,2,1,0:T(8,128)}, u32[]{:S(2)}) copy-start(s32[1,1,8,128]{3,2,1,0:T(8,128)} %param.24) | copy-start | bytes 12292
  3.3 14.9 %collective-permute-start = (f32[12288]{0:T(1024)S(1)}, f32[12288]{0:T(1024)S(1)}, u32[]{:S(2)}, u32[]{:S(2)}) collective-permute-start(f32[12288]{0:T(1024)S(1)} %get-tuple-element.66), channel_id=1, source_target_pairs={{0,8},{8,16},{16,24},{24,32},{32,40},{40,48},{48,56},{56,64},{64,7... | collective-permute-start | bytes 147464 | tf_op jit(solution)/shard_map/ppermute | solution.py:164
  7.1 11.2 %collective-permute-start.1 = (f32[12288]{0:T(1024)S(1)}, f32[12288]{0:T(1024)S(1)}, u32[]{:S(2)}, u32[]{:S(2)}) collective-permute-start(f32[12288]{0:T(1024)S(1)} %get-tuple-element.67), channel_id=1, source_target_pairs={{8,0},{16,8},{24,16},{32,24},{40,32},{48,40},{56,48},{64,56},{72,6... | collective-permute-start | bytes 147464 | tf_op jit(solution)/shard_map/ppermute | solution.py:165
  17.5 19.0 %copy-start.22 = (f32[8]{0:T(128)}, f32[8]{0:T(128)S(1)}, u32[]{:S(2)}) copy-start(f32[8]{0:T(128)S(1)} %multiply_subtract_fusion) | copy-start | bytes 100
  18.3 0.6 copy-start.9
  18.3 0.6 copy-start.7
  19.7 11.7 %collective-permute-start.2 = (f32[13152]{0:T(1024)S(1)}, f32[13152]{0:T(1024)S(1)}, u32[]{:S(2)}, u32[]{:S(2)}) collective-permute-start(f32[13152]{0:T(1024)S(1)} %get-tuple-element.64), channel_id=1, source_target_pairs={{0,1},{1,2},{2,3},{3,4},{4,5},{5,6},{6,7},{7,128},{128,129},{129,1... | collective-permute-start | bytes 157832 | tf_op jit(solution)/shard_map/ppermute | solution.py:164
  21.7 9.0 %collective-permute-start.3 = (f32[13152]{0:T(1024)S(1)}, f32[13152]{0:T(1024)S(1)}, u32[]{:S(2)}, u32[]{:S(2)}) collective-permute-start(f32[13152]{0:T(1024)S(1)} %get-tuple-element.65), channel_id=1, source_target_pairs={{1,0},{2,1},{3,2},{4,3},{5,4},{6,5},{7,6},{128,7},{129,128},{130,1... | collective-permute-start | bytes 157832 | tf_op jit(solution)/shard_map/ppermute | solution.py:165
  30.7 1.6 %copy-start.12 = (f32[13152]{0:T(1024)}, f32[13152]{0:T(1024)S(1)}, u32[]{:S(2)}) copy-start(f32[13152]{0:T(1024)S(1)} %collective-permute-done.3) | copy-start | bytes 157828
  31.4 0.7 copy-start.14
  37.7 1.2 %copy-start.15 = (f32[13152]{0:T(1024)S(1)}, f32[13152]{0:T(1024)}, u32[]{:S(2)}) copy-start(f32[13152]{0:T(1024)} %copy-done.14) | copy-start | bytes 157828
  37.7 1.3 %copy-start.13 = (f32[13152]{0:T(1024)S(1)}, f32[13152]{0:T(1024)}, u32[]{:S(2)}) copy-start(f32[13152]{0:T(1024)} %copy-done.12) | copy-start | bytes 157828
  37.7 1.5 %copy-start.10 = (f32[1,5,512]{2,1,0:T(8,128)S(1)}, f32[1,5,512]{2,1,0:T(8,128)}, u32[]{:S(2)}) copy-start(f32[1,5,512]{2,1,0:T(8,128)} %copy-done.9) | copy-start | bytes 30724
  37.8 1.5 %copy-start.8 = (f32[1,5,512]{2,1,0:T(8,128)S(1)}, f32[1,5,512]{2,1,0:T(8,128)}, u32[]{:S(2)}) copy-start(f32[1,5,512]{2,1,0:T(8,128)} %copy-done.7) | copy-start | bytes 30724
  39.0 0.8 copy-start.4
  42.2 10.6 %copy-start.16 = (f32[64,1,128,1]{2,1,0,3:T(1,128)S(1)}, f32[64,1,128,1]{2,1,0,3:T(1,128)}, u32[]{:S(2)}) copy-start(f32[64,1,128,1]{2,1,0,3:T(1,128)} %get-tuple-element.39) | copy-start | bytes 98308
  42.2 10.6 %copy-start.17 = (f32[64,1,128,1]{2,1,0,3:T(1,128)S(1)}, f32[64,1,128,1]{2,1,0,3:T(1,128)}, u32[]{:S(2)}) copy-start(f32[64,1,128,1]{2,1,0,3:T(1,128)} %get-tuple-element.40) | copy-start | bytes 98308
  42.2 10.6 %copy-start.18 = (f32[64,1,128,1]{2,1,0,3:T(1,128)S(1)}, f32[64,1,128,1]{2,1,0,3:T(1,128)}, u32[]{:S(2)}) copy-start(f32[64,1,128,1]{2,1,0,3:T(1,128)} %get-tuple-element.41) | copy-start | bytes 98308
  44.5 15.4 %copy-start.2 = (f32[2,8,72,136]{3,2,1,0:T(8,128)}, f32[2,8,72,136]{3,2,1,0:T(8,128)S(1)}, u32[]{:S(2)}) copy-start(f32[2,8,72,136]{3,2,1,0:T(8,128)S(1)} %fusion.40) | copy-start | bytes 1880068
  44.6 15.3 %copy-start.26 = (s32[64]{0:T(128)S(1)}, s32[64]{0:T(128)}, u32[]{:S(2)}) copy-start(s32[64]{0:T(128)} %slice_bitcast_fusion.2) | copy-start | bytes 772
  44.6 15.3 %copy-start.27 = (pred[64]{0:T(512)(128)(4,1)S(1)}, pred[64]{0:T(512)(128)(4,1)}, u32[]{:S(2)}) copy-start(pred[64]{0:T(512)(128)(4,1)} %iota_compare_fusion.3) | copy-start | bytes 196
  44.6 15.5 %collective-permute-start.4 = (f32[4,32,128]{2,1,0:T(8,128)S(1)}, f32[4,32,128]{2,1,0:T(8,128)S(1)}, u32[]{:S(2)}, u32[]{:S(2)}) collective-permute-start(f32[4,32,128]{2,1,0:T(8,128)S(1)} %get-tuple-element.50), channel_id=1, source_target_pairs={{0,8},{8,16},{16,24},{24,32},{32,40},{40,48},{48,56},{56,64},{64,7... | collective-permute-start | bytes 196616 | tf_op jit(solution)/shard_map/ppermute | solution.py:164
  46.6 13.6 %collective-permute-start.5 = (f32[4,32,128]{2,1,0:T(8,128)S(1)}, f32[4,32,128]{2,1,0:T(8,128)S(1)}, u32[]{:S(2)}, u32[]{:S(2)}) collective-permute-start(f32[4,32,128]{2,1,0:T(8,128)S(1)} %get-tuple-element.51), channel_id=1, source_target_pairs={{8,0},{16,8},{24,16},{32,24},{40,32},{48,40},{56,48},{64,56},{72,6... | collective-permute-start | bytes 196616 | tf_op jit(solution)/shard_map/ppermute | solution.py:165
  52.8 12.5 %copy-start.6 = (f32[1,1,2,2048]{3,2,1,0:T(2,128)S(1)}, f32[1,1,2,2048]{3,2,1,0:T(2,128)}, u32[]{:S(2)}) copy-start(f32[1,1,2,2048]{3,2,1,0:T(2,128)} %param.16) | copy-start | bytes 49156
  52.8 12.5 %copy-start.20 = (f32[2048]{0:T(1024)S(1)}, f32[2048]{0:T(1024)}, u32[]{:S(2)}) copy-start(f32[2048]{0:T(1024)} %multiply_multiply_fusion) | copy-start | bytes 24580
  52.8 12.5 %copy-start.21 = (f32[1,1,2048]{2,1,0:T(1,128)S(1)}, f32[1,1,2048]{2,1,0:T(1,128)}, u32[]{:S(2)}) copy-start(f32[1,1,2048]{2,1,0:T(1,128)} %param.19) | copy-start | bytes 24580
  73.1 6.6 %collective-permute-start.6 = (f32[3,40,128]{2,1,0:T(8,128)S(1)}, f32[3,40,128]{2,1,0:T(8,128)S(1)}, u32[]{:S(2)}, u32[]{:S(2)}) collective-permute-start(f32[3,40,128]{2,1,0:T(8,128)S(1)} %get-tuple-element.44), channel_id=1, source_target_pairs={{8,0},{16,8},{24,16},{32,24},{40,32},{48,40},{56,48},{64,56},{72,6... | collective-permute-start | bytes 184328 | tf_op jit(solution)/shard_map/ppermute | solution.py:165
  75.0 8.2 %collective-permute-start.7 = (f32[3,40,128]{2,1,0:T(8,128)S(1)}, f32[3,40,128]{2,1,0:T(8,128)S(1)}, u32[]{:S(2)}, u32[]{:S(2)}) collective-permute-start(f32[3,40,128]{2,1,0:T(8,128)S(1)} %get-tuple-element.45), channel_id=1, source_target_pairs={{0,8},{8,16},{16,24},{24,32},{32,40},{40,48},{48,56},{56,64},{64,7... | collective-permute-start | bytes 184328 | tf_op jit(solution)/shard_map/ppermute | solution.py:164
  83.2 7.6 %collective-permute-start.8 = (f32[3,40,128]{2,1,0:T(8,128)S(1)}, f32[3,40,128]{2,1,0:T(8,128)S(1)}, u32[]{:S(2)}, u32[]{:S(2)}) collective-permute-start(f32[3,40,128]{2,1,0:T(8,128)S(1)} %pad_maximum_fusion.8), channel_id=1, source_target_pairs={{1,0},{2,1},{3,2},{4,3},{5,4},{6,5},{7,6},{128,7},{129,128},{130,1... | collective-permute-start | bytes 184328 | tf_op jit(solution)/shard_map/ppermute | solution.py:165
  90.9 9.2 %collective-permute-start.9 = (f32[3,40,128]{2,1,0:T(8,128)S(1)}, f32[3,40,128]{2,1,0:T(8,128)S(1)}, u32[]{:S(2)}, u32[]{:S(2)}) collective-permute-start(f32[3,40,128]{2,1,0:T(8,128)S(1)} %pad_maximum_fusion.9), channel_id=1, source_target_pairs={{0,1},{1,2},{2,3},{3,4},{4,5},{5,6},{6,7},{7,128},{128,129},{129,1... | collective-permute-start | bytes 184328 | tf_op jit(solution)/shard_map/ppermute | solution.py:164

commit v4 on v3

--- a/solution.py
+++ b/solution.py
@@ -262,8 +262,17 @@
     )
     lists = contact_list[0, 0]
     count = contact_count[0, 0]
-    valid = jnp.arange(lists.shape[1], dtype=jnp.int32) < count
-    contact = contact_batch(table, lists, valid, blocks, GHOST)
+    slots = lists.shape[1]
+    batch = math.gcd(slots, 32)
+    rounds = (count + batch - 1) // batch
+
+    def accumulate(turn, total):
+        start = turn * batch
+        group = lax.dynamic_slice_in_dim(lists, start, batch, 1)
+        valid = start + jnp.arange(batch, dtype=jnp.int32) < count
+        return total + contact_batch(table, group, valid, blocks, GHOST)
+
+    contact = lax.fori_loop(0, rounds, accumulate, jnp.zeros((blocks, 2, 128), jnp.float32))
     contact = contact.transpose(1, 0, 2).reshape(2, floes)
     area = math.pi * radius * radius
     relative = sampled[0:2] - velocity

time: 102 us -> 97.8 us (0.959); the launches traced: 101 us -> 98.1 us
  other arithmetic: 26 us -> 21.9 us
  starting transfers between devices: 40.7 us -> 42.9 us
  local copies, waits for them, and re-layouts: 11.2 us -> 10.1 us
    reduce_sum x1, other arithmetic: 7.06 us -> 3.51 us  [pair_forces(): jnp.sum(magnitude * normal_x, axis=1)]
    ppermute x5, starting transfers between devices: 27.2 us -> 30.2 us  [exchange(): from_next = lax.ppermute(low, axis, down)]
  transfers between devices with their start and end apart: 10 -> 10, of which waited for: 4 -> 4; matrix products, arithmetic and copies ran while one was open for 16% -> 14% of each run, Pallas kernels for 0% -> 0%
where the time goes in v4:
time: 97.8 us; the launch traced here: 98.1 us
  starting transfers between devices  42.9 us (44%)
  other arithmetic  21.9 us (22%)
  waiting for transfers between devices  11.7 us (12%)
  local copies, waits for them, and re-layouts  10.1 us (10%)
  Pallas kernels  8.92 us (9%)
  between operations  2.2 us (2%)
    ppermute x5, starting transfers between devices, exchange(): from_next = lax.ppermute(low, axis, down)  30.2 us
    ppermute x5, starting transfers between devices, exchange(): from_previous = lax.ppermute(high, axis, up)  12.7 us
    ppermute x5, waiting for transfers between devices, exchange(): from_previous = lax.ppermute(high, axis, up)  9.33 us
    mul x4, other arithmetic, ocean_substep(): return (flow + horizontal * lap + vert + turning + surface) * wet[None]  5.52 us
    pallas_call x1, Pallas kernels, gather_records(): pl.pallas_call(gather_kernel, out_shape=jax.ShapeDtypeStruct((index.shape...  5.33 us
    pallas_call x1, Pallas kernels, sample_surface(): pl.pallas_call(sample_kernel, out_shape=jax.ShapeDtypeStruct((window.shap...  3.59 us
    reduce_sum x1, other arithmetic, pair_forces(): jnp.sum(magnitude * normal_x, axis=1)  3.51 us
    ppermute x5, waiting for transfers between devices, exchange(): from_next = lax.ppermute(low, axis, down)  2.33 us
  transfers between devices with their start and end apart: 10, of which 4 were waited for; matrix products, arithmetic and copies ran while one was open for 14% of the time, Pallas kernels for 0%

profile of v4, /device:TPU:24, one launch (start us, length us, event | category | flops | bytes accessed | tf_op | source)
XLA Modules:
  0.0 98.1 jit_solution(4796521711673956943)
XLA Ops:
  0.7 0.8 pad_maximum_fusion.17
  1.5 0.8 convert_bitcast_fusion
  2.3 0.9 pad_maximum_fusion.15
  3.3 3.8 %collective-permute-start = (f32[12288]{0:T(1024)S(1)}, f32[12288]{0:T(1024)S(1)}, u32[]{:S(2)}, u32[]{:S(2)}) collective-permute-start(f32[12288]{0:T(1024)S(1)} %get-tuple-element.116), channel_id=1, source_target_pairs={{0,8},{8,16},{16,24},{24,32},{32,40},{40,48},{48,56},{56,64},{64,7... | collective-permute-start | bytes 147464 | tf_op jit(solution)/shard_map/ppermute | solution.py:164
  7.1 6.0 %collective-permute-start.1 = (f32[12288]{0:T(1024)S(1)}, f32[12288]{0:T(1024)S(1)}, u32[]{:S(2)}, u32[]{:S(2)}) collective-permute-start(f32[12288]{0:T(1024)S(1)} %get-tuple-element.117), channel_id=1, source_target_pairs={{8,0},{16,8},{24,16},{32,24},{40,32},{48,40},{56,48},{64,56},{72,6... | collective-permute-start | bytes 147464 | tf_op jit(solution)/shard_map/ppermute | solution.py:165
  13.2 0.6 multiply_multiply_fusion
  13.8 0.6 and_select_fusion
  14.4 0.7 bitcast_select_fusion.index_ref
  15.1 0.6 fusion.64.rows_ref
  15.7 0.7 maximum_bitcast_fusion.2
  16.6 0.2 fusion.68
  16.9 0.1 copy-done.9
  17.1 0.4 reshape.336
  17.4 0.4 reshape.339
  17.9 1.9 %collective-permute-start.2 = (f32[13152]{0:T(1024)S(1)}, f32[13152]{0:T(1024)S(1)}, u32[]{:S(2)}, u32[]{:S(2)}) collective-permute-start(f32[13152]{0:T(1024)S(1)} %get-tuple-element.114), channel_id=1, source_target_pairs={{0,1},{1,2},{2,3},{3,4},{4,5},{5,6},{6,7},{7,128},{128,129},{129,1... | collective-permute-start | bytes 157832 | tf_op jit(solution)/shard_map/ppermute | solution.py:164
  19.8 7.3 %collective-permute-start.3 = (f32[13152]{0:T(1024)S(1)}, f32[13152]{0:T(1024)S(1)}, u32[]{:S(2)}, u32[]{:S(2)}) collective-permute-start(f32[13152]{0:T(1024)S(1)} %get-tuple-element.115), channel_id=1, source_target_pairs={{1,0},{2,1},{3,2},{4,3},{5,4},{6,5},{7,6},{128,7},{129,128},{130,1... | collective-permute-start | bytes 157832 | tf_op jit(solution)/shard_map/ppermute | solution.py:165
  27.8 0.6 copy.28
  28.4 0.5 collective-permute-done.3
  28.8 0.7 reshape.340
  29.6 0.7 reshape.338
  30.3 0.1 maximum_bitcast_fusion.1
  30.4 0.1 fusion.60
  30.6 0.7 pad_maximum_fusion
  31.5 0.1 broadcast_multiply_fusion
  31.6 0.1 slice_multiply_fusion.7
  31.7 0.2 fusion.58
  31.9 1.1 %fusion.51 = f32[2,8,72,136]{3,2,1,0:T(8,128)S(1)} fusion(f32[2,1,72,136]{3,2,1,0:T(8,128)S(1)} %fusion.60, f32[1,8,72,136]{3,2,1,0:T(8,128)S(1)} %get-tuple-element.87, f32[1,8,72,136]{3,2,1,0:T(8,128)S(1)} %get-tuple-element.86, f32[2,7,72,136]{3,2,1,0:T(8,128)S(1)} %fusion.58, f32[2,8,72,136]{3,2,1,0:T(8,128)S(1)} %broadcast_multiply_fusion, ...), kind=kLoop, calls=%fused_computation.94 | loop fusion | flops 2036736 | bytes 2820128 | tf_op jit(solution)/shard_map/mul | solution.py:55
  33.0 0.2 fusion.57
  33.1 0.1 slice_multiply_fusion.5
  33.3 1.1 %fusion.52 = f32[2,8,72,136]{3,2,1,0:T(8,128)S(1)} fusion(f32[2,1,72,136]{3,2,1,0:T(8,128)S(1)} %fusion.60, f32[1,8,72,136]{3,2,1,0:T(8,128)S(1)} %get-tuple-element.85, f32[1,8,72,136]{3,2,1,0:T(8,128)S(1)} %get-tuple-element.84, f32[2,7,72,136]{3,2,1,0:T(8,128)S(1)} %fusion.57, f32[2,8,72,136]{3,2,1,0:T(8,128)S(1)} %fusion.51, ...), kind=kLoop, calls=%fused_computation.95 | loop fusion | flops 2036736 | bytes 2820128 | tf_op jit(solution)/shard_map/mul | solution.py:55
  34.4 0.2 fusion.56
  34.5 0.1 slice_multiply_fusion.3
  34.6 1.1 %fusion.53 = f32[2,8,72,136]{3,2,1,0:T(8,128)S(1)} fusion(f32[2,1,72,136]{3,2,1,0:T(8,128)S(1)} %fusion.60, f32[1,8,72,136]{3,2,1,0:T(8,128)S(1)} %get-tuple-element.83, f32[1,8,72,136]{3,2,1,0:T(8,128)S(1)} %get-tuple-element.82, f32[2,7,72,136]{3,2,1,0:T(8,128)S(1)} %fusion.56, f32[2,8,72,136]{3,2,1,0:T(8,128)S(1)} %fusion.52, ...), kind=kLoop, calls=%fused_computation.96 | loop fusion | flops 2036736 | bytes 2820128 | tf_op jit(solution)/shard_map/mul | solution.py:55
  35.7 0.1 fusion.55
  35.9 1.2 %slice_multiply_fusion.1 = (f32[1,8,72,136]{3,2,1,0:T(8,128)}, f32[1,8,72,136]{3,2,1,0:T(8,128)}) fusion(f32[2,8,72,136]{3,2,1,0:T(8,128)S(1)} %fusion.53), kind=kLoop, calls=%fused_computation.108 | loop fusion | flops 156672 | bytes 1253376 | tf_op jit(solution)/shard_map/mul | solution.py:53
  37.2 0.1 fusion.75
  37.5 0.2 copy-done.21
  37.7 2.2 %fusion.54 = f32[2,8,72,136]{3,2,1,0:T(8,128)S(1)} fusion(f32[2,1,72,136]{3,2,1,0:T(8,128)S(1)} %fusion.60, f32[1,8,72,136]{3,2,1,0:T(8,128)} %get-tuple-element.81, f32[1,8,72,136]{3,2,1,0:T(8,128)} %get-tuple-element.80, f32[2,7,72,136]{3,2,1,0:T(8,128)S(1)} %fusion.55, f32[2,8,72,136]{3,2,1,0:T(8,128)S(1)} %fusion.53, f32[8]{0:T(128)S(1)} %copy-done.21, ...), kind=kLoop, calls=%fused_computation.97 | loop fusion | flops 2036736 | bytes 2820128 | tf_op jit(solution)/shard_map/mul | solution.py:55
  40.0 0.1 slice_bitcast_fusion.2
  40.1 1.9 %collective-permute-start.4 = (f32[4,32,128]{2,1,0:T(8,128)S(1)}, f32[4,32,128]{2,1,0:T(8,128)S(1)}, u32[]{:S(2)}, u32[]{:S(2)}) collective-permute-start(f32[4,32,128]{2,1,0:T(8,128)S(1)} %get-tuple-element.100), channel_id=1, source_target_pairs={{0,8},{8,16},{16,24},{24,32},{32,40},{40,48},{48,56},{56,64},{64,7... | collective-permute-start | bytes 196616 | tf_op jit(solution)/shard_map/ppermute | solution.py:164
  42.1 6.0 %collective-permute-start.5 = (f32[4,32,128]{2,1,0:T(8,128)S(1)}, f32[4,32,128]{2,1,0:T(8,128)S(1)}, u32[]{:S(2)}, u32[]{:S(2)}) collective-permute-start(f32[4,32,128]{2,1,0:T(8,128)S(1)} %get-tuple-element.101), channel_id=1, source_target_pairs={{8,0},{16,8},{24,16},{32,24},{40,32},{48,40},{56,48},{64,56},{72,6... | collective-permute-start | bytes 196616 | tf_op jit(solution)/shard_map/ppermute | solution.py:165
  48.2 6.0 %while.10 = (s32[]{:T(128)}, f32[16,2,128]{2,0,1:T(8,128)S(1)}, s32[]{:T(128)}, s32[3,64]{1,0:T(4,128)S(1)}, s32[]{:T(128)}, /*index=5*/f32[48,5,128]{2,1,0:T(8,...) while((s32[]{:T(128)}, f32[16,2,128]{2,0,1:T(8,128)S(1)}, s32[]{:T(128)}, s32[3,64]{1,0:T(4,128)S(1)}, ...), condition=%wide.region_3.4_spmd, body=%wide.region_0.3_spmd.sunk | while | flops 15744006 | bytes 928223 | solution.py:275
  48.2 0.7 add_compare_fusion.2
  49.0 0.6 gather_fusion
  49.6 0.6 gather_fusion.1
  50.3 3.5 %multiply_reduce_fusion.4 = (f32[32,128]{1,0:T(8,128)S(1)}, f32[32,128]{1,0:T(8,128)S(1)}) fusion(f32[32,128]{1,0:T(8,128)S(1)} %bitcast.149, f32[32,128]{1,0:T(8,128)S(1)} %bitcast.154, f32[32,128]{1,0:T(8,128)S(1)} %bitcast.150, f32[32,128]{1,0:T(8,128)S(1)} %bitcast.155, f32[32,128]{1,0:T(8,128)S(1)} %bitcast.147, f32[32,128]{1,0:T(8,128)S(1)} %bitcast.152, ...), kind=kLoop, calls=%fused_computation.15.clone.1 | loop fusion | flops 14147584 | bytes 196608 | tf_op jit(solution)/shard_map/while/body/reduce_sum | solution.py:73
  53.8 0.2 convolution_add_fusion.2
  54.2 0.7 pad_maximum_fusion.2.window_ref
  54.9 3.6 %shard_map.148 = f32[4,2048]{1,0:T(4,128)} custom-call(f32[4,128,128]{2,1,0:T(8,128)} %pad_maximum_fusion.2.window_ref, s32[1,2048]{1,0:T(1,128)} %fusion.64.rows_ref, s32[1,2048]{1,0:T(1,128)} %get-tuple-element.62.cols_ref), custom_call_target="tpu_custom_call" | custom-call | tf_op jit(solution)/shard_map/pallas_call | solution.py:127
  58.5 0.8 multiply_reduce_fusion.2
  59.3 0.9 multiply_add_fusion
  60.2 0.6 pad_maximum_fusion.16
  60.9 5.3 %shard_map.149 = f32[8,40,128]{2,1,0:T(8,128)} custom-call(f32[4,2048]{1,0:T(4,128)} %get-tuple-element.112.state_ref, f32[1,2048]{1,0:T(1,128)} %bitcast.165, f32[1,2048]{1,0:T(1,128)} %bitcast.169, f32[32,2048]{1,0:T(8,128)} %bitcast.160, s32[8,128]{1,0:T(8,128)} %bitcast_select_fusion.index_ref), custom_call_target="tpu_custom_call" | custom-call | tf_op jit(solution)/shard_map/pallas_call | solution.py:153
  66.2 0.9 fusion.70
  67.1 2.7 %collective-permute-start.6 = (f32[3,40,128]{2,1,0:T(8,128)S(1)}, f32[3,40,128]{2,1,0:T(8,128)S(1)}, u32[]{:S(2)}, u32[]{:S(2)}) collective-permute-start(f32[3,40,128]{2,1,0:T(8,128)S(1)} %get-tuple-element.94), channel_id=1, source_target_pairs={{8,0},{16,8},{24,16},{32,24},{40,32},{48,40},{56,48},{64,56},{72,6... | collective-permute-start | bytes 184328 | tf_op jit(solution)/shard_map/ppermute | solution.py:165
  69.8 3.1 %collective-permute-start.7 = (f32[3,40,128]{2,1,0:T(8,128)S(1)}, f32[3,40,128]{2,1,0:T(8,128)S(1)}, u32[]{:S(2)}, u32[]{:S(2)}) collective-permute-start(f32[3,40,128]{2,1,0:T(8,128)S(1)} %get-tuple-element.95), channel_id=1, source_target_pairs={{0,8},{8,16},{16,24},{24,32},{32,40},{40,48},{48,56},{56,64},{64,7... | collective-permute-start | bytes 184328 | tf_op jit(solution)/shard_map/ppermute | solution.py:164
  72.9 0.8 fusion.69
  73.7 4.3 %collective-permute-done.7 = f32[3,40,128]{2,1,0:T(8,128)S(1)} collective-permute-done((f32[3,40,128]{2,1,0:T(8,128)S(1)}, f32[3,40,128]{2,1,0:T(8,128)S(1)}, u32[]{:S(2)}, u32[]{:S(2)}) %collective-permute-start.7) | collective-permute-done | bytes 61472 | tf_op jit(solution)/shard_map/ppermute | solution.py:164
  78.0 8.2 %collective-permute-start.8 = (f32[3,40,128]{2,1,0:T(8,128)S(1)}, f32[3,40,128]{2,1,0:T(8,128)S(1)}, u32[]{:S(2)}, u32[]{:S(2)}) collective-permute-start(f32[3,40,128]{2,1,0:T(8,128)S(1)} %pad_maximum_fusion.8), channel_id=1, source_target_pairs={{1,0},{2,1},{3,2},{4,3},{5,4},{6,5},{7,6},{128,7},{129,128},{130,1... | collective-permute-start | bytes 184328 | tf_op jit(solution)/shard_map/ppermute | solution.py:165
  86.2 1.8 %collective-permute-done.8 = f32[3,40,128]{2,1,0:T(8,128)S(1)} collective-permute-done((f32[3,40,128]{2,1,0:T(8,128)S(1)}, f32[3,40,128]{2,1,0:T(8,128)S(1)}, u32[]{:S(2)}, u32[]{:S(2)}) %collective-permute-start.8) | collective-permute-done | bytes 61472 | tf_op jit(solution)/shard_map/ppermute | solution.py:165
  88.1 1.9 %collective-permute-start.9 = (f32[3,40,128]{2,1,0:T(8,128)S(1)}, f32[3,40,128]{2,1,0:T(8,128)S(1)}, u32[]{:S(2)}, u32[]{:S(2)}) collective-permute-start(f32[3,40,128]{2,1,0:T(8,128)S(1)} %pad_maximum_fusion.9), channel_id=1, source_target_pairs={{0,1},{1,2},{2,3},{3,4},{4,5},{5,6},{6,7},{7,128},{128,129},{129,1... | collective-permute-start | bytes 184328 | tf_op jit(solution)/shard_map/ppermute | solution.py:164
  90.0 2.3 %slice.485 = f32[2,8,64,128]{3,2,1,0:T(8,128)} slice(f32[2,8,72,136]{3,2,1,0:T(8,128)} %copy-done.2), slice={[0:2], [0:8], [4:68], [4:132]} | slice | bytes 1048576 | tf_op jit(solution)/shard_map/slice | solution.py:250
  92.3 5.0 %collective-permute-done.9 = f32[3,40,128]{2,1,0:T(8,128)S(1)} collective-permute-done((f32[3,40,128]{2,1,0:T(8,128)S(1)}, f32[3,40,128]{2,1,0:T(8,128)S(1)}, u32[]{:S(2)}, u32[]{:S(2)}) %collective-permute-start.9) | collective-permute-done | bytes 61472 | tf_op jit(solution)/shard_map/ppermute | solution.py:164
  97.4 0.7 copy.18
  (120 shorter events, 1.2 us)
Async XLA Ops:
  0.6 12.5 %copy-start.11 = (f32[1,1,2048]{2,1,0:T(1,128)S(1)}, f32[1,1,2048]{2,1,0:T(1,128)}, u32[]{:S(2)}) copy-start(f32[1,1,2048]{2,1,0:T(1,128)} %param.20) | copy-start | bytes 24580
  0.6 15.0 %copy-start.5 = (f32[1,1,2,2048]{3,2,1,0:T(2,128)S(1)}, f32[1,1,2,2048]{3,2,1,0:T(2,128)}, u32[]{:S(2)}) copy-start(f32[1,1,2,2048]{3,2,1,0:T(2,128)} %param.18) | copy-start | bytes 49156
  0.7 15.0 %copy-start.3 = (f32[1,1,2,2048]{3,2,1,0:T(2,128)S(1)}, f32[1,1,2,2048]{3,2,1,0:T(2,128)}, u32[]{:S(2)}) copy-start(f32[1,1,2,2048]{3,2,1,0:T(2,128)} %param.19) | copy-start | bytes 49156
  0.7 15.9 %copy-start.1 = (f32[2,64,128]{2,1,0:T(8,128)S(1)}, f32[2,64,128]{2,1,0:T(8,128)}, u32[]{:S(2)}) copy-start(f32[2,64,128]{2,1,0:T(8,128)} %param.16) | copy-start | bytes 196612
  0.7 15.9 %copy-start = (f32[2,8,64,128]{3,2,1,0:T(8,128)S(1)}, f32[2,8,64,128]{3,2,1,0:T(8,128)}, u32[]{:S(2)}) copy-start(f32[2,8,64,128]{3,2,1,0:T(8,128)} %param.15) | copy-start | bytes 1572868
  0.7 13.1 %copy-start.17 = (s32[1,1,2048]{2,1,0:T(1,128)S(1)}, s32[1,1,2048]{2,1,0:T(1,128)}, u32[]{:S(2)}) copy-start(s32[1,1,2048]{2,1,0:T(1,128)} %param.23) | copy-start | bytes 24580
  0.7 13.7 %copy-start.24 = (s32[1,1,8]{2,1,0:T(1,128)S(1)}, s32[1,1,8]{2,1,0:T(1,128)}, u32[]{:S(2)}) copy-start(s32[1,1,8]{2,1,0:T(1,128)} %param.27) | copy-start | bytes 100
  0.7 13.7 %copy-start.22 = (s32[1,1,8,128]{3,2,1,0:T(8,128)S(1)}, s32[1,1,8,128]{3,2,1,0:T(8,128)}, u32[]{:S(2)}) copy-start(s32[1,1,8,128]{3,2,1,0:T(8,128)} %param.26) | copy-start | bytes 12292
  3.3 13.1 %collective-permute-start = (f32[12288]{0:T(1024)S(1)}, f32[12288]{0:T(1024)S(1)}, u32[]{:S(2)}, u32[]{:S(2)}) collective-permute-start(f32[12288]{0:T(1024)S(1)} %get-tuple-element.116), channel_id=1, source_target_pairs={{0,8},{8,16},{16,24},{24,32},{32,40},{40,48},{48,56},{56,64},{64,7... | collective-permute-start | bytes 147464 | tf_op jit(solution)/shard_map/ppermute | solution.py:164
  7.1 9.3 %collective-permute-start.1 = (f32[12288]{0:T(1024)S(1)}, f32[12288]{0:T(1024)S(1)}, u32[]{:S(2)}, u32[]{:S(2)}) collective-permute-start(f32[12288]{0:T(1024)S(1)} %get-tuple-element.117), channel_id=1, source_target_pairs={{8,0},{16,8},{24,16},{32,24},{40,32},{48,40},{56,48},{64,56},{72,6... | collective-permute-start | bytes 147464 | tf_op jit(solution)/shard_map/ppermute | solution.py:165
  16.4 0.6 copy-start.9
  16.5 0.6 copy-start.7
  17.1 10.7 %copy-start.23 = (s32[1,1,3,64]{3,1,2,0:T(1,128)S(1)}, s32[1,1,3,64]{3,1,2,0:T(1,128)}, u32[]{:S(2)}) copy-start(s32[1,1,3,64]{3,1,2,0:T(1,128)} %param.25) | copy-start | bytes 2308
  17.9 11.7 %collective-permute-start.2 = (f32[13152]{0:T(1024)S(1)}, f32[13152]{0:T(1024)S(1)}, u32[]{:S(2)}, u32[]{:S(2)}) collective-permute-start(f32[13152]{0:T(1024)S(1)} %get-tuple-element.114), channel_id=1, source_target_pairs={{0,1},{1,2},{2,3},{3,4},{4,5},{5,6},{6,7},{7,128},{128,129},{129,1... | collective-permute-start | bytes 157832 | tf_op jit(solution)/shard_map/ppermute | solution.py:164
  19.8 9.0 %collective-permute-start.3 = (f32[13152]{0:T(1024)S(1)}, f32[13152]{0:T(1024)S(1)}, u32[]{:S(2)}, u32[]{:S(2)}) collective-permute-start(f32[13152]{0:T(1024)S(1)} %get-tuple-element.115), channel_id=1, source_target_pairs={{1,0},{2,1},{3,2},{4,3},{5,4},{6,5},{7,6},{128,7},{129,128},{130,1... | collective-permute-start | bytes 157832 | tf_op jit(solution)/shard_map/ppermute | solution.py:165
  27.1 7.6 %copy-start.20 = (f32[8]{0:T(128)}, f32[8]{0:T(128)S(1)}, u32[]{:S(2)}) copy-start(f32[8]{0:T(128)S(1)} %multiply_subtract_fusion) | copy-start | bytes 100
  28.8 1.6 %copy-start.13 = (f32[13152]{0:T(1024)}, f32[13152]{0:T(1024)S(1)}, u32[]{:S(2)}) copy-start(f32[13152]{0:T(1024)S(1)} %collective-permute-done.3) | copy-start | bytes 157828
  29.6 0.7 copy-start.15
  35.9 1.2 %copy-start.16 = (f32[13152]{0:T(1024)S(1)}, f32[13152]{0:T(1024)}, u32[]{:S(2)}) copy-start(f32[13152]{0:T(1024)} %copy-done.15) | copy-start | bytes 157828
  35.9 1.3 %copy-start.14 = (f32[13152]{0:T(1024)S(1)}, f32[13152]{0:T(1024)}, u32[]{:S(2)}) copy-start(f32[13152]{0:T(1024)} %copy-done.13) | copy-start | bytes 157828
  35.9 1.4 %copy-start.10 = (f32[1,5,512]{2,1,0:T(8,128)S(1)}, f32[1,5,512]{2,1,0:T(8,128)}, u32[]{:S(2)}) copy-start(f32[1,5,512]{2,1,0:T(8,128)} %copy-done.9) | copy-start | bytes 30724
  35.9 1.5 %copy-start.8 = (f32[1,5,512]{2,1,0:T(8,128)S(1)}, f32[1,5,512]{2,1,0:T(8,128)}, u32[]{:S(2)}) copy-start(f32[1,5,512]{2,1,0:T(8,128)} %copy-done.7) | copy-start | bytes 30724
  37.1 0.7 copy-start.21
  37.7 10.4 %copy-start.4 = (f32[16,5,128]{2,1,0:T(8,128)S(1)}, f32[16,5,128]{2,1,0:T(8,128)}, u32[]{:S(2)}) copy-start(f32[16,5,128]{2,1,0:T(8,128)} %maximum_bitcast_fusion.2) | copy-start | bytes 122884
  37.7 10.4 %copy-start.12 = (s32[1,1,3,64]{3,2,1,0:T(4,128)S(1)}, s32[1,1,3,64]{3,2,1,0:T(4,128)}, u32[]{:S(2)}) copy-start(s32[1,1,3,64]{3,2,1,0:T(4,128)} %copy.28) | copy-start | bytes 2308
  40.0 2.1 %copy-start.2 = (f32[2,8,72,136]{3,2,1,0:T(8,128)}, f32[2,8,72,136]{3,2,1,0:T(8,128)S(1)}, u32[]{:S(2)}) copy-start(f32[2,8,72,136]{3,2,1,0:T(8,128)S(1)} %fusion.54) | copy-start | bytes 1880068
  40.1 14.0 %collective-permute-start.4 = (f32[4,32,128]{2,1,0:T(8,128)S(1)}, f32[4,32,128]{2,1,0:T(8,128)S(1)}, u32[]{:S(2)}, u32[]{:S(2)}) collective-permute-start(f32[4,32,128]{2,1,0:T(8,128)S(1)} %get-tuple-element.100), channel_id=1, source_target_pairs={{0,8},{8,16},{16,24},{24,32},{32,40},{40,48},{48,56},{56,64},{64,7... | collective-permute-start | bytes 196616 | tf_op jit(solution)/shard_map/ppermute | solution.py:164
  42.1 12.1 %collective-permute-start.5 = (f32[4,32,128]{2,1,0:T(8,128)S(1)}, f32[4,32,128]{2,1,0:T(8,128)S(1)}, u32[]{:S(2)}, u32[]{:S(2)}) collective-permute-start(f32[4,32,128]{2,1,0:T(8,128)S(1)} %get-tuple-element.101), channel_id=1, source_target_pairs={{8,0},{16,8},{24,16},{32,24},{40,32},{48,40},{56,48},{64,56},{72,6... | collective-permute-start | bytes 196616 | tf_op jit(solution)/shard_map/ppermute | solution.py:165
  48.2 11.1 %copy-start.6 = (f32[1,1,2,2048]{3,2,1,0:T(2,128)S(1)}, f32[1,1,2,2048]{3,2,1,0:T(2,128)}, u32[]{:S(2)}) copy-start(f32[1,1,2,2048]{3,2,1,0:T(2,128)} %param.18) | copy-start | bytes 49156
  48.2 11.1 %copy-start.18 = (f32[2048]{0:T(1024)S(1)}, f32[2048]{0:T(1024)}, u32[]{:S(2)}) copy-start(f32[2048]{0:T(1024)} %multiply_multiply_fusion) | copy-start | bytes 24580
  48.2 11.1 %copy-start.19 = (f32[1,1,2048]{2,1,0:T(1,128)S(1)}, f32[1,1,2048]{2,1,0:T(1,128)}, u32[]{:S(2)}) copy-start(f32[1,1,2048]{2,1,0:T(1,128)} %param.21) | copy-start | bytes 24580
  67.1 6.6 %collective-permute-start.6 = (f32[3,40,128]{2,1,0:T(8,128)S(1)}, f32[3,40,128]{2,1,0:T(8,128)S(1)}, u32[]{:S(2)}, u32[]{:S(2)}) collective-permute-start(f32[3,40,128]{2,1,0:T(8,128)S(1)} %get-tuple-element.94), channel_id=1, source_target_pairs={{8,0},{16,8},{24,16},{32,24},{40,32},{48,40},{56,48},{64,56},{72,6... | collective-permute-start | bytes 184328 | tf_op jit(solution)/shard_map/ppermute | solution.py:165
  69.8 8.2 %collective-permute-start.7 = (f32[3,40,128]{2,1,0:T(8,128)S(1)}, f32[3,40,128]{2,1,0:T(8,128)S(1)}, u32[]{:S(2)}, u32[]{:S(2)}) collective-permute-start(f32[3,40,128]{2,1,0:T(8,128)S(1)} %get-tuple-element.95), channel_id=1, source_target_pairs={{0,8},{8,16},{16,24},{24,32},{32,40},{40,48},{48,56},{56,64},{64,7... | collective-permute-start | bytes 184328 | tf_op jit(solution)/shard_map/ppermute | solution.py:164
  78.0 10.0 %collective-permute-start.8 = (f32[3,40,128]{2,1,0:T(8,128)S(1)}, f32[3,40,128]{2,1,0:T(8,128)S(1)}, u32[]{:S(2)}, u32[]{:S(2)}) collective-permute-start(f32[3,40,128]{2,1,0:T(8,128)S(1)} %pad_maximum_fusion.8), channel_id=1, source_target_pairs={{1,0},{2,1},{3,2},{4,3},{5,4},{6,5},{7,6},{128,7},{129,128},{130,1... | collective-permute-start | bytes 184328 | tf_op jit(solution)/shard_map/ppermute | solution.py:165
  88.1 9.2 %collective-permute-start.9 = (f32[3,40,128]{2,1,0:T(8,128)S(1)}, f32[3,40,128]{2,1,0:T(8,128)S(1)}, u32[]{:S(2)}, u32[]{:S(2)}) collective-permute-start(f32[3,40,128]{2,1,0:T(8,128)S(1)} %pad_maximum_fusion.9), channel_id=1, source_target_pairs={{0,1},{1,2},{2,3},{3,4},{4,5},{5,6},{6,7},{7,128},{128,129},{129,1... | collective-permute-start | bytes 184328 | tf_op jit(solution)/shard_map/ppermute | solution.py:164

commit v5 on v4

--- a/solution.py
+++ b/solution.py
@@ -164,6 +164,22 @@
     from_previous = lax.ppermute(high, axis, up)
     from_next = lax.ppermute(low, axis, down)
     return from_previous, from_next
+
+
+def send_to(array, row_step, col_step):
+    sections, rows, cols = lax.axis_size("sec"), lax.axis_size("gx"), lax.axis_size("gy")
+
+    def flat(row, col):
+        return (col // cols) * rows * cols + row * cols + col % cols
+
+    width = sections * cols
+    pairs = [
+        (flat(r, c), flat(r + row_step, c + col_step))
+        for r in range(rows)
+        for c in range(width)
+        if 0 <= r + row_step < rows and 0 <= c + col_step < width
+    ]
+    return lax.ppermute(array, ("sec", "gx", "gy"), pairs)
 
 
 def shards(
@@ -287,21 +303,8 @@
     outgoing = gather_records(
         floe_next, radius[None], mass[None], floe_polygon[0, 0], jnp.where(valid_slots, leaving, -1)
     )
-    from_above, from_below = exchange(outgoing[0:3], outgoing[5:8], "gx")
-    heading_left = jnp.stack([from_below[0], outgoing[3], from_above[0]])
-    heading_right = jnp.stack([from_below[2], outgoing[4], from_above[2]])
-    from_left, from_right = exchange(heading_left, heading_right, columns)
     arrivals = jnp.stack(
-        [
-            from_right[0],
-            from_below[1],
-            from_left[0],
-            from_right[1],
-            from_left[1],
-            from_right[2],
-            from_above[1],
-            from_left[2],
-        ]
+        [send_to(outgoing[way], PLACES[way] // 3 - 1, PLACES[way] % 3 - 1) for way in range(8)]
     )
     arrivals = jnp.concatenate([arrivals[:, 0:6], arrivals[:, 8:]], axis=1)
     return (flow, floe_next[None, None], arrivals[None, None])

time: 97.8 us -> 121 us (1.24)
  the two profiles are of different devices: /device:TPU:24 before, /device:TPU:39 now
where the time goes in v5:
time: 121 us; the launch traced here: 120 us
  starting transfers between devices  58.6 us (48%)
  other arithmetic  21.9 us (18%)
  waiting for transfers between devices  18.6 us (15%)
  local copies, waits for them, and re-layouts  9.31 us (8%)
  Pallas kernels  8.92 us (7%)
  between operations  2.28 us (2%)
    ppermute x8, starting transfers between devices, send_to(): return lax.ppermute(array, ('sec', 'gx', 'gy'), pairs)  38.3 us
    ppermute x3, starting transfers between devices, exchange(): from_previous = lax.ppermute(high, axis, up)  14.6 us
    ppermute x8, waiting for transfers between devices, send_to(): return lax.ppermute(array, ('sec', 'gx', 'gy'), pairs)  12.8 us
    ppermute x3, waiting for transfers between devices, exchange(): from_next = lax.ppermute(low, axis, down)  5.87 us
    ppermute x3, starting transfers between devices, exchange(): from_next = lax.ppermute(low, axis, down)  5.76 us
    mul x4, other arithmetic, ocean_substep(): return (flow + horizontal * lap + vert + turning + surface) * wet[None]  5.52 us
    pallas_call x1, Pallas kernels, gather_records(): pl.pallas_call(gather_kernel, out_shape=jax.ShapeDtypeStruct((index.shape...  5.33 us
    pallas_call x1, Pallas kernels, sample_surface(): pl.pallas_call(sample_kernel, out_shape=jax.ShapeDtypeStruct((window.shap...  3.6 us
  transfers between devices with their start and end apart: 14, of which 4 were waited for; matrix products, arithmetic and copies ran while one was open for 10% of the time, Pallas kernels for 0%

profile of v5, /device:TPU:39, one launch (start us, length us, event | category | flops | bytes accessed | tf_op | source)
XLA Modules:
  0.0 120.1 jit_solution(18297131261302224128)
XLA Ops:
  0.7 0.8 pad_maximum_fusion.15
  1.5 0.8 convert_bitcast_fusion
  2.3 0.9 pad_maximum_fusion.13
  3.3 3.5 %collective-permute-start = (f32[12288]{0:T(1024)S(1)}, f32[12288]{0:T(1024)S(1)}, u32[]{:S(2)}, u32[]{:S(2)}) collective-permute-start(f32[12288]{0:T(1024)S(1)} %get-tuple-element.116), channel_id=1, source_target_pairs={{0,8},{8,16},{16,24},{24,32},{32,40},{40,48},{48,56},{56,64},{64,7... | collective-permute-start | bytes 147464 | tf_op jit(solution)/shard_map/ppermute | solution.py:164
  6.8 1.9 %collective-permute-start.1 = (f32[12288]{0:T(1024)S(1)}, f32[12288]{0:T(1024)S(1)}, u32[]{:S(2)}, u32[]{:S(2)}) collective-permute-start(f32[12288]{0:T(1024)S(1)} %get-tuple-element.117), channel_id=1, source_target_pairs={{8,0},{16,8},{24,16},{32,24},{40,32},{48,40},{56,48},{64,56},{72,6... | collective-permute-start | bytes 147464 | tf_op jit(solution)/shard_map/ppermute | solution.py:165
  8.8 0.6 multiply_multiply_fusion
  9.4 0.6 and_select_fusion
  10.0 0.7 bitcast_select_fusion.index_ref
  10.7 0.6 fusion.64.rows_ref
  11.3 0.7 maximum_bitcast_fusion.2
  12.2 0.2 fusion.68
  12.5 0.1 copy-done.9
  12.7 0.4 reshape.336
  13.0 0.4 reshape.339
  13.5 6.3 %collective-permute-start.2 = (f32[13152]{0:T(1024)S(1)}, f32[13152]{0:T(1024)S(1)}, u32[]{:S(2)}, u32[]{:S(2)}) collective-permute-start(f32[13152]{0:T(1024)S(1)} %get-tuple-element.114), channel_id=1, source_target_pairs={{0,1},{1,2},{2,3},{3,4},{4,5},{5,6},{6,7},{7,128},{128,129},{129,1... | collective-permute-start | bytes 157832 | tf_op jit(solution)/shard_map/ppermute | solution.py:164
  19.8 1.9 %collective-permute-start.3 = (f32[13152]{0:T(1024)S(1)}, f32[13152]{0:T(1024)S(1)}, u32[]{:S(2)}, u32[]{:S(2)}) collective-permute-start(f32[13152]{0:T(1024)S(1)} %get-tuple-element.115), channel_id=1, source_target_pairs={{1,0},{2,1},{3,2},{4,3},{5,4},{6,5},{7,6},{128,7},{129,128},{130,1... | collective-permute-start | bytes 157832 | tf_op jit(solution)/shard_map/ppermute | solution.py:165
  22.5 0.6 copy.28
  23.0 5.9 %collective-permute-done.3 = f32[13152]{0:T(1024)S(1)} collective-permute-done((f32[13152]{0:T(1024)S(1)}, f32[13152]{0:T(1024)S(1)}, u32[]{:S(2)}, u32[]{:S(2)}) %collective-permute-start.3) | collective-permute-done | bytes 52640 | tf_op jit(solution)/shard_map/ppermute | solution.py:165
  28.9 0.7 reshape.340
  29.7 0.7 reshape.338
  30.5 0.1 fusion.60
  30.7 0.7 pad_maximum_fusion
  31.6 0.1 broadcast_multiply_fusion
  31.7 0.1 slice_multiply_fusion.7
  31.8 0.2 fusion.58
  32.0 1.1 fusion.51
  33.1 0.2 fusion.57
  33.2 0.1 slice_multiply_fusion.5
  33.3 1.1 fusion.52
  34.4 0.2 fusion.56
  34.6 0.1 slice_multiply_fusion.3
  34.7 1.1 fusion.53
  35.8 0.1 fusion.55
  36.0 1.2 slice_multiply_fusion.1
  37.6 0.2 copy-done.21
  37.8 2.2 %fusion.54 = f32[2,8,72,136]{3,2,1,0:T(8,128)S(1)} fusion(f32[2,1,72,136]{3,2,1,0:T(8,128)S(1)} %fusion.60, f32[1,8,72,136]{3,2,1,0:T(8,128)} %get-tuple-element.81, f32[1,8,72,136]{3,2,1,0:T(8,128)} %get-tuple-element.80, f32[2,7,72,136]{3,2,1,0:T(8,128)S(1)} %fusion.55, f32[2,8,72,136]{3,2,1,0:T(8,128)S(1)} %fusion.53, f32[8]{0:T(128)S(1)} %copy-done.21, ...), kind=kLoop, calls=%fused_computation.97 | loop fusion | flops 2036736 | bytes 2820128 | tf_op jit(solution)/shard_map/mul | solution.py:55
  40.2 4.7 %collective-permute-start.4 = (f32[4,32,128]{2,1,0:T(8,128)S(1)}, f32[4,32,128]{2,1,0:T(8,128)S(1)}, u32[]{:S(2)}, u32[]{:S(2)}) collective-permute-start(f32[4,32,128]{2,1,0:T(8,128)S(1)} %get-tuple-element.104), channel_id=1, source_target_pairs={{0,8},{8,16},{16,24},{24,32},{32,40},{40,48},{48,56},{56,64},{64,7... | collective-permute-start | bytes 196616 | tf_op jit(solution)/shard_map/ppermute | solution.py:164
  44.9 1.9 %collective-permute-start.5 = (f32[4,32,128]{2,1,0:T(8,128)S(1)}, f32[4,32,128]{2,1,0:T(8,128)S(1)}, u32[]{:S(2)}, u32[]{:S(2)}) collective-permute-start(f32[4,32,128]{2,1,0:T(8,128)S(1)} %get-tuple-element.105), channel_id=1, source_target_pairs={{8,0},{16,8},{24,16},{32,24},{40,32},{48,40},{56,48},{64,56},{72,6... | collective-permute-start | bytes 196616 | tf_op jit(solution)/shard_map/ppermute | solution.py:165
  46.9 6.0 %while.10 = (s32[]{:T(128)}, f32[16,2,128]{2,0,1:T(8,128)S(1)}, s32[]{:T(128)}, s32[3,64]{1,0:T(4,128)S(1)}, s32[]{:T(128)}, /*index=5*/f32[48,5,128]{2,1,0:T(8,...) while((s32[]{:T(128)}, f32[16,2,128]{2,0,1:T(8,128)S(1)}, s32[]{:T(128)}, s32[3,64]{1,0:T(4,128)S(1)}, ...), condition=%wide.region_3.4_spmd, body=%wide.region_0.3_spmd.sunk | while | flops 15744006 | bytes 928223 | solution.py:291
  46.9 0.7 add_compare_fusion.2
  47.7 0.6 gather_fusion
  48.4 0.6 gather_fusion.1
  49.0 3.5 %multiply_reduce_fusion.4 = (f32[32,128]{1,0:T(8,128)S(1)}, f32[32,128]{1,0:T(8,128)S(1)}) fusion(f32[32,128]{1,0:T(8,128)S(1)} %bitcast.181, f32[32,128]{1,0:T(8,128)S(1)} %bitcast.186, f32[32,128]{1,0:T(8,128)S(1)} %bitcast.182, f32[32,128]{1,0:T(8,128)S(1)} %bitcast.187, f32[32,128]{1,0:T(8,128)S(1)} %bitcast.179, f32[32,128]{1,0:T(8,128)S(1)} %bitcast.184, ...), kind=kLoop, calls=%fused_computation.15.clone.1 | loop fusion | flops 14147584 | bytes 196608 | tf_op jit(solution)/shard_map/while/body/reduce_sum | solution.py:73
  52.5 0.2 convolution_add_fusion.2
  52.9 0.7 pad_maximum_fusion.2.window_ref
  53.6 3.6 %shard_map.148 = f32[4,2048]{1,0:T(4,128)} custom-call(f32[4,128,128]{2,1,0:T(8,128)} %pad_maximum_fusion.2.window_ref, s32[1,2048]{1,0:T(1,128)} %fusion.64.rows_ref, s32[1,2048]{1,0:T(1,128)} %get-tuple-element.62.cols_ref), custom_call_target="tpu_custom_call" | custom-call | tf_op jit(solution)/shard_map/pallas_call | solution.py:127
  57.2 0.8 multiply_reduce_fusion.2
  58.0 0.9 multiply_add_fusion
  58.9 0.6 pad_maximum_fusion.14
  59.6 5.3 %shard_map.149 = f32[8,40,128]{2,1,0:T(8,128)} custom-call(f32[4,2048]{1,0:T(4,128)} %get-tuple-element.112.state_ref, f32[1,2048]{1,0:T(1,128)} %bitcast.197, f32[1,2048]{1,0:T(1,128)} %bitcast.201, f32[32,2048]{1,0:T(8,128)} %bitcast.192, s32[8,128]{1,0:T(8,128)} %bitcast_select_fusion.index_ref), custom_call_target="tpu_custom_call" | custom-call | tf_op jit(solution)/shard_map/pallas_call | solution.py:153
  64.9 0.9 slice_bitcast_fusion.3
  65.8 1.9 %collective-permute-start.6 = (f32[40,128]{1,0:T(8,128)S(1)}, f32[40,128]{1,0:T(8,128)S(1)}, u32[]{:S(2)}, u32[]{:S(2)}) collective-permute-start(f32[40,128]{1,0:T(8,128)S(1)} %get-tuple-element.99), channel_id=1, source_target_pairs={{9,0},{10,1},{11,2},{12,3},{13,4},{14,5},{15,6},{136,7},{137,128},... | collective-permute-start | bytes 61448 | tf_op jit(solution)/shard_map/ppermute | solution.py:182
  67.7 2.3 %slice.453 = f32[2,8,64,128]{3,2,1,0:T(8,128)} slice(f32[2,8,72,136]{3,2,1,0:T(8,128)} %copy-done.2), slice={[0:2], [0:8], [4:68], [4:132]} | slice | bytes 1048576 | tf_op jit(solution)/shard_map/slice | solution.py:266
  70.0 8.1 %collective-permute-start.13 = (f32[40,128]{1,0:T(8,128)S(1)}, f32[40,128]{1,0:T(8,128)S(1)}, u32[]{:S(2)}, u32[]{:S(2)}) collective-permute-start(f32[40,128]{1,0:T(8,128)S(1)} %get-tuple-element.92), channel_id=1, source_target_pairs={{0,9},{1,10},{2,11},{3,12},{4,13},{5,14},{6,15},{7,136},{128,137},... | collective-permute-start | bytes 61448 | tf_op jit(solution)/shard_map/ppermute | solution.py:182
  78.1 6.1 %collective-permute-start.12 = (f32[40,128]{1,0:T(8,128)S(1)}, f32[40,128]{1,0:T(8,128)S(1)}, u32[]{:S(2)}, u32[]{:S(2)}) collective-permute-start(f32[40,128]{1,0:T(8,128)S(1)} %get-tuple-element.93), channel_id=1, source_target_pairs={{0,8},{1,9},{2,10},{3,11},{4,12},{5,13},{6,14},{7,15},{128,136},{1... | collective-permute-start | bytes 61448 | tf_op jit(solution)/shard_map/ppermute | solution.py:182
  84.3 1.9 %collective-permute-start.11 = (f32[40,128]{1,0:T(8,128)S(1)}, f32[40,128]{1,0:T(8,128)S(1)}, u32[]{:S(2)}, u32[]{:S(2)}) collective-permute-start(f32[40,128]{1,0:T(8,128)S(1)} %get-tuple-element.94), channel_id=1, source_target_pairs={{1,8},{2,9},{3,10},{4,11},{5,12},{6,13},{7,14},{128,15},{129,136},... | collective-permute-start | bytes 61448 | tf_op jit(solution)/shard_map/ppermute | solution.py:182
  86.2 14.1 %collective-permute-start.10 = (f32[40,128]{1,0:T(8,128)S(1)}, f32[40,128]{1,0:T(8,128)S(1)}, u32[]{:S(2)}, u32[]{:S(2)}) collective-permute-start(f32[40,128]{1,0:T(8,128)S(1)} %get-tuple-element.95), channel_id=1, source_target_pairs={{0,1},{1,2},{2,3},{3,4},{4,5},{5,6},{6,7},{7,128},{128,129},{129,1... | collective-permute-start | bytes 61448 | tf_op jit(solution)/shard_map/ppermute | solution.py:182
  100.4 1.9 %collective-permute-start.7 = (f32[40,128]{1,0:T(8,128)S(1)}, f32[40,128]{1,0:T(8,128)S(1)}, u32[]{:S(2)}, u32[]{:S(2)}) collective-permute-start(f32[40,128]{1,0:T(8,128)S(1)} %get-tuple-element.98), channel_id=1, source_target_pairs={{8,0},{9,1},{10,2},{11,3},{12,4},{13,5},{14,6},{15,7},{136,128},{1... | collective-permute-start | bytes 61448 | tf_op jit(solution)/shard_map/ppermute | solution.py:182
  102.3 2.9 %collective-permute-done.7 = f32[40,128]{1,0:T(8,128)S(1)} collective-permute-done((f32[40,128]{1,0:T(8,128)S(1)}, f32[40,128]{1,0:T(8,128)S(1)}, u32[]{:S(2)}, u32[]{:S(2)}) %collective-permute-start.7) | collective-permute-done | bytes 20512 | tf_op jit(solution)/shard_map/ppermute | solution.py:182
  105.2 2.2 %collective-permute-start.8 = (f32[40,128]{1,0:T(8,128)S(1)}, f32[40,128]{1,0:T(8,128)S(1)}, u32[]{:S(2)}, u32[]{:S(2)}) collective-permute-start(f32[40,128]{1,0:T(8,128)S(1)} %get-tuple-element.97), channel_id=1, source_target_pairs={{8,1},{9,2},{10,3},{11,4},{12,5},{13,6},{14,7},{15,128},{136,129},... | collective-permute-start | bytes 61448 | tf_op jit(solution)/shard_map/ppermute | solution.py:182
  107.4 3.1 %collective-permute-done.8 = f32[40,128]{1,0:T(8,128)S(1)} collective-permute-done((f32[40,128]{1,0:T(8,128)S(1)}, f32[40,128]{1,0:T(8,128)S(1)}, u32[]{:S(2)}, u32[]{:S(2)}) %collective-permute-start.8) | collective-permute-done | bytes 20512 | tf_op jit(solution)/shard_map/ppermute | solution.py:182
  110.5 1.9 %collective-permute-start.9 = (f32[40,128]{1,0:T(8,128)S(1)}, f32[40,128]{1,0:T(8,128)S(1)}, u32[]{:S(2)}, u32[]{:S(2)}) collective-permute-start(f32[40,128]{1,0:T(8,128)S(1)} %get-tuple-element.96), channel_id=1, source_target_pairs={{1,0},{2,1},{3,2},{4,3},{5,4},{6,5},{7,6},{128,7},{129,128},{130,1... | collective-permute-start | bytes 61448 | tf_op jit(solution)/shard_map/ppermute | solution.py:182
  112.4 6.8 %collective-permute-done.9 = f32[40,128]{1,0:T(8,128)S(1)} collective-permute-done((f32[40,128]{1,0:T(8,128)S(1)}, f32[40,128]{1,0:T(8,128)S(1)}, u32[]{:S(2)}, u32[]{:S(2)}) %collective-permute-start.9) | collective-permute-done | bytes 20512 | tf_op jit(solution)/shard_map/ppermute | solution.py:182
  119.4 0.7 copy.18
  (123 shorter events, 1.5 us)
Async XLA Ops:
  0.6 8.1 %copy-start.11 = (f32[1,1,2048]{2,1,0:T(1,128)S(1)}, f32[1,1,2048]{2,1,0:T(1,128)}, u32[]{:S(2)}) copy-start(f32[1,1,2048]{2,1,0:T(1,128)} %param.20) | copy-start | bytes 24580
  0.6 10.6 %copy-start.5 = (f32[1,1,2,2048]{3,2,1,0:T(2,128)S(1)}, f32[1,1,2,2048]{3,2,1,0:T(2,128)}, u32[]{:S(2)}) copy-start(f32[1,1,2,2048]{3,2,1,0:T(2,128)} %param.18) | copy-start | bytes 49156
  0.7 10.6 %copy-start.3 = (f32[1,1,2,2048]{3,2,1,0:T(2,128)S(1)}, f32[1,1,2,2048]{3,2,1,0:T(2,128)}, u32[]{:S(2)}) copy-start(f32[1,1,2,2048]{3,2,1,0:T(2,128)} %param.19) | copy-start | bytes 49156
  0.7 11.5 %copy-start.1 = (f32[2,64,128]{2,1,0:T(8,128)S(1)}, f32[2,64,128]{2,1,0:T(8,128)}, u32[]{:S(2)}) copy-start(f32[2,64,128]{2,1,0:T(8,128)} %param.16) | copy-start | bytes 196612
  0.7 11.5 %copy-start = (f32[2,8,64,128]{3,2,1,0:T(8,128)S(1)}, f32[2,8,64,128]{3,2,1,0:T(8,128)}, u32[]{:S(2)}) copy-start(f32[2,8,64,128]{3,2,1,0:T(8,128)} %param.15) | copy-start | bytes 1572868
  0.7 8.7 %copy-start.17 = (s32[1,1,2048]{2,1,0:T(1,128)S(1)}, s32[1,1,2048]{2,1,0:T(1,128)}, u32[]{:S(2)}) copy-start(s32[1,1,2048]{2,1,0:T(1,128)} %param.23) | copy-start | bytes 24580
  0.7 9.3 %copy-start.24 = (s32[1,1,8]{2,1,0:T(1,128)S(1)}, s32[1,1,8]{2,1,0:T(1,128)}, u32[]{:S(2)}) copy-start(s32[1,1,8]{2,1,0:T(1,128)} %param.27) | copy-start | bytes 100
  0.7 9.3 %copy-start.22 = (s32[1,1,8,128]{3,2,1,0:T(8,128)S(1)}, s32[1,1,8,128]{3,2,1,0:T(8,128)}, u32[]{:S(2)}) copy-start(s32[1,1,8,128]{3,2,1,0:T(8,128)} %param.26) | copy-start | bytes 12292
  3.3 8.7 %collective-permute-start = (f32[12288]{0:T(1024)S(1)}, f32[12288]{0:T(1024)S(1)}, u32[]{:S(2)}, u32[]{:S(2)}) collective-permute-start(f32[12288]{0:T(1024)S(1)} %get-tuple-element.116), channel_id=1, source_target_pairs={{0,8},{8,16},{16,24},{24,32},{32,40},{40,48},{48,56},{56,64},{64,7... | collective-permute-start | bytes 147464 | tf_op jit(solution)/shard_map/ppermute | solution.py:164
  6.8 5.2 %collective-permute-start.1 = (f32[12288]{0:T(1024)S(1)}, f32[12288]{0:T(1024)S(1)}, u32[]{:S(2)}, u32[]{:S(2)}) collective-permute-start(f32[12288]{0:T(1024)S(1)} %get-tuple-element.117), channel_id=1, source_target_pairs={{8,0},{16,8},{24,16},{32,24},{40,32},{48,40},{56,48},{64,56},{72,6... | collective-permute-start | bytes 147464 | tf_op jit(solution)/shard_map/ppermute | solution.py:165
  12.0 0.6 copy-start.9
  12.1 0.6 copy-start.7
  12.7 9.8 %copy-start.23 = (s32[1,1,3,64]{3,1,2,0:T(1,128)S(1)}, s32[1,1,3,64]{3,1,2,0:T(1,128)}, u32[]{:S(2)}) copy-start(s32[1,1,3,64]{3,1,2,0:T(1,128)} %param.25) | copy-start | bytes 2308
  13.5 16.2 %collective-permute-start.2 = (f32[13152]{0:T(1024)S(1)}, f32[13152]{0:T(1024)S(1)}, u32[]{:S(2)}, u32[]{:S(2)}) collective-permute-start(f32[13152]{0:T(1024)S(1)} %get-tuple-element.114), channel_id=1, source_target_pairs={{0,1},{1,2},{2,3},{3,4},{4,5},{5,6},{6,7},{7,128},{128,129},{129,1... | collective-permute-start | bytes 157832 | tf_op jit(solution)/shard_map/ppermute | solution.py:164
  19.8 9.1 %collective-permute-start.3 = (f32[13152]{0:T(1024)S(1)}, f32[13152]{0:T(1024)S(1)}, u32[]{:S(2)}, u32[]{:S(2)}) collective-permute-start(f32[13152]{0:T(1024)S(1)} %get-tuple-element.115), channel_id=1, source_target_pairs={{1,0},{2,1},{3,2},{4,3},{5,4},{6,5},{7,6},{128,7},{129,128},{130,1... | collective-permute-start | bytes 157832 | tf_op jit(solution)/shard_map/ppermute | solution.py:165
  21.8 12.9 %copy-start.20 = (f32[8]{0:T(128)}, f32[8]{0:T(128)S(1)}, u32[]{:S(2)}) copy-start(f32[8]{0:T(128)S(1)} %multiply_subtract_fusion) | copy-start | bytes 100
  28.9 1.6 %copy-start.13 = (f32[13152]{0:T(1024)}, f32[13152]{0:T(1024)S(1)}, u32[]{:S(2)}) copy-start(f32[13152]{0:T(1024)S(1)} %collective-permute-done.3) | copy-start | bytes 157828
  29.6 0.7 copy-start.15
  35.9 1.2 %copy-start.16 = (f32[13152]{0:T(1024)S(1)}, f32[13152]{0:T(1024)}, u32[]{:S(2)}) copy-start(f32[13152]{0:T(1024)} %copy-done.15) | copy-start | bytes 157828
  35.9 1.3 %copy-start.14 = (f32[13152]{0:T(1024)S(1)}, f32[13152]{0:T(1024)}, u32[]{:S(2)}) copy-start(f32[13152]{0:T(1024)} %copy-done.13) | copy-start | bytes 157828
  36.0 1.4 %copy-start.10 = (f32[1,5,512]{2,1,0:T(8,128)S(1)}, f32[1,5,512]{2,1,0:T(8,128)}, u32[]{:S(2)}) copy-start(f32[1,5,512]{2,1,0:T(8,128)} %copy-done.9) | copy-start | bytes 30724
  36.0 1.5 %copy-start.8 = (f32[1,5,512]{2,1,0:T(8,128)S(1)}, f32[1,5,512]{2,1,0:T(8,128)}, u32[]{:S(2)}) copy-start(f32[1,5,512]{2,1,0:T(8,128)} %copy-done.7) | copy-start | bytes 30724
  37.2 0.7 copy-start.21
  37.8 9.0 %copy-start.4 = (f32[16,5,128]{2,1,0:T(8,128)S(1)}, f32[16,5,128]{2,1,0:T(8,128)}, u32[]{:S(2)}) copy-start(f32[16,5,128]{2,1,0:T(8,128)} %maximum_bitcast_fusion.2) | copy-start | bytes 122884
  37.8 9.0 %copy-start.12 = (s32[1,1,3,64]{3,2,1,0:T(4,128)S(1)}, s32[1,1,3,64]{3,2,1,0:T(4,128)}, u32[]{:S(2)}) copy-start(s32[1,1,3,64]{3,2,1,0:T(4,128)} %copy.28) | copy-start | bytes 2308
  40.1 4.8 %copy-start.2 = (f32[2,8,72,136]{3,2,1,0:T(8,128)}, f32[2,8,72,136]{3,2,1,0:T(8,128)S(1)}, u32[]{:S(2)}) copy-start(f32[2,8,72,136]{3,2,1,0:T(8,128)S(1)} %fusion.54) | copy-start | bytes 1880068
  40.2 12.7 %collective-permute-start.4 = (f32[4,32,128]{2,1,0:T(8,128)S(1)}, f32[4,32,128]{2,1,0:T(8,128)S(1)}, u32[]{:S(2)}, u32[]{:S(2)}) collective-permute-start(f32[4,32,128]{2,1,0:T(8,128)S(1)} %get-tuple-element.104), channel_id=1, source_target_pairs={{0,8},{8,16},{16,24},{24,32},{32,40},{40,48},{48,56},{56,64},{64,7... | collective-permute-start | bytes 196616 | tf_op jit(solution)/shard_map/ppermute | solution.py:164
  44.9 8.0 %collective-permute-start.5 = (f32[4,32,128]{2,1,0:T(8,128)S(1)}, f32[4,32,128]{2,1,0:T(8,128)S(1)}, u32[]{:S(2)}, u32[]{:S(2)}) collective-permute-start(f32[4,32,128]{2,1,0:T(8,128)S(1)} %get-tuple-element.105), channel_id=1, source_target_pairs={{8,0},{16,8},{24,16},{32,24},{40,32},{48,40},{56,48},{64,56},{72,6... | collective-permute-start | bytes 196616 | tf_op jit(solution)/shard_map/ppermute | solution.py:165
  46.9 11.2 %copy-start.6 = (f32[1,1,2,2048]{3,2,1,0:T(2,128)S(1)}, f32[1,1,2,2048]{3,2,1,0:T(2,128)}, u32[]{:S(2)}) copy-start(f32[1,1,2,2048]{3,2,1,0:T(2,128)} %param.18) | copy-start | bytes 49156
  46.9 11.1 %copy-start.18 = (f32[2048]{0:T(1024)S(1)}, f32[2048]{0:T(1024)}, u32[]{:S(2)}) copy-start(f32[2048]{0:T(1024)} %multiply_multiply_fusion) | copy-start | bytes 24580
  46.9 11.1 %copy-start.19 = (f32[1,1,2048]{2,1,0:T(1,128)S(1)}, f32[1,1,2048]{2,1,0:T(1,128)}, u32[]{:S(2)}) copy-start(f32[1,1,2048]{2,1,0:T(1,128)} %param.21) | copy-start | bytes 24580
  65.8 34.6 %collective-permute-start.6 = (f32[40,128]{1,0:T(8,128)S(1)}, f32[40,128]{1,0:T(8,128)S(1)}, u32[]{:S(2)}, u32[]{:S(2)}) collective-permute-start(f32[40,128]{1,0:T(8,128)S(1)} %get-tuple-element.99), channel_id=1, source_target_pairs={{9,0},{10,1},{11,2},{12,3},{13,4},{14,5},{15,6},{136,7},{137,128},... | collective-permute-start | bytes 61448 | tf_op jit(solution)/shard_map/ppermute | solution.py:182
  70.0 49.3 %collective-permute-start.13 = (f32[40,128]{1,0:T(8,128)S(1)}, f32[40,128]{1,0:T(8,128)S(1)}, u32[]{:S(2)}, u32[]{:S(2)}) collective-permute-start(f32[40,128]{1,0:T(8,128)S(1)} %get-tuple-element.92), channel_id=1, source_target_pairs={{0,9},{1,10},{2,11},{3,12},{4,13},{5,14},{6,15},{7,136},{128,137},... | collective-permute-start | bytes 61448 | tf_op jit(solution)/shard_map/ppermute | solution.py:182
  78.1 41.2 %collective-permute-start.12 = (f32[40,128]{1,0:T(8,128)S(1)}, f32[40,128]{1,0:T(8,128)S(1)}, u32[]{:S(2)}, u32[]{:S(2)}) collective-permute-start(f32[40,128]{1,0:T(8,128)S(1)} %get-tuple-element.93), channel_id=1, source_target_pairs={{0,8},{1,9},{2,10},{3,11},{4,12},{5,13},{6,14},{7,15},{128,136},{1... | collective-permute-start | bytes 61448 | tf_op jit(solution)/shard_map/ppermute | solution.py:182
  84.3 35.0 %collective-permute-start.11 = (f32[40,128]{1,0:T(8,128)S(1)}, f32[40,128]{1,0:T(8,128)S(1)}, u32[]{:S(2)}, u32[]{:S(2)}) collective-permute-start(f32[40,128]{1,0:T(8,128)S(1)} %get-tuple-element.94), channel_id=1, source_target_pairs={{1,8},{2,9},{3,10},{4,11},{5,12},{6,13},{7,14},{128,15},{129,136},... | collective-permute-start | bytes 61448 | tf_op jit(solution)/shard_map/ppermute | solution.py:182
  86.2 33.0 %collective-permute-start.10 = (f32[40,128]{1,0:T(8,128)S(1)}, f32[40,128]{1,0:T(8,128)S(1)}, u32[]{:S(2)}, u32[]{:S(2)}) collective-permute-start(f32[40,128]{1,0:T(8,128)S(1)} %get-tuple-element.95), channel_id=1, source_target_pairs={{0,1},{1,2},{2,3},{3,4},{4,5},{5,6},{6,7},{7,128},{128,129},{129,1... | collective-permute-start | bytes 61448 | tf_op jit(solution)/shard_map/ppermute | solution.py:182
  100.4 4.8 %collective-permute-start.7 = (f32[40,128]{1,0:T(8,128)S(1)}, f32[40,128]{1,0:T(8,128)S(1)}, u32[]{:S(2)}, u32[]{:S(2)}) collective-permute-start(f32[40,128]{1,0:T(8,128)S(1)} %get-tuple-element.98), channel_id=1, source_target_pairs={{8,0},{9,1},{10,2},{11,3},{12,4},{13,5},{14,6},{15,7},{136,128},{1... | collective-permute-start | bytes 61448 | tf_op jit(solution)/shard_map/ppermute | solution.py:182
  105.2 5.3 %collective-permute-start.8 = (f32[40,128]{1,0:T(8,128)S(1)}, f32[40,128]{1,0:T(8,128)S(1)}, u32[]{:S(2)}, u32[]{:S(2)}) collective-permute-start(f32[40,128]{1,0:T(8,128)S(1)} %get-tuple-element.97), channel_id=1, source_target_pairs={{8,1},{9,2},{10,3},{11,4},{12,5},{13,6},{14,7},{15,128},{136,129},... | collective-permute-start | bytes 61448 | tf_op jit(solution)/shard_map/ppermute | solution.py:182
  110.5 8.7 %collective-permute-start.9 = (f32[40,128]{1,0:T(8,128)S(1)}, f32[40,128]{1,0:T(8,128)S(1)}, u32[]{:S(2)}, u32[]{:S(2)}) collective-permute-start(f32[40,128]{1,0:T(8,128)S(1)} %get-tuple-element.96), channel_id=1, source_target_pairs={{1,0},{2,1},{3,2},{4,3},{5,4},{6,5},{7,6},{128,7},{129,128},{130,1... | collective-permute-start | bytes 61448 | tf_op jit(solution)/shard_map/ppermute | solution.py:182
